TPU v7x, 256 devices: a whole 4x4x8 slice. The times are simulated.
256 devices in a mesh: neuron: 16 (over z, x_hi), tm: 16 (over y, x_lo, core).
Axes of the slice: x: 4 (x_hi: 2, x_lo: 2; x = x_hi * 2 + x_lo), y: 4, z: 8, core: 2. Of those that a mesh axis runs over, the one named last changes fastest.
Arguments:
- signal: bfloat16 [8192, 65536], P('tm', 'neuron'), may hold values from -6 to 6
- readin: bfloat16 [65536, 256], P('neuron'), may hold values from -0.0234375 to 0.0234375
- proj: bfloat16 [256, 512], replicated, may hold values from -0.375 to 0.375
- kernel: float32 [63, 512], replicated, may hold values from -0.75 to 0.75
- gain: float32 [512], replicated, may hold values from 0.5 to 1.5
- w_one: bfloat16 [512, 2048], P(None, 'neuron'), may hold values from -0.25 to 0.25
- w_two: bfloat16 [2048, 512], P('neuron'), may hold values from -0.125 to 0.125
- cotangent: bfloat16 [8192, 512], P('tm'), may hold values from -6 to 6
Outputs:
- denoised: bfloat16 [8192, 512], P('tm')
- grad_readin: float32 [65536, 256], P(('neuron', 'tm'))
- grad_proj: float32 [256, 512], replicated
- grad_kernel: float32 [63, 512], replicated
- grad_gain: float32 [512], replicated
- grad_w_one: float32 [512, 2048], P(None, 'neuron')
- grad_w_two: float32 [2048, 512], P('neuron')
All inputs are finite; a program needn't handle non-finite values.
Results may differ from a plain program's by a relative error of at most 0.0085.
Values may be sent and summed in bfloat16 or wider, within the bound.
No kernel may reach another device: no remote copies, remote signals or barrier semaphores. Data moves between devices by JAX's collectives and lax.ppermute only.
A program may use at most 64 MiB of HBM per device.

v0:
```python
import jax
import jax.numpy as jnp
from jax import lax
from jax.sharding import PartitionSpec as P


def with_halo(block, sides, width):
    for axis, dim in sides:
        count = lax.axis_size(axis)
        forward = [(i, i + 1) for i in range(count - 1)]
        backward = [(target, source) for source, target in forward]
        low = lax.ppermute(
            lax.slice_in_dim(block, block.shape[dim] - width, None, axis=dim), axis, forward
        )
        high = lax.ppermute(lax.slice_in_dim(block, 0, width, axis=dim), axis, backward)
        block = jnp.concatenate([low, block, high], axis=dim)
    return block


def conv_time(padded, kernel, rows):

    def step(index, total):
        window = lax.dynamic_slice_in_dim(padded, index, rows, 0)
        taps = lax.dynamic_slice_in_dim(kernel, index, 1, 0)
        return total + taps * window

    start = jnp.zeros((rows, padded.shape[1]), jnp.float32)
    return lax.fori_loop(0, kernel.shape[0], step, start)


def over_time(left, right):
    return lax.dot_general(
        left, right, (((0,), (0,)), ((), ())), preferred_element_type=jnp.float32
    )


def body(signal, readin, proj, kernel, gain, w_one, w_two, cotangent):
    rows = signal.shape[0]
    taps = kernel.shape[0]
    half = (taps - 1) // 2
    partial_latent = jnp.dot(signal, readin, preferred_element_type=jnp.float32)
    latent = lax.psum(partial_latent, "neuron").astype(jnp.bfloat16)
    lifted = jnp.dot(latent, proj, preferred_element_type=jnp.float32)
    padded = with_halo(lifted, (("tm", 0),), half)
    mixed = lifted + conv_time(padded, kernel, rows)
    scale = lax.rsqrt(jnp.mean(mixed * mixed, axis=1, keepdims=True) + 1e-05)
    normed = (mixed * scale * gain[None, :]).astype(jnp.bfloat16)
    pre = jnp.dot(normed, w_one, preferred_element_type=jnp.float32)
    act = jax.nn.silu(pre).astype(jnp.bfloat16)
    partial_mix = jnp.dot(act, w_two, preferred_element_type=jnp.float32)
    denoised = (mixed + lax.psum(partial_mix, "neuron")).astype(jnp.bfloat16)
    local_w_two = over_time(act, cotangent)
    dact = jnp.dot(cotangent, w_two.T, preferred_element_type=jnp.float32)
    sig = jax.nn.sigmoid(pre)
    dpre = (dact * sig * (1.0 + pre * (1.0 - sig))).astype(jnp.bfloat16)
    local_w_one = over_time(normed, dpre)
    partial_normed = jnp.dot(dpre, w_one.T, preferred_element_type=jnp.float32)
    dnormed = lax.psum(partial_normed, "neuron")
    local_gain = jnp.sum(dnormed * mixed * scale, axis=0)
    dgained = dnormed * gain[None, :]
    inner = jnp.mean(dgained * mixed, axis=1, keepdims=True)
    dmixed = cotangent.astype(jnp.float32) + scale * dgained - mixed * scale**3 * inner

    def kernel_row(index):
        window = lax.dynamic_slice_in_dim(padded, index, rows, 0)
        return jnp.sum(dmixed * window, axis=0)

    local_kernel = lax.map(kernel_row, jnp.arange(taps, dtype=jnp.int32))
    padded_grad = with_halo(dmixed, (("tm", 0),), half)
    dlifted = (dmixed + conv_time(padded_grad, kernel[::-1], rows)).astype(jnp.bfloat16)
    local_proj = over_time(latent, dlifted)
    dlatent = jnp.dot(dlifted, proj.T, preferred_element_type=jnp.float32).astype(jnp.bfloat16)
    grad_w_one, grad_w_two, grad_gain, grad_kernel, grad_proj = lax.psum(
        (local_w_one, local_w_two, local_gain, local_kernel, local_proj), "tm"
    )
    grad_readin = lax.psum_scatter(
        over_time(signal, dlatent), "tm", scatter_dimension=0, tiled=True
    )
    return (denoised, grad_readin, grad_proj, grad_kernel, grad_gain, grad_w_one, grad_w_two)


def solution(mesh):
    in_specs = (
        P("tm", "neuron"),
        P("neuron", None),
        P(),
        P(),
        P(),
        P(None, "neuron"),
        P("neuron", None),
        P("tm", None),
    )
    out_specs = (
        P("tm", None),
        P(("neuron", "tm"), None),
        P(),
        P(),
        P(),
        P(None, "neuron"),
        P("neuron", None),
    )
    return jax.shard_map(body, mesh=mesh, in_specs=in_specs, out_specs=out_specs, check_vma=False)
```

profile of v0, /device:TPU:1, one launch (start us, length us, event | category | flops | bytes accessed | tf_op | source)
XLA Modules:
  0.0 1194.0 jit_solution(17673050417110770765)
XLA Ops:
  8.8 3.4 fusion.12
  12.2 73.1 %all-reduce.9 = bf16[512,256]{1,0:T(8,128)(2,1)S(1)} all-reduce(f32[512,256]{1,0:T(8,128)S(1)} %fusion.12), channel_id=1, replica_groups=mesh['neuron'=16,'tm'=16] {'neuron'}, use_global_device_ids=true, to_apply=%region_0.0 | all-reduce | flops 131072 | bytes 786432 | tf_op jit(solution)/shard_map/psum | solution.py:42
  86.6 16.6 %collective-permute-start = (f32[31,512]{1,0:T(8,128)S(1)}, f32[31,512]{1,0:T(8,128)S(1)}, u32[]{:S(2)}, u32[]{:S(2)}) collective-permute-start(f32[31,512]{1,0:T(8,128)S(1)} %get-tuple-element.272), channel_id=1, source_target_pairs={{0,1},{1,2},{2,3},{3,4},{4,5},{5,6},{6,7},{7,8},{8,9},{9,10},{10,1... | collective-permute-start | bytes 190472 | tf_op jit(solution)/shard_map/ppermute | solution.py:12
  105.8 3.1 collective-permute-done.1
  110.3 200.2 %while.39 = (s32[]{:T(128)}, f32[512,512]{1,0:T(8,128)}, f32[63,512]{1,0:T(8,128)}, f32[574,512]{1,0:T(8,128)S(1)}, s32[]{:T(128)}, /*index=5*/s32[]{:T(128)}) while((s32[]{:T(128)}, f32[512,512]{1,0:T(8,128)}, f32[63,512]{1,0:T(8,128)}, f32[574,512]{1,0:T(8,128)S(1)}, s32[]{:T(128)}, /*index=5*/s32[]{:T(128)}) %tuple.83), condition=%wide.region_2.0_spmd.clone, body=%wide.region_1.0_spmd.clone.sunk | while | flops 786435 | bytes 3151959 | solution.py:28
  316.9 2.8 rev.3
  322.1 149.1 %all-reduce.8.cloned.1.call-done = (f32[512,512]{1,0:T(8,128)}, f32[512,512]{1,0:T(8,128)}) async-done(((f32[512,512]{1,0:T(8,128)}, f32[512,512]{1,0:T(8,128)}), (f32[512,512]{1,0:T(8,128)}, f32[512,512]{1,0:T(8,128)})) %all-reduce.8.cloned.1.call-update) | async-done | bytes 2097168 | tf_op jit(solution)/shard_map/psum | solution.py:51
  476.0 13.9 %collective-permute-start.2 = (f32[31,512]{1,0:T(8,128)S(1)}, f32[31,512]{1,0:T(8,128)S(1)}, u32[]{:S(2)}, u32[]{:S(2)}) collective-permute-start(f32[31,512]{1,0:T(8,128)S(1)} %get-tuple-element.268), channel_id=1, source_target_pairs={{0,1},{1,2},{2,3},{3,4},{4,5},{5,6},{6,7},{7,8},{8,9},{9,10},{10,1... | collective-permute-start | bytes 190472 | tf_op jit(solution)/shard_map/ppermute | solution.py:12
  496.7 219.1 %while.40 = (s32[]{:T(128)}, f32[512,512]{1,0:T(8,128)}, f32[63,512]{1,0:T(8,128)}, f32[574,512]{1,0:T(8,128)}, s32[]{:T(128)}, /*index=5*/s32[]{:T(128)}) while((s32[]{:T(128)}, f32[512,512]{1,0:T(8,128)}, f32[63,512]{1,0:T(8,128)}, f32[574,512]{1,0:T(8,128)}, s32[]{:T(128)}, /*index=5*/s32[]{:T(128)}) %tuple.86), condition=%wide.region_8.9_spmd.clone, body=%wide.region_7.8_spmd.clone.sunk | while | flops 786435 | bytes 3151959 | solution.py:28
  500.6 2.8 select_add_fusion.5
  504.0 2.8 select_add_fusion.5
  507.5 2.8 select_add_fusion.5
  511.0 2.8 select_add_fusion.5
  514.5 2.8 select_add_fusion.5
  518.0 2.8 select_add_fusion.5
  521.5 2.8 select_add_fusion.5
  524.9 2.8 select_add_fusion.5
  528.4 2.8 select_add_fusion.5
  531.9 2.8 select_add_fusion.5
  535.4 2.8 select_add_fusion.5
  538.9 2.8 select_add_fusion.5
  542.4 2.8 select_add_fusion.5
  545.8 2.8 select_add_fusion.5
  549.3 2.8 select_add_fusion.5
  552.8 2.8 select_add_fusion.5
  556.3 2.8 select_add_fusion.5
  559.8 2.8 select_add_fusion.5
  563.3 2.8 select_add_fusion.5
  566.7 2.8 select_add_fusion.5
  570.2 2.8 select_add_fusion.5
  573.7 2.8 select_add_fusion.5
  577.2 2.8 select_add_fusion.5
  580.7 2.8 select_add_fusion.5
  584.2 2.8 select_add_fusion.5
  587.6 2.8 select_add_fusion.5
  591.1 2.8 select_add_fusion.5
  594.6 2.8 select_add_fusion.5
  598.1 2.8 select_add_fusion.5
  601.6 2.8 select_add_fusion.5
  605.1 2.8 select_add_fusion.5
  608.5 2.8 select_add_fusion.5
  612.0 2.8 select_add_fusion.5
  615.5 2.8 select_add_fusion.5
  619.0 2.8 select_add_fusion.5
  718.3 6.3 convolution_bitcast_fusion
  724.6 331.9 %while.38 = (s32[]{:T(128)}, f32[63,512]{1,0:T(8,128)}, s32[63]{0:T(128)S(1)}, f32[574,512]{1,0:T(8,128)S(1)}, f32[512,512]{1,0:T(8,128)}, /*index=5*/s32[]{:T(128)}, s32[]{:T(128)}, s32[]{:T(128)}) while((s32[]{:T(128)}, f32[63,512]{1,0:T(8,128)}, s32[63]{0:T(128)S(1)}, f32[574,512]{1,0:T(8,128)S(1)}, f32[512,512]{1,0:T(8,128)}, ...), condition=%wide.region_13.14_spmd, body=%wide.region_11.13_spmd.sunk | while | flops 523781 | bytes 2103435 | solution.py:68
  1058.8 25.6 %psum.61 = f32[512]{0:T(512)} all-reduce(f32[512]{0:T(512)S(1)} %get-tuple-element.232), channel_id=1, replica_groups=mesh['neuron'=16,'tm'=16] {'tm'}, use_global_device_ids=true, to_apply=%region_16.17 | all-reduce | flops 512 | bytes 4096 | tf_op jit(solution)/shard_map/psum | solution.py:73
  1086.2 96.4 %all-reduce.6.cloned.1.call-done = (f32[256,512]{1,0:T(8,128)}, f32[63,512]{1,0:T(8,128)}, f32[512,128]{1,0:T(8,128)}, f32[128,512]{1,0:T(8,128)}) async-done(((f32[256,512]{1,0:T(8,128)}, f32[63,512]{1,0:T(8,128)}, f32[512,128]{1,0:T(8,128)}, f32[128,512]{1,0:T(8,128)}), (f32[256,512]{1,0:T(8,128)}, f32[63,512]{1,0:T(8,128)}, f32[512,128]{1,0:T(8,128)}, f32[128,512]{1,0:T(8,128)})) %all-reduce.6.cloned.1.call-update) | async-done | bytes 1177616 | tf_op jit(solution)/shard_map/psum | solution.py:73
  (481 shorter events, 570.5 us)
Async XLA Ops:
  7.2 1.6 copy-start
  7.2 78.1 %copy-start.6 = (bf16[256,512]{1,0:T(8,128)(2,1)S(1)}, bf16[256,512]{1,0:T(8,128)(2,1)}, u32[]{:S(2)}) copy-start(bf16[256,512]{1,0:T(8,128)(2,1)} %param.16) | copy-start | bytes 786436
  7.2 464.0 %all-reduce.8.cloned.1.call-start = ((), (), s32[]{:S(2)}) async-start(), calls=%async_computation.3 | async-start | bytes 4194304 | tf_op jit(solution)/shard_map/psum | solution.py:51
  85.6 1.0 copy-start.4
  86.6 18.5 %collective-permute-start = (f32[31,512]{1,0:T(8,128)S(1)}, f32[31,512]{1,0:T(8,128)S(1)}, u32[]{:S(2)}, u32[]{:S(2)}) collective-permute-start(f32[31,512]{1,0:T(8,128)S(1)} %get-tuple-element.272), channel_id=1, source_target_pairs={{0,1},{1,2},{2,3},{3,4},{4,5},{5,6},{6,7},{7,8},{8,9},{9,10},{10,1... | collective-permute-start | bytes 190472 | tf_op jit(solution)/shard_map/ppermute | solution.py:12
  103.2 5.7 collective-permute-start.1
  105.2 0.6 copy-start.16
  310.5 1.8 copy-start.11
  310.5 1.8 copy-start.17
  312.2 2.4 copy-start.2
  312.2 1.0 copy-start.15
  312.3 2.3 copy-start.9
  313.3 1.6 copy-start.7
  314.9 0.7 copy-start.12
  316.9 767.5 %reduce-scatter.2.cloned.1.call-start = ((), (), s32[]{:S(2)}) async-start(), calls=%async_computation.1 | async-start | bytes 4456448 | tf_op jit(solution)/shard_map/reduce_scatter | solution.py:76
  471.2 2.1 copy-start.3
  471.2 2.2 copy-start.5
  473.4 18.5 %copy-start.8 = (f32[512,128]{1,0:T(8,128)S(1)}, f32[512,128]{1,0:T(8,128)}, u32[]{:S(2)}) copy-start(f32[512,128]{1,0:T(8,128)} %copy-done.7) | copy-start | bytes 786436
  473.4 18.5 %copy-start.10 = (bf16[512,512]{1,0:T(8,128)(2,1)S(1)}, bf16[512,512]{1,0:T(8,128)(2,1)}, u32[]{:S(2)}) copy-start(bf16[512,512]{1,0:T(8,128)(2,1)} %param.21) | copy-start | bytes 1572868
  476.0 20.6 %copy-start.1 = (f32[512,512]{1,0:T(8,128)}, f32[512,512]{1,0:T(8,128)S(1)}, u32[]{:S(2)}) copy-start(f32[512,512]{1,0:T(8,128)S(1)} %get-tuple-element.397) | copy-start | bytes 3145732
  476.0 16.8 %collective-permute-start.2 = (f32[31,512]{1,0:T(8,128)S(1)}, f32[31,512]{1,0:T(8,128)S(1)}, u32[]{:S(2)}, u32[]{:S(2)}) collective-permute-start(f32[31,512]{1,0:T(8,128)S(1)} %get-tuple-element.268), channel_id=1, source_target_pairs={{0,1},{1,2},{2,3},{3,4},{4,5},{5,6},{6,7},{7,8},{8,9},{9,10},{10,1... | collective-permute-start | bytes 190472 | tf_op jit(solution)/shard_map/ppermute | solution.py:12
  489.9 5.6 collective-permute-start.3
  724.6 458.0 %all-reduce.6.cloned.1.call-start = ((), (), s32[]{:S(2)}) async-start(), calls=%async_computation.2 | async-start | bytes 2359296 | tf_op jit(solution)/shard_map/psum | solution.py:73
  1182.6 3.5 copy-start.14
  1182.6 4.2 copy-start.13
Sparse Core Ops, SparseCore 0:
  317.0 154.1 all-reduce.7
  724.7 68.6 reduce-scatter.1
  1058.9 123.6 all-reduce.5
where the time goes:
time: 1210 us; the launch traced here: 1190 us
  other arithmetic  429 us (35%)
  waiting for transfers between devices  251 us (21%)
  local copies, waits for them, and re-layouts  226 us (19%)
  loops' own time  123 us (10%)
  blocking collectives  98.8 us (8%)
  starting transfers between devices  34.4 us (3%)
  matrix products  18.8 us (2%)
  between operations  14 us (1%)
    add x126, other arithmetic, step(): return total + taps * window  328 us
    psum x1, waiting for transfers between devices, body(): denoised = (mixed + lax.psum(partial_mix, 'neuron')).astype(jnp.bfloat16)  149 us
    another operation x1, loops' own time, body(): local_kernel = lax.map(kernel_row, jnp.arange(taps, dtype=jnp.int32))  123 us
    psum x1, waiting for transfers between devices, body(): lax.psum((local_w_one, local_w_two, local_gain, local_kernel, local_proj)...  96.4 us
    dynamic_slice x126, local copies, waits for them, and re-layouts, step(): taps = lax.dynamic_slice_in_dim(kernel, index, 1, 0)  91 us
    reduce_sum x63, other arithmetic, kernel_row(): return jnp.sum(dmixed * window, axis=0)  88.8 us
    dynamic_update_slice x63, local copies, waits for them, and re-layouts, body(): local_kernel = lax.map(kernel_row, jnp.arange(taps, dtype=jnp.int32))  83.9 us
    psum x1, blocking collectives, body(): latent = lax.psum(partial_latent, 'neuron').astype(jnp.bfloat16)  73.1 us
  transfers between devices with their start and end apart: 7, of which 4 were waited for; matrix products, arithmetic and copies ran while one was open for 18% of the time, Pallas kernels for 0%

commit v1 on v0

--- a/solution.py
+++ b/solution.py
@@ -1,7 +1,12 @@
 import jax
 import jax.numpy as jnp
 from jax import lax
+from jax.experimental import pallas as pl
 from jax.sharding import PartitionSpec as P
+
+LANES = 128
+CHUNK = 128
+RCHUNK = 64
 
 
 def with_halo(block, sides, width):
@@ -17,15 +22,70 @@
     return block
 
 
-def conv_time(padded, kernel, rows):
+def _fwd_conv_kernel(x_ref, mid_ref, k_ref, o_ref):
+    rows, lanes = o_ref.shape
+    taps = k_ref.shape[0]
+    for r0 in range(0, rows, CHUNK):
+        acc = jnp.zeros((CHUNK, lanes), jnp.float32)
+        for j in range(taps):
+            acc = acc + k_ref[pl.ds(j, 1), :] * x_ref[pl.ds(r0 + j, CHUNK), :]
+        o_ref[pl.ds(r0, CHUNK), :] = mid_ref[pl.ds(r0, CHUNK), :] + acc
 
-    def step(index, total):
-        window = lax.dynamic_slice_in_dim(padded, index, rows, 0)
-        taps = lax.dynamic_slice_in_dim(kernel, index, 1, 0)
-        return total + taps * window
 
-    start = jnp.zeros((rows, padded.shape[1]), jnp.float32)
-    return lax.fori_loop(0, kernel.shape[0], step, start)
+def fwd_conv(padded, mid, kernel):
+    rows, width = mid.shape
+    taps = kernel.shape[0]
+    return pl.pallas_call(
+        _fwd_conv_kernel,
+        out_shape=jax.ShapeDtypeStruct((rows, width), jnp.float32),
+        grid=(width // LANES,),
+        in_specs=[
+            pl.BlockSpec((padded.shape[0], LANES), lambda c: (0, c)),
+            pl.BlockSpec((rows, LANES), lambda c: (0, c)),
+            pl.BlockSpec((taps, LANES), lambda c: (0, c)),
+        ],
+        out_specs=pl.BlockSpec((rows, LANES), lambda c: (0, c)),
+    )(padded, mid, kernel)
+
+
+def _bwd_conv_kernel(g_ref, d_ref, x_ref, k_ref, dl_ref, gk_ref):
+    rows, lanes = dl_ref.shape
+    taps = k_ref.shape[0]
+    for r0 in range(0, rows, CHUNK):
+        acc = jnp.zeros((CHUNK, lanes), jnp.float32)
+        for j in range(taps):
+            acc = acc + k_ref[pl.ds(taps - 1 - j, 1), :] * g_ref[pl.ds(r0 + j, CHUNK), :]
+        dl_ref[pl.ds(r0, CHUNK), :] = (d_ref[pl.ds(r0, CHUNK), :] + acc).astype(dl_ref.dtype)
+    for j in range(taps):
+        part = jnp.zeros((8, lanes), jnp.float32)
+        for r0 in range(0, rows, RCHUNK):
+            prod = d_ref[pl.ds(r0, RCHUNK), :] * x_ref[pl.ds(r0 + j, RCHUNK), :]
+            part = part + prod.reshape(RCHUNK // 8, 8, lanes).sum(axis=0)
+        gk_ref[pl.ds(j, 1), :] = part.sum(axis=0, keepdims=True)
+
+
+def bwd_conv(padded_grad, dmixed, padded, kernel):
+    rows, width = dmixed.shape
+    taps = kernel.shape[0]
+    full = padded.shape[0]
+    return pl.pallas_call(
+        _bwd_conv_kernel,
+        out_shape=(
+            jax.ShapeDtypeStruct((rows, width), jnp.bfloat16),
+            jax.ShapeDtypeStruct((taps, width), jnp.float32),
+        ),
+        grid=(width // LANES,),
+        in_specs=[
+            pl.BlockSpec((full, LANES), lambda c: (0, c)),
+            pl.BlockSpec((rows, LANES), lambda c: (0, c)),
+            pl.BlockSpec((full, LANES), lambda c: (0, c)),
+            pl.BlockSpec((taps, LANES), lambda c: (0, c)),
+        ],
+        out_specs=(
+            pl.BlockSpec((rows, LANES), lambda c: (0, c)),
+            pl.BlockSpec((taps, LANES), lambda c: (0, c)),
+        ),
+    )(padded_grad, dmixed, padded, kernel)
 
 
 def over_time(left, right):
@@ -35,14 +95,13 @@
 
 
 def body(signal, readin, proj, kernel, gain, w_one, w_two, cotangent):
-    rows = signal.shape[0]
     taps = kernel.shape[0]
     half = (taps - 1) // 2
     partial_latent = jnp.dot(signal, readin, preferred_element_type=jnp.float32)
     latent = lax.psum(partial_latent, "neuron").astype(jnp.bfloat16)
     lifted = jnp.dot(latent, proj, preferred_element_type=jnp.float32)
     padded = with_halo(lifted, (("tm", 0),), half)
-    mixed = lifted + conv_time(padded, kernel, rows)
+    mixed = fwd_conv(padded, lifted, kernel)
     scale = lax.rsqrt(jnp.mean(mixed * mixed, axis=1, keepdims=True) + 1e-05)
     normed = (mixed * scale * gain[None, :]).astype(jnp.bfloat16)
     pre = jnp.dot(normed, w_one, preferred_element_type=jnp.float32)
@@ -60,19 +119,16 @@
     dgained = dnormed * gain[None, :]
     inner = jnp.mean(dgained * mixed, axis=1, keepdims=True)
     dmixed = cotangent.astype(jnp.float32) + scale * dgained - mixed * scale**3 * inner
-
-    def kernel_row(index):
-        window = lax.dynamic_slice_in_dim(padded, index, rows, 0)
-        return jnp.sum(dmixed * window, axis=0)
-
-    local_kernel = lax.map(kernel_row, jnp.arange(taps, dtype=jnp.int32))
     padded_grad = with_halo(dmixed, (("tm", 0),), half)
-    dlifted = (dmixed + conv_time(padded_grad, kernel[::-1], rows)).astype(jnp.bfloat16)
+    dlifted, local_kernel = bwd_conv(padded_grad, dmixed, padded, kernel)
     local_proj = over_time(latent, dlifted)
     dlatent = jnp.dot(dlifted, proj.T, preferred_element_type=jnp.float32).astype(jnp.bfloat16)
-    grad_w_one, grad_w_two, grad_gain, grad_kernel, grad_proj = lax.psum(
-        (local_w_one, local_w_two, local_gain, local_kernel, local_proj), "tm"
+    local_small = jnp.concatenate([local_kernel, local_gain[None, :]], axis=0)
+    grad_w_one, grad_w_two, grad_small, grad_proj = lax.psum(
+        (local_w_one, local_w_two, local_small, local_proj), "tm"
     )
+    grad_kernel = grad_small[:taps]
+    grad_gain = grad_small[taps]
     grad_readin = lax.psum_scatter(
         over_time(signal, dlatent), "tm", scatter_dimension=0, tiled=True
     )

time: 1210 us -> 532 us (0.44); the launches traced: 1190 us -> 530 us
  other arithmetic: 429 us -> 9.37 us
  local copies, waits for them, and re-layouts: 226 us -> 12.1 us
  loops' own time: 123 us -> 0 us
  waiting for transfers between devices: 251 us -> 350 us
  blocking collectives: 98.8 us -> 73.1 us
  Pallas kernels: 0 us -> 18.2 us
    add x126 -> x0, other arithmetic: 328 us -> none  [step(): return total + taps * window]
    dynamic_slice x189 -> x0, local copies, waits for them, and re-layouts: 128 us -> none  [the longest x126 91 us: step(): taps = lax.dynamic_slice_in_dim(kernel, index, 1, 0)]
    another operation x3 -> x0, loops' own time: 123 us -> none  [the longest x1 123 us: body(): local_kernel = lax.map(kernel_row, jnp.arange(taps, dtype=jnp.int32))]
    reduce_sum x63 -> x0, other arithmetic: 88.8 us -> none  [kernel_row(): return jnp.sum(dmixed * window, axis=0)]
    dynamic_update_slice x63 -> x0, local copies, waits for them, and re-layouts: 83.9 us -> none  [body(): local_kernel = lax.map(kernel_row, jnp.arange(taps, dtype=jnp.int32))]
    reduce_scatter x1, waiting for transfers between devices: 0.01 us -> 73.1 us  [body(): lax.psum_scatter(over_time(signal, dlatent), 'tm', scatter_dimension=0, t...]
    psum x1 -> x0, blocking collectives: 25.6 us -> none  [body(): lax.psum((local_w_one, local_w_two, local_gain, local_kernel, local_proj)...]
    psum x1, waiting for transfers between devices: 96.4 us -> 118 us  [body(): lax.psum((local_w_one, local_w_two, local_small, local_proj), 'tm')]
  transfers between devices with their start and end apart: 7 -> 7, of which waited for: 4 -> 5; matrix products, arithmetic and copies ran while one was open for 18% -> 2% of each run, Pallas kernels for 0% -> 0%
where the time goes in v1:
time: 532 us; the launch traced here: 530 us
  waiting for transfers between devices  350 us (66%)
  blocking collectives  73.1 us (14%)
  starting transfers between devices  34.4 us (6%)
  matrix products  19.4 us (4%)
  Pallas kernels  18.2 us (3%)
  between operations  14 us (3%)
  local copies, waits for them, and re-layouts  12.1 us (2%)
  other arithmetic  9.37 us (2%)
    psum x1, waiting for transfers between devices, body(): denoised = (mixed + lax.psum(partial_mix, 'neuron')).astype(jnp.bfloat16)  152 us
    psum x1, waiting for transfers between devices, body(): lax.psum((local_w_one, local_w_two, local_small, local_proj), 'tm')  118 us
    reduce_scatter x1, waiting for transfers between devices, body(): lax.psum_scatter(over_time(signal, dlatent), 'tm', scatter_dimension=0, t...  73.1 us
    psum x1, blocking collectives, body(): latent = lax.psum(partial_latent, 'neuron').astype(jnp.bfloat16)  73.1 us
    ppermute x2, starting transfers between devices, with_halo(): lax.ppermute(lax.slice_in_dim(block, block.shape[dim] - width, None, axis...  30.4 us
    pallas_call x1, Pallas kernels, bwd_conv(): pl.pallas_call(_bwd_conv_kernel, out_shape=(jax.ShapeDtypeStruct((rows, w...  11.4 us
    unnamed x41, local copies, waits for them, and re-layouts  10.8 us
  transfers between devices with their start and end apart: 7, of which 5 were waited for; matrix products, arithmetic and copies ran while one was open for 2% of the time, Pallas kernels for 0%

profile of v1, /device:TPU:1, one launch (start us, length us, event | category | flops | bytes accessed | tf_op | source)
XLA Modules:
  0.0 530.2 jit_solution(5951981754812045607)
XLA Ops:
  7.2 0.0 copy-start
  7.2 0.0 all-reduce.8.cloned.1.call-start
  7.2 1.5 copy-done
  8.8 3.4 fusion.12
  12.2 73.1 %all-reduce.9 = bf16[512,256]{1,0:T(8,128)(2,1)S(1)} all-reduce(f32[512,256]{1,0:T(8,128)S(1)} %fusion.12), channel_id=1, replica_groups=mesh['neuron'=16,'tm'=16] {'neuron'}, use_global_device_ids=true, to_apply=%region_0.0 | all-reduce | flops 131072 | bytes 786432 | tf_op jit(solution)/shard_map/psum | solution.py:101
  85.3 1.2 fusion.15.mid_ref
  86.6 16.6 %collective-permute-start = (f32[31,512]{1,0:T(8,128)S(1)}, f32[31,512]{1,0:T(8,128)S(1)}, u32[]{:S(2)}, u32[]{:S(2)}) collective-permute-start(f32[31,512]{1,0:T(8,128)S(1)} %get-tuple-element.30), channel_id=1, source_target_pairs={{0,1},{1,2},{2,3},{3,4},{4,5},{5,6},{6,7},{7,8},{8,9},{9,10},{10,1... | collective-permute-start | bytes 190472 | tf_op jit(solution)/shard_map/ppermute | solution.py:17
  103.2 1.9 collective-permute-start.1
  105.1 3.6 collective-permute-done.1
  108.8 1.2 pad_maximum_fusion.x_ref
  110.0 6.8 %shard_map.135 = f32[512,512]{1,0:T(8,128)} custom-call(f32[574,512]{1,0:T(8,128)} %pad_maximum_fusion.x_ref, f32[512,512]{1,0:T(8,128)} %copy-done.3, f32[63,512]{1,0:T(8,128)} %k_ref.3), custom_call_target="tpu_custom_call" | custom-call | tf_op jit(solution)/shard_map/pallas_call | solution.py:38
  116.8 1.4 multiply_reduce_fusion.2
  118.2 1.6 fusion.7
  119.8 0.0 copy-start.8
  119.8 1.3 fusion.9
  121.2 0.3 fusion.1
  121.5 0.0 copy-start.13
  121.5 0.6 copy-done.13
  122.1 1.3 fusion.13
  123.4 0.0 all-reduce.8.cloned.1.call-update
  123.4 0.0 all-reduce.6.cloned.1.call-start
  123.5 0.8 copy-done.14
  124.3 1.1 fusion.6
  125.4 152.3 %all-reduce.8.cloned.1.call-done = (f32[512,512]{1,0:T(8,128)}, f32[512,512]{1,0:T(8,128)}) async-done(((f32[512,512]{1,0:T(8,128)}, f32[512,512]{1,0:T(8,128)}), (f32[512,512]{1,0:T(8,128)}, f32[512,512]{1,0:T(8,128)})) %all-reduce.8.cloned.1.call-update) | async-done | bytes 2097168 | tf_op jit(solution)/shard_map/psum | solution.py:110
  277.8 1.7 multiply_reduce_fusion
  279.5 0.1 copy-done.6
  279.6 2.3 multiply_subtract_fusion
  282.0 13.9 %collective-permute-start.2 = (f32[31,512]{1,0:T(8,128)S(1)}, f32[31,512]{1,0:T(8,128)S(1)}, u32[]{:S(2)}, u32[]{:S(2)}) collective-permute-start(f32[31,512]{1,0:T(8,128)S(1)} %get-tuple-element.26), channel_id=1, source_target_pairs={{0,1},{1,2},{2,3},{3,4},{4,5},{5,6},{6,7},{7,8},{8,9},{9,10},{10,1... | collective-permute-start | bytes 190472 | tf_op jit(solution)/shard_map/ppermute | solution.py:17
  295.8 1.9 collective-permute-start.3
  297.8 1.0 fusion.8
  298.8 0.0 collective-permute-done.2
  298.8 2.6 collective-permute-done.3
  301.4 1.1 pad_maximum_fusion.1.g_ref
  302.5 11.4 %shard_map.136 = (bf16[512,512]{1,0:T(8,128)(2,1)}, f32[63,512]{1,0:T(8,128)}) custom-call(f32[574,512]{1,0:T(8,128)} %pad_maximum_fusion.1.g_ref, f32[512,512]{1,0:T(8,128)} %copy-done.2, f32[574,512]{1,0:T(8,128)} %pad_maximum_fusion.x_ref, f32[63,512]{1,0:T(8,128)} %k_ref.3), custom_call_target="tpu_custom_call" | custom-call | tf_op jit(solution)/shard_map/pallas_call | solution.py:71
  314.0 2.2 fusion.14
  316.2 1.6 pad_maximum_fusion.2
  317.8 0.0 all-reduce.6.cloned.1.call-update
  317.8 0.0 reduce-scatter.2.cloned.1.call-start
  317.9 5.9 %convolution_bitcast_fusion = f32[4096,256]{0,1:T(8,128)} fusion(bf16[512,4096]{1,0:T(8,128)(2,1)} %param.8, bf16[512,512]{1,0:T(8,128)(2,1)S(1)} %copy-done.5, bf16[256,512]{1,0:T(8,128)(2,1)S(1)} %copy-done.7), kind=kOutput, calls=%fused_computation | convolution fusion | flops 1208090624 | bytes 9175040 | tf_op jit(solution)/shard_map/dot_general | solution.py:92
  323.8 0.0 reduce-scatter.2.cloned.1.call-update
  323.8 117.8 %all-reduce.6.cloned.1.call-done = (f32[256,512]{1,0:T(8,128)}, f32[64,512]{1,0:T(8,128)}, f32[512,128]{1,0:T(8,128)}, f32[128,512]{1,0:T(8,128)}) async-done(((f32[256,512]{1,0:T(8,128)}, f32[64,512]{1,0:T(8,128)}, f32[512,128]{1,0:T(8,128)}, f32[128,512]{1,0:T(8,128)}), (f32[256,512]{1,0:T(8,128)}, f32[64,512]{1,0:T(8,128)}, f32[512,128]{1,0:T(8,128)}, f32[128,512]{1,0:T(8,128)})) %all-reduce.6.cloned.1.call-update) | async-done | bytes 1179664 | tf_op jit(solution)/shard_map/psum | solution.py:127
  441.6 1.3 slice.29
  442.9 73.1 %reduce-scatter.2.cloned.1.call-done = f32[256,256]{0,1:T(8,128)} async-done(((f32[4096,256]{0,1:T(8,128)}), f32[256,256]{0,1:T(8,128)}) %reduce-scatter.2.cloned.1.call-update) | async-done | bytes 262160 | tf_op jit(solution)/shard_map/reduce_scatter | solution.py:132
  516.1 1.8 copy.15
  517.8 1.9 copy.24
  519.7 1.6 copy.25
  521.3 1.7 copy.26
  523.0 0.7 copy.27
  (34 shorter events, 0.1 us)
Async XLA Ops:
  7.2 1.6 copy-start
  7.2 270.6 %all-reduce.8.cloned.1.call-start = ((), (), s32[]{:S(2)}) async-start(), calls=%async_computation.3 | async-start | bytes 4194304 | tf_op jit(solution)/shard_map/psum | solution.py:110
  86.6 23.4 %copy-start.3 = (f32[512,512]{1,0:T(8,128)}, f32[512,512]{1,0:T(8,128)S(1)}, u32[]{:S(2)}) copy-start(f32[512,512]{1,0:T(8,128)S(1)} %fusion.15.mid_ref) | copy-start | bytes 3145732
  86.6 18.5 %collective-permute-start = (f32[31,512]{1,0:T(8,128)S(1)}, f32[31,512]{1,0:T(8,128)S(1)}, u32[]{:S(2)}, u32[]{:S(2)}) collective-permute-start(f32[31,512]{1,0:T(8,128)S(1)} %get-tuple-element.30), channel_id=1, source_target_pairs={{0,1},{1,2},{2,3},{3,4},{4,5},{5,6},{6,7},{7,8},{8,9},{9,10},{10,1... | collective-permute-start | bytes 190472 | tf_op jit(solution)/shard_map/ppermute | solution.py:17
  103.2 5.6 %collective-permute-start.1 = (f32[31,512]{1,0:T(8,128)S(1)}, f32[31,512]{1,0:T(8,128)S(1)}, u32[]{:S(2)}, u32[]{:S(2)}) collective-permute-start(f32[31,512]{1,0:T(8,128)S(1)} %get-tuple-element.31), channel_id=1, source_target_pairs={{1,0},{2,1},{3,2},{4,3},{5,4},{6,5},{7,6},{8,7},{9,8},{10,9},{11,1... | collective-permute-start | bytes 190472 | tf_op jit(solution)/shard_map/ppermute | solution.py:20
  110.0 8.3 %copy-start.12 = (bf16[512,128]{1,0:T(8,128)(2,1)S(1)}, bf16[512,128]{1,0:T(8,128)(2,1)}, u32[]{:S(2)}) copy-start(bf16[512,128]{1,0:T(8,128)(2,1)} %param.13) | copy-start | bytes 393220
  110.0 8.3 %copy-start.17 = (f32[512]{0:T(512)S(1)}, f32[512]{0:T(512)}, u32[]{:S(2)}) copy-start(f32[512]{0:T(512)} %param.12) | copy-start | bytes 6148
  116.8 3.1 copy-start.16
  116.8 4.4 copy-start.10
  119.8 1.3 copy-start.8
  121.5 0.7 copy-start.13
  122.1 1.3 copy-start.1
  123.4 0.9 copy-start.14
  123.4 318.2 %all-reduce.6.cloned.1.call-start = ((), (), s32[]{:S(2)}) async-start(), calls=%async_computation.2 | async-start | bytes 2359296 | tf_op jit(solution)/shard_map/psum | solution.py:127
  277.8 1.7 copy-start.4
  277.8 1.9 copy-start.6
  279.6 18.1 %copy-start.9 = (f32[512,128]{1,0:T(8,128)S(1)}, f32[512,128]{1,0:T(8,128)}, u32[]{:S(2)}) copy-start(f32[512,128]{1,0:T(8,128)} %copy-done.8) | copy-start | bytes 786436
  279.6 18.1 %copy-start.11 = (bf16[512,512]{1,0:T(8,128)(2,1)S(1)}, bf16[512,512]{1,0:T(8,128)(2,1)}, u32[]{:S(2)}) copy-start(bf16[512,512]{1,0:T(8,128)(2,1)} %param.15) | copy-start | bytes 1572868
  282.0 19.5 %copy-start.2 = (f32[512,512]{1,0:T(8,128)}, f32[512,512]{1,0:T(8,128)S(1)}, u32[]{:S(2)}) copy-start(f32[512,512]{1,0:T(8,128)S(1)} %get-tuple-element.28.d_ref) | copy-start | bytes 3145732
  282.0 16.8 %collective-permute-start.2 = (f32[31,512]{1,0:T(8,128)S(1)}, f32[31,512]{1,0:T(8,128)S(1)}, u32[]{:S(2)}, u32[]{:S(2)}) collective-permute-start(f32[31,512]{1,0:T(8,128)S(1)} %get-tuple-element.26), channel_id=1, source_target_pairs={{0,1},{1,2},{2,3},{3,4},{4,5},{5,6},{6,7},{7,8},{8,9},{9,10},{10,1... | collective-permute-start | bytes 190472 | tf_op jit(solution)/shard_map/ppermute | solution.py:17
  295.8 5.6 %collective-permute-start.3 = (f32[31,512]{1,0:T(8,128)S(1)}, f32[31,512]{1,0:T(8,128)S(1)}, u32[]{:S(2)}, u32[]{:S(2)}) collective-permute-start(f32[31,512]{1,0:T(8,128)S(1)} %get-tuple-element.27), channel_id=1, source_target_pairs={{1,0},{2,1},{3,2},{4,3},{5,4},{6,5},{7,6},{8,7},{9,8},{10,9},{11,1... | collective-permute-start | bytes 190472 | tf_op jit(solution)/shard_map/ppermute | solution.py:20
  314.0 3.9 copy-start.5
  314.0 3.9 copy-start.7
  317.8 198.3 %reduce-scatter.2.cloned.1.call-start = ((), (), s32[]{:S(2)}) async-start(), calls=%async_computation.1 | async-start | bytes 4456448 | tf_op jit(solution)/shard_map/reduce_scatter | solution.py:132
  441.6 81.4 %copy-start.15 = (f32[128,512]{1,0:T(8,128)S(1)}, f32[128,512]{1,0:T(8,128)}, u32[]{:S(2)}) copy-start(f32[128,512]{1,0:T(8,128)} %get-tuple-element.40) | copy-start | bytes 786436
Sparse Core Ops, SparseCore 0:
  123.5 154.1 all-reduce.7
  317.9 123.6 all-reduce.5
  444.2 71.8 reduce-scatter.1

commit v2 on v1

--- a/solution.py
+++ b/solution.py
@@ -94,11 +94,32 @@
     )
 
 
+def scatter_sum(parts, axis):
+    got = lax.all_to_all(parts, axis, 0, 0, tiled=False)
+    return jnp.sum(got, axis=0)
+
+
+def gather_all(piece, axis):
+    count = lax.axis_size(axis)
+    spread = jnp.broadcast_to(piece[None], (count,) + piece.shape)
+    return lax.all_to_all(spread, axis, 0, 0, tiled=False)
+
+
+def split_rows(x, count):
+    return x.reshape((count, x.shape[0] // count) + x.shape[1:])
+
+
 def body(signal, readin, proj, kernel, gain, w_one, w_two, cotangent):
+    rows = signal.shape[0]
     taps = kernel.shape[0]
     half = (taps - 1) // 2
+    nn = lax.axis_size("neuron")
+    nt = lax.axis_size("tm")
+    me = lax.axis_index("neuron")
+    share = rows // nn
     partial_latent = jnp.dot(signal, readin, preferred_element_type=jnp.float32)
-    latent = lax.psum(partial_latent, "neuron").astype(jnp.bfloat16)
+    latent_rows = scatter_sum(split_rows(partial_latent, nn), "neuron").astype(jnp.bfloat16)
+    latent = gather_all(latent_rows, "neuron").reshape(rows, -1)
     lifted = jnp.dot(latent, proj, preferred_element_type=jnp.float32)
     padded = with_halo(lifted, (("tm", 0),), half)
     mixed = fwd_conv(padded, lifted, kernel)
@@ -107,14 +128,20 @@
     pre = jnp.dot(normed, w_one, preferred_element_type=jnp.float32)
     act = jax.nn.silu(pre).astype(jnp.bfloat16)
     partial_mix = jnp.dot(act, w_two, preferred_element_type=jnp.float32)
-    denoised = (mixed + lax.psum(partial_mix, "neuron")).astype(jnp.bfloat16)
     local_w_two = over_time(act, cotangent)
     dact = jnp.dot(cotangent, w_two.T, preferred_element_type=jnp.float32)
     sig = jax.nn.sigmoid(pre)
     dpre = (dact * sig * (1.0 + pre * (1.0 - sig))).astype(jnp.bfloat16)
     local_w_one = over_time(normed, dpre)
+    grad_w_one, grad_w_two = lax.psum((local_w_one, local_w_two), "tm")
     partial_normed = jnp.dot(dpre, w_one.T, preferred_element_type=jnp.float32)
-    dnormed = lax.psum(partial_normed, "neuron")
+    both = jnp.stack([split_rows(partial_mix, nn), split_rows(partial_normed, nn)], axis=1)
+    summed = scatter_sum(both, "neuron")
+    mixed_rows = lax.dynamic_slice_in_dim(mixed, me * share, share, 0)
+    denoised_rows = (mixed_rows + summed[0]).astype(jnp.bfloat16).astype(jnp.float32)
+    back = gather_all(jnp.stack([denoised_rows, summed[1]]), "neuron")
+    denoised = back[:, 0].reshape(rows, -1).astype(jnp.bfloat16)
+    dnormed = back[:, 1].reshape(rows, -1)
     local_gain = jnp.sum(dnormed * mixed * scale, axis=0)
     dgained = dnormed * gain[None, :]
     inner = jnp.mean(dgained * mixed, axis=1, keepdims=True)
@@ -123,15 +150,21 @@
     dlifted, local_kernel = bwd_conv(padded_grad, dmixed, padded, kernel)
     local_proj = over_time(latent, dlifted)
     dlatent = jnp.dot(dlifted, proj.T, preferred_element_type=jnp.float32).astype(jnp.bfloat16)
-    local_small = jnp.concatenate([local_kernel, local_gain[None, :]], axis=0)
-    grad_w_one, grad_w_two, grad_small, grad_proj = lax.psum(
-        (local_w_one, local_w_two, local_small, local_proj), "tm"
+    local_readin = over_time(signal, dlatent)
+    small = jnp.concatenate(
+        [local_proj.reshape(-1), local_kernel.reshape(-1), local_gain.reshape(-1)]
     )
-    grad_kernel = grad_small[:taps]
-    grad_gain = grad_small[taps]
-    grad_readin = lax.psum_scatter(
-        over_time(signal, dlatent), "tm", scatter_dimension=0, tiled=True
-    )
+    readin_part = local_readin.reshape(nt, -1)
+    packed = jnp.concatenate([readin_part, small.reshape(nt, -1)], axis=1)
+    reduced = scatter_sum(packed, "tm")
+    cut = readin_part.shape[1]
+    grad_readin = reduced[:cut].reshape(-1, local_readin.shape[1])
+    small_sum = gather_all(reduced[cut:], "tm").reshape(-1)
+    n_proj = local_proj.size
+    n_kernel = local_kernel.size
+    grad_proj = small_sum[:n_proj].reshape(local_proj.shape)
+    grad_kernel = small_sum[n_proj:n_proj + n_kernel].reshape(local_kernel.shape)
+    grad_gain = small_sum[n_proj + n_kernel:]
     return (denoised, grad_readin, grad_proj, grad_kernel, grad_gain, grad_w_one, grad_w_two)
 
 

time: 532 us -> 466 us (0.88)
  waiting for transfers between devices: 350 us -> 226 us
  blocking collectives: 73.1 us -> 99.5 us
  local copies, waits for them, and re-layouts: 12.1 us -> 36.5 us
  other arithmetic: 9.37 us -> 21.5 us
    psum x2 -> x1, waiting for transfers between devices: 270 us -> 107 us  [body(): grad_w_one, grad_w_two = lax.psum((local_w_one, local_w_two), 'tm')]
    all_to_all x0 -> x3, waiting for transfers between devices: none -> 112 us  [the longest x2 106 us: scatter_sum(): got = lax.all_to_all(parts, axis, 0, 0, tiled=False)]
    all_to_all x0 -> x3, blocking collectives: none -> 99.5 us  [the longest x2 70.9 us: gather_all(): return lax.all_to_all(spread, axis, 0, 0, tiled=False)]
    reduce_scatter x1 -> x0, waiting for transfers between devices: 73.1 us -> none  [body(): lax.psum_scatter(over_time(signal, dlatent), 'tm', scatter_dimension=0, t...]
    psum x1 -> x0, blocking collectives: 73.1 us -> none  [body(): latent = lax.psum(partial_latent, 'neuron').astype(jnp.bfloat16)]
    ppermute x2, starting transfers between devices: 30.4 us -> 11.5 us  [with_halo(): lax.ppermute(lax.slice_in_dim(block, block.shape[dim] - width, None, axis...]
    all_to_all x0 -> x3, starting transfers between devices: none -> 15 us  [the longest x2 10.7 us: scatter_sum(): got = lax.all_to_all(parts, axis, 0, 0, tiled=False)]
    all_to_all x0 -> x1, local copies, waits for them, and re-layouts: none -> 9.59 us  [scatter_sum(): got = lax.all_to_all(parts, axis, 0, 0, tiled=False)]
  transfers between devices with their start and end apart: 7 -> 8, of which waited for: 5 -> 6; matrix products, arithmetic and copies ran while one was open for 2% -> 3% of each run, Pallas kernels for 0% -> 0%
where the time goes in v2:
time: 466 us; the launch traced here: 465 us
  waiting for transfers between devices  226 us (48%)
  blocking collectives  99.5 us (21%)
  local copies, waits for them, and re-layouts  36.5 us (8%)
  starting transfers between devices  30.6 us (7%)
  other arithmetic  21.5 us (5%)
  matrix products  18.7 us (4%)
  Pallas kernels  18.2 us (4%)
  between operations  14.3 us (3%)
    psum x1, waiting for transfers between devices, body(): grad_w_one, grad_w_two = lax.psum((local_w_one, local_w_two), 'tm')  107 us
    all_to_all x2, waiting for transfers between devices, scatter_sum(): got = lax.all_to_all(parts, axis, 0, 0, tiled=False)  106 us
    all_to_all x2, blocking collectives, gather_all(): return lax.all_to_all(spread, axis, 0, 0, tiled=False)  70.9 us
    all_to_all x1, blocking collectives, scatter_sum(): got = lax.all_to_all(parts, axis, 0, 0, tiled=False)  28.6 us
    dot_general x4, matrix products, over_time(): lax.dot_general(left, right, (((0,), (0,)), ((), ())), preferred_element_...  11.6 us
    ppermute x2, starting transfers between devices, with_halo(): lax.ppermute(lax.slice_in_dim(block, block.shape[dim] - width, None, axis...  11.5 us
    pallas_call x1, Pallas kernels, bwd_conv(): pl.pallas_call(_bwd_conv_kernel, out_shape=(jax.ShapeDtypeStruct((rows, w...  11.4 us
    all_to_all x2, starting transfers between devices, scatter_sum(): got = lax.all_to_all(parts, axis, 0, 0, tiled=False)  10.7 us
  transfers between devices with their start and end apart: 8, of which 6 were waited for; matrix products, arithmetic and copies ran while one was open for 3% of the time, Pallas kernels for 0%

profile of v2, /device:TPU:1, one launch (start us, length us, event | category | flops | bytes accessed | tf_op | source)
XLA Modules:
  0.0 465.1 jit_solution(6409163413245722069)
XLA Ops:
  7.2 1.6 copy-done
  8.8 3.4 fusion.14
  12.2 28.6 %all_to_all.35 = f32[16,32,256]{2,1,0:T(8,128)S(1)} all-to-all(f32[16,32,256]{2,1,0:T(8,128)S(1)} %bitcast.67), channel_id=1, replica_groups=mesh['neuron'=16,'tm'=16] {'neuron'}, dimensions={0} | all-to-all | bytes 1048576 | tf_op jit(solution)/shard_map/all_to_all | solution.py:98
  40.8 16.8 %all_to_all.36 = bf16[16,32,256]{2,1,0:T(8,128)(2,1)S(1)} all-to-all(bf16[16,32,256]{2,1,0:T(8,128)(2,1)S(1)} %broadcast_in_dim.6), channel_id=1, replica_groups=mesh['neuron'=16,'tm'=16] {'neuron'}, dimensions={0} | all-to-all | bytes 524288 | tf_op jit(solution)/shard_map/all_to_all | solution.py:105
  57.7 1.2 fusion.15.mid_ref
  58.9 4.2 collective-permute-start
  63.2 1.9 collective-permute-start.1
  65.1 3.6 collective-permute-done.1
  68.8 1.1 pad_maximum_fusion.1.x_ref
  69.9 6.8 %shard_map.135 = f32[512,512]{1,0:T(8,128)} custom-call(f32[574,512]{1,0:T(8,128)} %pad_maximum_fusion.1.x_ref, f32[512,512]{1,0:T(8,128)} %copy-done.3, f32[63,512]{1,0:T(8,128)} %k_ref.3), custom_call_target="tpu_custom_call" | custom-call | tf_op jit(solution)/shard_map/pallas_call | solution.py:38
  76.7 1.4 multiply_reduce_fusion.1
  78.2 1.6 fusion.9
  81.1 1.5 pad_maximum_fusion
  82.6 4.4 all-to-all-start.2
  87.0 50.4 %all-to-all-done.2 = f32[16,2,32,512]{3,2,1,0:T(8,128)} async-done(((f32[16,2,32,512]{3,2,1,0:T(8,128)}), f32[16,2,32,512]{3,2,1,0:T(8,128)}, u32[]{:S(2)}, u32[]{:S(2)}) %all-to-all-start.2) | async-done | bytes 2097184 | tf_op jit(solution)/shard_map/all_to_all | solution.py:98
  137.4 1.8 reduce_sum.56
  139.5 54.1 %all_to_all.37 = f32[16,2,32,512]{3,2,1,0:T(8,128)S(1)} all-to-all(f32[16,2,32,512]{3,2,1,0:T(8,128)S(1)} %broadcast_in_dim.7), channel_id=1, replica_groups=mesh['neuron'=16,'tm'=16] {'neuron'}, dimensions={0} | all-to-all | bytes 4194304 | tf_op jit(solution)/shard_map/all_to_all | solution.py:105
  194.1 0.8 copy-done.4
  195.4 7.3 %collective-permute-start.2 = (f32[31,512]{1,0:T(8,128)S(1)}, f32[31,512]{1,0:T(8,128)S(1)}, u32[]{:S(2)}, u32[]{:S(2)}) collective-permute-start(f32[31,512]{1,0:T(8,128)S(1)} %get-tuple-element.15), channel_id=1, source_target_pairs={{0,1},{1,2},{2,3},{3,4},{4,5},{5,6},{6,7},{7,8},{8,9},{9,10},{10,1... | collective-permute-start | bytes 190472 | tf_op jit(solution)/shard_map/ppermute | solution.py:17
  202.7 2.1 collective-permute-start.3
  204.8 3.5 collective-permute-done.3
  208.2 1.2 pad_maximum_fusion.2.g_ref
  209.4 11.4 %shard_map.136 = (bf16[512,512]{1,0:T(8,128)(2,1)}, f32[63,512]{1,0:T(8,128)}) custom-call(f32[574,512]{1,0:T(8,128)} %pad_maximum_fusion.2.g_ref, f32[512,512]{1,0:T(8,128)} %copy-done.2, f32[574,512]{1,0:T(8,128)} %pad_maximum_fusion.1.x_ref, f32[63,512]{1,0:T(8,128)} %k_ref.3), custom_call_target="tpu_custom_call" | custom-call | tf_op jit(solution)/shard_map/pallas_call | solution.py:71
  220.8 2.2 convolution_bitcast_fusion.1
  223.0 6.2 %convolution_bitcast_fusion = f32[4096,256]{0,1:T(8,128)} fusion(bf16[512,4096]{1,0:T(8,128)(2,1)} %param.8, bf16[512,512]{1,0:T(8,128)(2,1)} %get-tuple-element.9, bf16[256,512]{1,0:T(8,128)(2,1)} %param.10), kind=kOutput, calls=%fused_computation | convolution fusion | flops 1208090624 | bytes 9175040 | tf_op jit(solution)/shard_map/dot_general | solution.py:92
  229.2 1.2 copy.20
  230.4 0.9 pad_maximum_fusion.3
  231.3 2.0 reshape.88
  233.3 5.7 %copy.18 = f32[4096,256]{1,0:T(8,128)} copy(f32[4096,256]{0,1:T(8,128)} %convolution_bitcast_fusion) | data formatting | bytes 8388608 | tf_op jit(solution)/shard_map/dot_general | solution.py:92
  239.0 4.0 reshape.85
  243.0 4.9 %maximum_bitcast_fusion = f32[16,1,75776]{2,0,1:T(8,128)} fusion(f32[16,10240]{1,0:T(8,128)} %reshape.88, f32[16,65536]{1,0:T(8,128)} %reshape.85), kind=kLoop, calls=%fused_computation.1 | loop fusion | flops 1212416 | bytes 9699328 | tf_op jit(solution)/shard_map/all_to_all | solution.py:98
  247.8 9.6 %copy.19 = f32[16,1,75776]{2,1,0:T(1,128)} copy(f32[16,1,75776]{2,0,1:T(8,128)} %maximum_bitcast_fusion) | data formatting | bytes 9699328 | tf_op jit(solution)/shard_map/all_to_all | solution.py:98
  257.4 6.3 %all-to-all-start.4 = ((f32[16,1,75776]{2,1,0:T(1,128)}), f32[16,1,75776]{2,1,0:T(1,128)}, u32[]{:S(2)}, u32[]{:S(2)}) async-start(f32[16,1,75776]{2,1,0:T(1,128)} %copy.19), calls=%async_computation.4 | async-start | bytes 9699328 | tf_op jit(solution)/shard_map/all_to_all | solution.py:98
  263.7 1.1 fusion.8
  264.8 55.4 %all-to-all-done.4 = f32[16,1,75776]{2,1,0:T(1,128)} async-done(((f32[16,1,75776]{2,1,0:T(1,128)}), f32[16,1,75776]{2,1,0:T(1,128)}, u32[]{:S(2)}, u32[]{:S(2)}) %all-to-all-start.4) | async-done | bytes 4849696 | tf_op jit(solution)/shard_map/all_to_all | solution.py:98
  320.2 5.4 %reduce_sum.59 = f32[75776]{0:T(1024)S(1)} reduce(f32[16,1,75776]{2,1,0:T(1,128)} %all-to-all-done.4, f32[]{:T(128)} %constant.5.clone.1), dimensions={0,1}, to_apply=%region_5.6 | reduce | flops 1136640 | bytes 5152772 | tf_op jit(solution)/shard_map/reduce_sum | solution.py:99
  325.6 1.2 broadcast_in_dim.8
  326.8 4.4 all-to-all-start.5
  331.2 2.0 fusion.10
  333.3 2.1 slice.92
  335.4 0.8 slice.63
  336.2 6.2 %all-to-all-done.5 = f32[16,1,10240]{2,1,0:T(1,128)S(1)} async-done(((f32[16,1,10240]{2,1,0:T(1,128)}), f32[16,1,10240]{2,1,0:T(1,128)S(1)}, u32[]{:S(2)}, u32[]{:S(2)}) %all-to-all-start.5) | async-done | bytes 655392 | tf_op jit(solution)/shard_map/all_to_all | solution.py:105
  342.4 2.5 reduce.1
  344.9 1.3 slice.65
  346.9 0.8 slice.79
  348.3 106.6 %all-reduce.3.cloned.1.call-done = (f32[512,128]{1,0:T(8,128)}, f32[128,512]{1,0:T(8,128)}) async-done(((f32[512,128]{1,0:T(8,128)}, f32[128,512]{1,0:T(8,128)}), (f32[512,128]{1,0:T(8,128)}, f32[128,512]{1,0:T(8,128)})) %all-reduce.3.cloned.1.call-update) | async-done | bytes 524304 | tf_op jit(solution)/shard_map/psum | solution.py:136
  454.9 1.7 copy.23
  456.5 1.7 copy.24
  (53 shorter events, 3.9 us)
Async XLA Ops:
  7.2 1.6 copy-start
  58.9 11.0 %copy-start.3 = (f32[512,512]{1,0:T(8,128)}, f32[512,512]{1,0:T(8,128)S(1)}, u32[]{:S(2)}) copy-start(f32[512,512]{1,0:T(8,128)S(1)} %fusion.15.mid_ref) | copy-start | bytes 3145732
  58.9 6.2 %collective-permute-start = (f32[31,512]{1,0:T(8,128)S(1)}, f32[31,512]{1,0:T(8,128)S(1)}, u32[]{:S(2)}, u32[]{:S(2)}) collective-permute-start(f32[31,512]{1,0:T(8,128)S(1)} %get-tuple-element.17), channel_id=1, source_target_pairs={{0,1},{1,2},{2,3},{3,4},{4,5},{5,6},{6,7},{7,8},{8,9},{9,10},{10,1... | collective-permute-start | bytes 190472 | tf_op jit(solution)/shard_map/ppermute | solution.py:17
  63.2 5.6 %collective-permute-start.1 = (f32[31,512]{1,0:T(8,128)S(1)}, f32[31,512]{1,0:T(8,128)S(1)}, u32[]{:S(2)}, u32[]{:S(2)}) collective-permute-start(f32[31,512]{1,0:T(8,128)S(1)} %get-tuple-element.18), channel_id=1, source_target_pairs={{1,0},{2,1},{3,2},{4,3},{5,4},{6,5},{7,6},{8,7},{9,8},{10,9},{11,1... | collective-permute-start | bytes 190472 | tf_op jit(solution)/shard_map/ppermute | solution.py:20
  69.9 8.3 %copy-start.9 = (bf16[512,128]{1,0:T(8,128)(2,1)S(1)}, bf16[512,128]{1,0:T(8,128)(2,1)}, u32[]{:S(2)}) copy-start(bf16[512,128]{1,0:T(8,128)(2,1)} %param.13) | copy-start | bytes 393220
  69.9 8.3 %copy-start.14 = (f32[512]{0:T(512)S(1)}, f32[512]{0:T(512)}, u32[]{:S(2)}) copy-start(f32[512]{0:T(512)} %param.12) | copy-start | bytes 6148
  76.7 3.1 copy-start.13
  76.7 3.4 copy-start.7
  79.8 0.9 copy-start.5
  80.4 0.7 copy-start.10
  82.6 54.8 %all-to-all-start.2 = ((f32[16,2,32,512]{3,2,1,0:T(8,128)}), f32[16,2,32,512]{3,2,1,0:T(8,128)}, u32[]{:S(2)}, u32[]{:S(2)}) async-start(f32[16,2,32,512]{3,2,1,0:T(8,128)} %pad_maximum_fusion), calls=%async_computation.2 | async-start | bytes 4194304 | tf_op jit(solution)/shard_map/all_to_all | solution.py:98
  87.0 52.2 %copy-start.1 = (f32[512,512]{1,0:T(8,128)S(1)}, f32[512,512]{1,0:T(8,128)}, u32[]{:S(2)}) copy-start(f32[512,512]{1,0:T(8,128)} %shard_map.135) | copy-start | bytes 3145732
  193.6 1.3 copy-start.4
  193.6 1.4 copy-start.8
  195.3 12.9 %copy-start.2 = (f32[512,512]{1,0:T(8,128)}, f32[512,512]{1,0:T(8,128)S(1)}, u32[]{:S(2)}) copy-start(f32[512,512]{1,0:T(8,128)S(1)} %multiply_subtract_fusion.d_ref) | copy-start | bytes 3145732
  195.4 9.4 %collective-permute-start.2 = (f32[31,512]{1,0:T(8,128)S(1)}, f32[31,512]{1,0:T(8,128)S(1)}, u32[]{:S(2)}, u32[]{:S(2)}) collective-permute-start(f32[31,512]{1,0:T(8,128)S(1)} %get-tuple-element.15), channel_id=1, source_target_pairs={{0,1},{1,2},{2,3},{3,4},{4,5},{5,6},{6,7},{7,8},{8,9},{9,10},{10,1... | collective-permute-start | bytes 190472 | tf_op jit(solution)/shard_map/ppermute | solution.py:17
  202.7 5.6 %collective-permute-start.3 = (f32[31,512]{1,0:T(8,128)S(1)}, f32[31,512]{1,0:T(8,128)S(1)}, u32[]{:S(2)}, u32[]{:S(2)}) collective-permute-start(f32[31,512]{1,0:T(8,128)S(1)} %get-tuple-element.16), channel_id=1, source_target_pairs={{1,0},{2,1},{3,2},{4,3},{5,4},{6,5},{7,6},{8,7},{9,8},{10,9},{11,1... | collective-permute-start | bytes 190472 | tf_op jit(solution)/shard_map/ppermute | solution.py:20
  223.0 6.2 %copy-start.12 = (f32[63,512]{1,0:T(8,128)S(1)}, f32[63,512]{1,0:T(8,128)}, u32[]{:S(2)}) copy-start(f32[63,512]{1,0:T(8,128)} %get-tuple-element.10) | copy-start | bytes 387076
  257.4 6.3 %copy-start.11 = (bf16[512,128]{1,0:T(8,128)(2,1)S(1)}, bf16[512,128]{1,0:T(8,128)(2,1)}, u32[]{:S(2)}) copy-start(bf16[512,128]{1,0:T(8,128)(2,1)} %copy-done.10) | copy-start | bytes 393220
  257.4 62.8 %all-to-all-start.4 = ((f32[16,1,75776]{2,1,0:T(1,128)}), f32[16,1,75776]{2,1,0:T(1,128)}, u32[]{:S(2)}, u32[]{:S(2)}) async-start(f32[16,1,75776]{2,1,0:T(1,128)} %copy.19), calls=%async_computation.4 | async-start | bytes 9699328 | tf_op jit(solution)/shard_map/all_to_all | solution.py:98
  264.8 66.4 %copy-start.6 = (f32[512,128]{1,0:T(8,128)S(1)}, f32[512,128]{1,0:T(8,128)}, u32[]{:S(2)}) copy-start(f32[512,128]{1,0:T(8,128)} %copy-done.5) | copy-start | bytes 786436
  326.8 15.6 %all-to-all-start.5 = ((f32[16,1,10240]{2,1,0:T(1,128)}), f32[16,1,10240]{2,1,0:T(1,128)S(1)}, u32[]{:S(2)}, u32[]{:S(2)}) async-start(f32[16,1,10240]{2,1,0:T(1,128)} %broadcast_in_dim.8), calls=%async_computation.5 | async-start | bytes 1310720 | tf_op jit(solution)/shard_map/all_to_all | solution.py:105
  331.1 123.7 %all-reduce.3.cloned.1.call-start = ((), (), s32[]{:S(2)}) async-start(), calls=%async_computation.6 | async-start | bytes 1048576 | tf_op jit(solution)/shard_map/psum | solution.py:136
Sparse Core Ops, SparseCore 0:
  335.2 119.6 all-reduce.2

commit v3 on v2

--- a/solution.py
+++ b/solution.py
@@ -133,7 +133,6 @@
     sig = jax.nn.sigmoid(pre)
     dpre = (dact * sig * (1.0 + pre * (1.0 - sig))).astype(jnp.bfloat16)
     local_w_one = over_time(normed, dpre)
-    grad_w_one, grad_w_two = lax.psum((local_w_one, local_w_two), "tm")
     partial_normed = jnp.dot(dpre, w_one.T, preferred_element_type=jnp.float32)
     both = jnp.stack([split_rows(partial_mix, nn), split_rows(partial_normed, nn)], axis=1)
     summed = scatter_sum(both, "neuron")
@@ -151,20 +150,20 @@
     local_proj = over_time(latent, dlifted)
     dlatent = jnp.dot(dlifted, proj.T, preferred_element_type=jnp.float32).astype(jnp.bfloat16)
     local_readin = over_time(signal, dlatent)
-    small = jnp.concatenate(
-        [local_proj.reshape(-1), local_kernel.reshape(-1), local_gain.reshape(-1)]
-    )
-    readin_part = local_readin.reshape(nt, -1)
-    packed = jnp.concatenate([readin_part, small.reshape(nt, -1)], axis=1)
-    reduced = scatter_sum(packed, "tm")
+    grads = (local_proj, local_kernel, local_gain, local_w_one, local_w_two)
+    width = local_readin.shape[1]
+    small = jnp.concatenate([g.reshape(-1) for g in grads]).reshape(nt, -1, width)
+    readin_part = local_readin.reshape(nt, -1, width)
     cut = readin_part.shape[1]
-    grad_readin = reduced[:cut].reshape(-1, local_readin.shape[1])
+    reduced = scatter_sum(jnp.concatenate([readin_part, small], axis=1), "tm")
+    grad_readin = reduced[:cut]
     small_sum = gather_all(reduced[cut:], "tm").reshape(-1)
-    n_proj = local_proj.size
-    n_kernel = local_kernel.size
-    grad_proj = small_sum[:n_proj].reshape(local_proj.shape)
-    grad_kernel = small_sum[n_proj:n_proj + n_kernel].reshape(local_kernel.shape)
-    grad_gain = small_sum[n_proj + n_kernel:]
+    outs = []
+    at = 0
+    for g in grads:
+        outs.append(small_sum[at:at + g.size].reshape(g.shape))
+        at += g.size
+    grad_proj, grad_kernel, grad_gain, grad_w_one, grad_w_two = outs
     return (denoised, grad_readin, grad_proj, grad_kernel, grad_gain, grad_w_one, grad_w_two)
 
 

time: 466 us -> 350 us (0.75)
  waiting for transfers between devices: 226 us -> 70.9 us
  blocking collectives: 99.5 us -> 168 us
  between operations: 14.3 us -> 0.95 us
  other arithmetic: 21.5 us -> 13.8 us
  starting transfers between devices: 30.6 us -> 24.8 us
    psum x1 -> x0, waiting for transfers between devices: 107 us -> none  [body(): grad_w_one, grad_w_two = lax.psum((local_w_one, local_w_two), 'tm')]
    all_to_all x1 -> x2, blocking collectives: 28.6 us -> 96.9 us  [scatter_sum(): got = lax.all_to_all(parts, axis, 0, 0, tiled=False)]
    all_to_all x2 -> x1, waiting for transfers between devices: 106 us -> 50.4 us  [scatter_sum(): got = lax.all_to_all(parts, axis, 0, 0, tiled=False)]
    all_to_all x1 -> x0, local copies, waits for them, and re-layouts: 9.59 us -> none  [scatter_sum(): got = lax.all_to_all(parts, axis, 0, 0, tiled=False)]
    slice x6 -> x8, local copies, waits for them, and re-layouts: 4.15 us -> 13 us  [the longest x7 12.2 us: body(): outs.append(small_sum[at:at + g.size].reshape(g.shape))]
    all_to_all x1, waiting for transfers between devices: 6.2 us -> 14.5 us  [gather_all(): return lax.all_to_all(spread, axis, 0, 0, tiled=False)]
    all_to_all x2 -> x0, other arithmetic: 7.42 us -> none  [the longest x1 4.87 us: scatter_sum(): got = lax.all_to_all(parts, axis, 0, 0, tiled=False)]
    all_to_all x2 -> x1, starting transfers between devices: 10.7 us -> 4.42 us  [scatter_sum(): got = lax.all_to_all(parts, axis, 0, 0, tiled=False)]
  transfers between devices with their start and end apart: 8 -> 6, of which waited for: 6 -> 4; matrix products, arithmetic and copies ran while one was open for 3% -> 1% of each run, Pallas kernels for 0% -> 0%
where the time goes in v3:
time: 350 us; the launch traced here: 349 us
  blocking collectives  168 us (48%)
  waiting for transfers between devices  70.9 us (20%)
  local copies, waits for them, and re-layouts  36.5 us (10%)
  starting transfers between devices  24.8 us (7%)
  Pallas kernels  18.2 us (5%)
  matrix products  15.7 us (4%)
  other arithmetic  13.8 us (4%)
    all_to_all x2, blocking collectives, scatter_sum(): got = lax.all_to_all(parts, axis, 0, 0, tiled=False)  96.9 us
    all_to_all x2, blocking collectives, gather_all(): return lax.all_to_all(spread, axis, 0, 0, tiled=False)  70.9 us
    all_to_all x1, waiting for transfers between devices, scatter_sum(): got = lax.all_to_all(parts, axis, 0, 0, tiled=False)  50.4 us
    all_to_all x1, waiting for transfers between devices, gather_all(): return lax.all_to_all(spread, axis, 0, 0, tiled=False)  14.5 us
    slice x7, local copies, waits for them, and re-layouts, body(): outs.append(small_sum[at:at + g.size].reshape(g.shape))  12.2 us
    ppermute x2, starting transfers between devices, with_halo(): lax.ppermute(lax.slice_in_dim(block, block.shape[dim] - width, None, axis...  11.5 us
    pallas_call x1, Pallas kernels, bwd_conv(): pl.pallas_call(_bwd_conv_kernel, out_shape=(jax.ShapeDtypeStruct((rows, w...  11.4 us
    unnamed x38, local copies, waits for them, and re-layouts  11 us
  transfers between devices with their start and end apart: 6, of which 4 were waited for; matrix products, arithmetic and copies ran while one was open for 1% of the time, Pallas kernels for 0%

profile of v3, /device:TPU:1, one launch (start us, length us, event | category | flops | bytes accessed | tf_op | source)
XLA Modules:
  0.0 348.7 jit_solution(13946242466195453351)
XLA Ops:
  0.6 1.6 copy-done
  2.2 3.4 fusion.13
  5.7 28.6 %all_to_all.30 = f32[16,32,256]{2,1,0:T(8,128)S(1)} all-to-all(f32[16,32,256]{2,1,0:T(8,128)S(1)} %bitcast.76), channel_id=1, replica_groups=mesh['neuron'=16,'tm'=16] {'neuron'}, dimensions={0} | all-to-all | bytes 1048576 | tf_op jit(solution)/shard_map/all_to_all | solution.py:98
  34.3 16.8 %all_to_all.31 = bf16[16,32,256]{2,1,0:T(8,128)(2,1)S(1)} all-to-all(bf16[16,32,256]{2,1,0:T(8,128)(2,1)S(1)} %broadcast_in_dim.6), channel_id=1, replica_groups=mesh['neuron'=16,'tm'=16] {'neuron'}, dimensions={0} | all-to-all | bytes 524288 | tf_op jit(solution)/shard_map/all_to_all | solution.py:105
  51.1 1.2 fusion.14.mid_ref
  52.4 4.2 %collective-permute-start = (f32[31,512]{1,0:T(8,128)S(1)}, f32[31,512]{1,0:T(8,128)S(1)}, u32[]{:S(2)}, u32[]{:S(2)}) collective-permute-start(f32[31,512]{1,0:T(8,128)S(1)} %get-tuple-element.22), channel_id=1, source_target_pairs={{0,1},{1,2},{2,3},{3,4},{4,5},{5,6},{6,7},{7,8},{8,9},{9,10},{10,1... | collective-permute-start | bytes 190472 | tf_op jit(solution)/shard_map/ppermute | solution.py:17
  56.6 1.9 collective-permute-start.1
  58.6 3.6 %collective-permute-done.1 = f32[31,512]{1,0:T(8,128)S(1)} collective-permute-done((f32[31,512]{1,0:T(8,128)S(1)}, f32[31,512]{1,0:T(8,128)S(1)}, u32[]{:S(2)}, u32[]{:S(2)}) %collective-permute-start.1) | collective-permute-done | bytes 63520 | tf_op jit(solution)/shard_map/ppermute | solution.py:20
  62.2 1.2 pad_maximum_fusion.2.x_ref
  63.4 6.8 %shard_map.135 = f32[512,512]{1,0:T(8,128)} custom-call(f32[574,512]{1,0:T(8,128)} %pad_maximum_fusion.2.x_ref, f32[512,512]{1,0:T(8,128)} %copy-done.3, f32[63,512]{1,0:T(8,128)} %k_ref.3), custom_call_target="tpu_custom_call" | custom-call | tf_op jit(solution)/shard_map/pallas_call | solution.py:38
  70.2 1.5 multiply_reduce_fusion.1
  73.8 1.5 pad_maximum_fusion.1
  75.3 4.4 %all-to-all-start.2 = ((f32[16,2,32,512]{3,2,1,0:T(8,128)}), f32[16,2,32,512]{3,2,1,0:T(8,128)}, u32[]{:S(2)}, u32[]{:S(2)}) async-start(f32[16,2,32,512]{3,2,1,0:T(8,128)} %pad_maximum_fusion.1), calls=%async_computation.2 | async-start | bytes 4194304 | tf_op jit(solution)/shard_map/all_to_all | solution.py:98
  79.7 50.4 %all-to-all-done.2 = f32[16,2,32,512]{3,2,1,0:T(8,128)} async-done(((f32[16,2,32,512]{3,2,1,0:T(8,128)}), f32[16,2,32,512]{3,2,1,0:T(8,128)}, u32[]{:S(2)}, u32[]{:S(2)}) %all-to-all-start.2) | async-done | bytes 2097184 | tf_op jit(solution)/shard_map/all_to_all | solution.py:98
  130.1 1.8 reduce_sum.56
  132.2 54.1 %all_to_all.32 = f32[16,2,32,512]{3,2,1,0:T(8,128)S(1)} all-to-all(f32[16,2,32,512]{3,2,1,0:T(8,128)S(1)} %broadcast_in_dim.7), channel_id=1, replica_groups=mesh['neuron'=16,'tm'=16] {'neuron'}, dimensions={0} | all-to-all | bytes 4194304 | tf_op jit(solution)/shard_map/all_to_all | solution.py:105
  186.7 0.9 copy-done.4
  188.2 7.3 %collective-permute-start.2 = (f32[31,512]{1,0:T(8,128)S(1)}, f32[31,512]{1,0:T(8,128)S(1)}, u32[]{:S(2)}, u32[]{:S(2)}) collective-permute-start(f32[31,512]{1,0:T(8,128)S(1)} %get-tuple-element.20), channel_id=1, source_target_pairs={{0,1},{1,2},{2,3},{3,4},{4,5},{5,6},{6,7},{7,8},{8,9},{9,10},{10,1... | collective-permute-start | bytes 190472 | tf_op jit(solution)/shard_map/ppermute | solution.py:17
  195.5 2.1 collective-permute-start.3
  197.9 0.8 copy.27
  198.6 2.4 collective-permute-done.3
  201.1 1.2 pad_maximum_fusion.3.g_ref
  202.2 11.4 %shard_map.136 = (bf16[512,512]{1,0:T(8,128)(2,1)}, f32[63,512]{1,0:T(8,128)}) custom-call(f32[574,512]{1,0:T(8,128)} %pad_maximum_fusion.3.g_ref, f32[512,512]{1,0:T(8,128)} %copy-done.2, f32[574,512]{1,0:T(8,128)} %pad_maximum_fusion.2.x_ref, f32[63,512]{1,0:T(8,128)} %k_ref.3), custom_call_target="tpu_custom_call" | custom-call | tf_op jit(solution)/shard_map/pallas_call | solution.py:71
  213.6 2.2 convolution_bitcast_fusion.2
  215.8 6.2 %convolution_bitcast_fusion.1 = f32[4096,256]{0,1:T(8,128)} fusion(bf16[512,4096]{1,0:T(8,128)(2,1)} %param.8, bf16[512,512]{1,0:T(8,128)(2,1)} %get-tuple-element.9, bf16[256,512]{1,0:T(8,128)(2,1)} %param.10), kind=kOutput, calls=%fused_computation.2 | convolution fusion | flops 1208090624 | bytes 9175040 | tf_op jit(solution)/shard_map/dot_general | solution.py:92
  222.1 1.2 copy.26
  223.3 0.8 constant_dynamic-update-slice_fusion.3
  224.1 1.6 constant_dynamic-update-slice_fusion.2
  225.7 1.3 constant_dynamic-update-slice_fusion.1
  227.0 1.2 fusion
  228.2 0.7 constant_dynamic-update-slice_fusion
  228.9 2.6 reshape.85
  231.4 5.6 %copy.22 = f32[4096,256]{1,0:T(8,128)} copy(f32[4096,256]{0,1:T(8,128)} %convolution_bitcast_fusion.1) | data formatting | bytes 8388608 | tf_op jit(solution)/shard_map/reshape | solution.py:156
  237.1 3.1 pad_maximum_fusion
  240.1 68.3 %all_to_all.33 = f32[16,328,256]{2,1,0:T(8,128)} all-to-all(f32[16,328,256]{2,1,0:T(8,128)S(1)} %pad_maximum_fusion), channel_id=1, replica_groups=mesh['neuron'=16,'tm'=16] {'tm'}, dimensions={0} | all-to-all | bytes 10747904 | tf_op jit(solution)/shard_map/all_to_all | solution.py:98
  308.5 2.9 reduce_sum.59
  311.4 1.1 broadcast_in_dim.8
  312.5 4.8 %all-to-all-start.5 = ((f32[16,72,256]{2,1,0:T(8,128)}), f32[16,72,256]{2,1,0:T(8,128)}, u32[]{:S(2)}, u32[]{:S(2)}) async-start(f32[16,72,256]{2,1,0:T(8,128)} %broadcast_in_dim.8), calls=%async_computation.5 | async-start | bytes 2359296 | tf_op jit(solution)/shard_map/all_to_all | solution.py:105
  317.2 2.1 slice.96
  319.3 0.7 slice.79
  320.1 14.5 %all-to-all-done.5 = f32[16,72,256]{2,1,0:T(8,128)} async-done(((f32[16,72,256]{2,1,0:T(8,128)}), f32[16,72,256]{2,1,0:T(8,128)}, u32[]{:S(2)}, u32[]{:S(2)}) %all-to-all-start.5) | async-done | bytes 1179680 | tf_op jit(solution)/shard_map/all_to_all | solution.py:105
  334.6 2.6 slice.64
  337.1 1.6 slice.82
  338.7 1.7 slice.85
  340.4 1.9 slice.81
  342.2 1.9 copy.28
  344.7 2.3 slice.68
  347.0 1.7 slice.84
  (53 shorter events, 4.3 us)
Async XLA Ops:
  0.6 1.6 copy-start
  52.4 11.0 %copy-start.3 = (f32[512,512]{1,0:T(8,128)}, f32[512,512]{1,0:T(8,128)S(1)}, u32[]{:S(2)}) copy-start(f32[512,512]{1,0:T(8,128)S(1)} %fusion.14.mid_ref) | copy-start | bytes 3145732
  52.4 6.2 %collective-permute-start = (f32[31,512]{1,0:T(8,128)S(1)}, f32[31,512]{1,0:T(8,128)S(1)}, u32[]{:S(2)}, u32[]{:S(2)}) collective-permute-start(f32[31,512]{1,0:T(8,128)S(1)} %get-tuple-element.22), channel_id=1, source_target_pairs={{0,1},{1,2},{2,3},{3,4},{4,5},{5,6},{6,7},{7,8},{8,9},{9,10},{10,1... | collective-permute-start | bytes 190472 | tf_op jit(solution)/shard_map/ppermute | solution.py:17
  56.6 5.6 %collective-permute-start.1 = (f32[31,512]{1,0:T(8,128)S(1)}, f32[31,512]{1,0:T(8,128)S(1)}, u32[]{:S(2)}, u32[]{:S(2)}) collective-permute-start(f32[31,512]{1,0:T(8,128)S(1)} %get-tuple-element.23), channel_id=1, source_target_pairs={{1,0},{2,1},{3,2},{4,3},{5,4},{6,5},{7,6},{8,7},{9,8},{10,9},{11,1... | collective-permute-start | bytes 190472 | tf_op jit(solution)/shard_map/ppermute | solution.py:20
  63.4 8.3 %copy-start.10 = (bf16[512,128]{1,0:T(8,128)(2,1)S(1)}, bf16[512,128]{1,0:T(8,128)(2,1)}, u32[]{:S(2)}) copy-start(bf16[512,128]{1,0:T(8,128)(2,1)} %param.13) | copy-start | bytes 393220
  63.4 8.3 %copy-start.15 = (f32[512]{0:T(512)S(1)}, f32[512]{0:T(512)}, u32[]{:S(2)}) copy-start(f32[512]{0:T(512)} %param.12) | copy-start | bytes 6148
  70.2 1.5 copy-start.1
  70.2 1.9 copy-start.14
  71.8 1.0 copy-start.8
  72.1 1.0 copy-start.6
  73.1 0.7 copy-start.11
  75.3 54.8 %all-to-all-start.2 = ((f32[16,2,32,512]{3,2,1,0:T(8,128)}), f32[16,2,32,512]{3,2,1,0:T(8,128)}, u32[]{:S(2)}, u32[]{:S(2)}) async-start(f32[16,2,32,512]{3,2,1,0:T(8,128)} %pad_maximum_fusion.1), calls=%async_computation.2 | async-start | bytes 4194304 | tf_op jit(solution)/shard_map/all_to_all | solution.py:98
  186.2 1.4 copy-start.4
  186.3 1.4 copy-start.9
  187.8 9.8 %copy-start.7 = (f32[512,128]{1,0:T(8,128)S(1)}, f32[512,128]{1,0:T(8,128)}, u32[]{:S(2)}) copy-start(f32[512,128]{1,0:T(8,128)} %copy-done.6) | copy-start | bytes 786436
  188.1 12.9 %copy-start.2 = (f32[512,512]{1,0:T(8,128)}, f32[512,512]{1,0:T(8,128)S(1)}, u32[]{:S(2)}) copy-start(f32[512,512]{1,0:T(8,128)S(1)} %multiply_subtract_fusion.d_ref) | copy-start | bytes 3145732
  188.2 10.5 %collective-permute-start.2 = (f32[31,512]{1,0:T(8,128)S(1)}, f32[31,512]{1,0:T(8,128)S(1)}, u32[]{:S(2)}, u32[]{:S(2)}) collective-permute-start(f32[31,512]{1,0:T(8,128)S(1)} %get-tuple-element.20), channel_id=1, source_target_pairs={{0,1},{1,2},{2,3},{3,4},{4,5},{5,6},{6,7},{7,8},{8,9},{9,10},{10,1... | collective-permute-start | bytes 190472 | tf_op jit(solution)/shard_map/ppermute | solution.py:17
  195.5 5.6 %collective-permute-start.3 = (f32[31,512]{1,0:T(8,128)S(1)}, f32[31,512]{1,0:T(8,128)S(1)}, u32[]{:S(2)}, u32[]{:S(2)}) collective-permute-start(f32[31,512]{1,0:T(8,128)S(1)} %get-tuple-element.21), channel_id=1, source_target_pairs={{1,0},{2,1},{3,2},{4,3},{5,4},{6,5},{7,6},{8,7},{9,8},{10,9},{11,1... | collective-permute-start | bytes 190472 | tf_op jit(solution)/shard_map/ppermute | solution.py:20
  215.8 6.2 %copy-start.13 = (f32[63,512]{1,0:T(8,128)S(1)}, f32[63,512]{1,0:T(8,128)}, u32[]{:S(2)}) copy-start(f32[63,512]{1,0:T(8,128)} %get-tuple-element.10) | copy-start | bytes 387076
  222.0 5.0 %copy-start.12 = (bf16[512,128]{1,0:T(8,128)(2,1)S(1)}, bf16[512,128]{1,0:T(8,128)(2,1)}, u32[]{:S(2)}) copy-start(bf16[512,128]{1,0:T(8,128)(2,1)} %copy-done.11) | copy-start | bytes 393220
  223.3 4.9 %copy-start.5 = (f32[16,4,8,128]{3,1,2,0:T(4,128)S(1)}, f32[16,4,8,128]{3,1,2,0:T(4,128)}, u32[]{:S(2)}) copy-start(f32[16,4,8,128]{3,1,2,0:T(4,128)} %copy.27) | copy-start | bytes 786436
  312.5 22.1 %all-to-all-start.5 = ((f32[16,72,256]{2,1,0:T(8,128)}), f32[16,72,256]{2,1,0:T(8,128)}, u32[]{:S(2)}, u32[]{:S(2)}) async-start(f32[16,72,256]{2,1,0:T(8,128)} %broadcast_in_dim.8), calls=%async_computation.5 | async-start | bytes 2359296 | tf_op jit(solution)/shard_map/all_to_all | solution.py:105

commit v4 on v3

--- a/solution.py
+++ b/solution.py
@@ -134,13 +134,12 @@
     dpre = (dact * sig * (1.0 + pre * (1.0 - sig))).astype(jnp.bfloat16)
     local_w_one = over_time(normed, dpre)
     partial_normed = jnp.dot(dpre, w_one.T, preferred_element_type=jnp.float32)
-    both = jnp.stack([split_rows(partial_mix, nn), split_rows(partial_normed, nn)], axis=1)
-    summed = scatter_sum(both, "neuron")
+    dnormed_rows = scatter_sum(split_rows(partial_normed, nn), "neuron")
+    dnormed = gather_all(dnormed_rows, "neuron").reshape(rows, -1)
+    mix_rows = scatter_sum(split_rows(partial_mix, nn), "neuron")
     mixed_rows = lax.dynamic_slice_in_dim(mixed, me * share, share, 0)
-    denoised_rows = (mixed_rows + summed[0]).astype(jnp.bfloat16).astype(jnp.float32)
-    back = gather_all(jnp.stack([denoised_rows, summed[1]]), "neuron")
-    denoised = back[:, 0].reshape(rows, -1).astype(jnp.bfloat16)
-    dnormed = back[:, 1].reshape(rows, -1)
+    denoised_rows = (mixed_rows + mix_rows).astype(jnp.bfloat16)
+    denoised = gather_all(denoised_rows, "neuron").reshape(rows, -1)
     local_gain = jnp.sum(dnormed * mixed * scale, axis=0)
     dgained = dnormed * gain[None, :]
     inner = jnp.mean(dgained * mixed, axis=1, keepdims=True)
@@ -152,17 +151,18 @@
     local_readin = over_time(signal, dlatent)
     grads = (local_proj, local_kernel, local_gain, local_w_one, local_w_two)
     width = local_readin.shape[1]
-    small = jnp.concatenate([g.reshape(-1) for g in grads]).reshape(nt, -1, width)
+    small = jnp.concatenate([g.reshape(-1, width) for g in grads]).reshape(nt, -1, width)
     readin_part = local_readin.reshape(nt, -1, width)
     cut = readin_part.shape[1]
     reduced = scatter_sum(jnp.concatenate([readin_part, small], axis=1), "tm")
     grad_readin = reduced[:cut]
-    small_sum = gather_all(reduced[cut:], "tm").reshape(-1)
+    small_sum = gather_all(reduced[cut:], "tm").reshape(-1, width)
     outs = []
     at = 0
     for g in grads:
-        outs.append(small_sum[at:at + g.size].reshape(g.shape))
-        at += g.size
+        count = g.size // width
+        outs.append(small_sum[at:at + count].reshape(g.shape))
+        at += count
     grad_proj, grad_kernel, grad_gain, grad_w_one, grad_w_two = outs
     return (denoised, grad_readin, grad_proj, grad_kernel, grad_gain, grad_w_one, grad_w_two)
 

time: 350 us -> 339 us (0.969)
  blocking collectives: 168 us -> 76.6 us
  waiting for transfers between devices: 70.9 us -> 121 us
  starting transfers between devices: 24.8 us -> 43.9 us
  other arithmetic: 13.8 us -> 18.6 us
  matrix products: 15.7 us -> 19.6 us
    all_to_all x2 -> x1, blocking collectives: 70.9 us -> 16.8 us  [gather_all(): return lax.all_to_all(spread, axis, 0, 0, tiled=False)]
    all_to_all x1 -> x3, waiting for transfers between devices: 14.5 us -> 56.4 us  [gather_all(): return lax.all_to_all(spread, axis, 0, 0, tiled=False)]
    all_to_all x2, blocking collectives: 96.9 us -> 59.8 us  [scatter_sum(): got = lax.all_to_all(parts, axis, 0, 0, tiled=False)]
    all_to_all x1 -> x3, starting transfers between devices: 4.77 us -> 21.2 us  [gather_all(): return lax.all_to_all(spread, axis, 0, 0, tiled=False)]
    slice x11 -> x4, local copies, waits for them, and re-layouts: 14.4 us -> 2.23 us  [the longest x3 2.23 us: body(): outs.append(small_sum[at:at + count].reshape(g.shape))]
    all_to_all x1 -> x2, waiting for transfers between devices: 50.4 us -> 60.8 us  [scatter_sum(): got = lax.all_to_all(parts, axis, 0, 0, tiled=False)]
    reshape x2 -> x9, local copies, waits for them, and re-layouts: 2.59 us -> 12.3 us  [the longest x5 6.27 us: body(): g.reshape(-1, width)]
    all_to_all x1 -> x2, starting transfers between devices: 4.42 us -> 12.1 us  [scatter_sum(): got = lax.all_to_all(parts, axis, 0, 0, tiled=False)]
  transfers between devices with their start and end apart: 6 -> 9, of which waited for: 4 -> 5; matrix products, arithmetic and copies ran while one was open for 1% -> 14% of each run, Pallas kernels for 0% -> 3%
where the time goes in v4:
time: 339 us; the launch traced here: 338 us
  waiting for transfers between devices  121 us (36%)
  blocking collectives  76.6 us (23%)
  starting transfers between devices  43.9 us (13%)
  local copies, waits for them, and re-layouts  38.9 us (11%)
  matrix products  19.6 us (6%)
  other arithmetic  18.6 us (5%)
  Pallas kernels  18.2 us (5%)
    all_to_all x2, waiting for transfers between devices, scatter_sum(): got = lax.all_to_all(parts, axis, 0, 0, tiled=False)  60.8 us
    all_to_all x2, blocking collectives, scatter_sum(): got = lax.all_to_all(parts, axis, 0, 0, tiled=False)  59.8 us
    all_to_all x3, waiting for transfers between devices, gather_all(): return lax.all_to_all(spread, axis, 0, 0, tiled=False)  56.4 us
    all_to_all x3, starting transfers between devices, gather_all(): return lax.all_to_all(spread, axis, 0, 0, tiled=False)  21.2 us
    all_to_all x1, blocking collectives, gather_all(): return lax.all_to_all(spread, axis, 0, 0, tiled=False)  16.8 us
    all_to_all x2, starting transfers between devices, scatter_sum(): got = lax.all_to_all(parts, axis, 0, 0, tiled=False)  12.1 us
    pallas_call x1, Pallas kernels, bwd_conv(): pl.pallas_call(_bwd_conv_kernel, out_shape=(jax.ShapeDtypeStruct((rows, w...  11.4 us
    dot_general x4, matrix products, over_time(): lax.dot_general(left, right, (((0,), (0,)), ((), ())), preferred_element_...  10.5 us
  transfers between devices with their start and end apart: 9, of which 5 were waited for; matrix products, arithmetic and copies ran while one was open for 14% of the time, Pallas kernels for 3%

profile of v4, /device:TPU:1, one launch (start us, length us, event | category | flops | bytes accessed | tf_op | source)
XLA Modules:
  0.0 337.6 jit_solution(13157500079591014287)
XLA Ops:
  0.6 1.6 copy-done
  2.2 3.4 %fusion.11 = f32[512,256]{1,0:T(8,128)S(1)} fusion(bf16[512,4096]{1,0:T(8,128)(2,1)} %param.8, bf16[4096,256]{1,0:T(8,128)(2,1)S(1)} %copy-done), kind=kOutput, calls=%fused_computation.30 | convolution fusion | flops 1073741824 | bytes 6815744 | tf_op jit(solution)/shard_map/dot_general | solution.py:120
  5.7 28.6 %all_to_all.40 = f32[16,32,256]{2,1,0:T(8,128)S(1)} all-to-all(f32[16,32,256]{2,1,0:T(8,128)S(1)} %bitcast.52), channel_id=1, replica_groups=mesh['neuron'=16,'tm'=16] {'neuron'}, dimensions={0} | all-to-all | bytes 1048576 | tf_op jit(solution)/shard_map/all_to_all | solution.py:98
  34.3 16.8 %all_to_all.41 = bf16[16,32,256]{2,1,0:T(8,128)(2,1)S(1)} all-to-all(bf16[16,32,256]{2,1,0:T(8,128)(2,1)S(1)} %broadcast_in_dim.8), channel_id=1, replica_groups=mesh['neuron'=16,'tm'=16] {'neuron'}, dimensions={0} | all-to-all | bytes 524288 | tf_op jit(solution)/shard_map/all_to_all | solution.py:105
  51.1 1.2 fusion.12.mid_ref
  52.4 4.2 %collective-permute-start = (f32[31,512]{1,0:T(8,128)S(1)}, f32[31,512]{1,0:T(8,128)S(1)}, u32[]{:S(2)}, u32[]{:S(2)}) collective-permute-start(f32[31,512]{1,0:T(8,128)S(1)} %get-tuple-element.24), channel_id=1, source_target_pairs={{0,1},{1,2},{2,3},{3,4},{4,5},{5,6},{6,7},{7,8},{8,9},{9,10},{10,1... | collective-permute-start | bytes 190472 | tf_op jit(solution)/shard_map/ppermute | solution.py:17
  56.6 1.9 collective-permute-start.1
  58.6 3.6 %collective-permute-done.1 = f32[31,512]{1,0:T(8,128)S(1)} collective-permute-done((f32[31,512]{1,0:T(8,128)S(1)}, f32[31,512]{1,0:T(8,128)S(1)}, u32[]{:S(2)}, u32[]{:S(2)}) %collective-permute-start.1) | collective-permute-done | bytes 63520 | tf_op jit(solution)/shard_map/ppermute | solution.py:20
  62.2 1.2 pad_maximum_fusion.1.x_ref
  63.4 6.8 %shard_map.135 = f32[512,512]{1,0:T(8,128)} custom-call(f32[574,512]{1,0:T(8,128)} %pad_maximum_fusion.1.x_ref, f32[512,512]{1,0:T(8,128)} %copy-done.3, f32[63,512]{1,0:T(8,128)} %k_ref.3), custom_call_target="tpu_custom_call" | custom-call | tf_op jit(solution)/shard_map/pallas_call | solution.py:38
  70.2 1.4 multiply_reduce_fusion.1
  71.7 1.6 fusion.5
  74.9 31.2 %all_to_all.42 = f32[16,32,512]{2,1,0:T(8,128)S(1)} all-to-all(f32[16,32,512]{2,1,0:T(8,128)S(1)} %bitcast.47), channel_id=1, replica_groups=mesh['neuron'=16,'tm'=16] {'neuron'}, dimensions={0} | all-to-all | bytes 2097152 | tf_op jit(solution)/shard_map/all_to_all | solution.py:98
  106.8 2.0 broadcast_in_dim.10
  108.9 4.3 %all-to-all-start.5 = ((f32[16,32,512]{2,1,0:T(8,128)}), f32[16,32,512]{2,1,0:T(8,128)}, u32[]{:S(2)}, u32[]{:S(2)}) async-start(f32[16,32,512]{2,1,0:T(8,128)} %broadcast_in_dim.10), calls=%async_computation.5 | async-start | bytes 2097152 | tf_op jit(solution)/shard_map/all_to_all | solution.py:105
  113.2 2.3 fusion.7
  115.5 1.1 fusion.4
  116.6 26.4 %all-to-all-done.5 = f32[16,32,512]{2,1,0:T(8,128)} async-done(((f32[16,32,512]{2,1,0:T(8,128)}), f32[16,32,512]{2,1,0:T(8,128)}, u32[]{:S(2)}, u32[]{:S(2)}) %all-to-all-start.5) | async-done | bytes 1048608 | tf_op jit(solution)/shard_map/all_to_all | solution.py:105
  143.0 4.3 %all-to-all-start.2 = ((f32[16,32,512]{2,1,0:T(8,128)}), f32[16,32,512]{2,1,0:T(8,128)}, u32[]{:S(2)}, u32[]{:S(2)}) async-start(f32[16,32,512]{2,1,0:T(8,128)} %bitcast.48), calls=%async_computation.2 | async-start | bytes 2097152 | tf_op jit(solution)/shard_map/all_to_all | solution.py:98
  147.4 1.6 fusion.3
  149.1 1.6 multiply_subtract_fusion.d_ref
  152.3 2.4 collective-permute-start.2
  154.7 2.1 collective-permute-start.3
  156.9 1.0 fusion.6
  157.9 1.7 reshape.106
  159.6 1.7 reshape.107
  161.3 2.4 pad_maximum_fusion.2.g_ref
  163.7 11.4 %shard_map.136 = (bf16[512,512]{1,0:T(8,128)(2,1)}, f32[63,512]{1,0:T(8,128)}) custom-call(f32[574,512]{1,0:T(8,128)} %pad_maximum_fusion.2.g_ref, f32[512,512]{1,0:T(8,128)} %copy-done.2, f32[574,512]{1,0:T(8,128)} %pad_maximum_fusion.1.x_ref, f32[63,512]{1,0:T(8,128)} %k_ref.3), custom_call_target="tpu_custom_call" | custom-call | tf_op jit(solution)/shard_map/pallas_call | solution.py:71
  176.0 2.2 fusion.14
  178.2 1.9 reshape.103
  180.1 6.2 %convolution_bitcast_fusion = f32[4096,256]{0,1:T(8,128)} fusion(bf16[512,4096]{1,0:T(8,128)(2,1)} %param.8, bf16[512,512]{1,0:T(8,128)(2,1)} %get-tuple-element.9, bf16[256,512]{1,0:T(8,128)(2,1)} %param.10), kind=kOutput, calls=%fused_computation | convolution fusion | flops 1208090624 | bytes 9175040 | tf_op jit(solution)/shard_map/dot_general | solution.py:92
  186.3 5.7 %copy.21 = f32[4096,256]{1,0:T(8,128)} copy(f32[4096,256]{0,1:T(8,128)} %convolution_bitcast_fusion) | data formatting | bytes 8388608 | tf_op jit(solution)/shard_map/reshape | solution.py:155
  192.0 6.1 %concatenate.14 = f32[1152,256]{1,0:T(8,128)} concatenate(f32[512,256]{1,0:T(8,128)} %reshape.103, f32[126,256]{1,0:T(8,128)S(1)} %reshape.104, f32[2,256]{1,0:T(2,128)S(1)} %reshape.105, f32[256,256]{1,0:T(8,128)S(1)} %copy-done.8, f32[256,256]{1,0:T(8,128)} %reshape.107), dimensions={0} | concatenate | bytes 2359296 | tf_op jit(solution)/shard_map/concatenate | solution.py:154
  198.2 5.4 %pad_maximum_fusion = f32[16,328,256]{2,1,0:T(8,128)} fusion(f32[16,72,256]{2,1,0:T(8,128)} %bitcast.46, f32[16,256,256]{2,1,0:T(8,128)} %bitcast.41), kind=kLoop, calls=%fused_computation.1 | loop fusion | flops 1343488 | bytes 10747904 | tf_op jit(solution)/shard_map/concatenate | solution.py:157
  203.6 7.8 %all-to-all-start.6 = ((f32[16,328,256]{2,1,0:T(8,128)}), f32[16,328,256]{2,1,0:T(8,128)}, u32[]{:S(2)}, u32[]{:S(2)}) async-start(f32[16,328,256]{2,1,0:T(8,128)} %pad_maximum_fusion), calls=%async_computation.6 | async-start | bytes 10747904 | tf_op jit(solution)/shard_map/all_to_all | solution.py:98
  211.4 1.3 reduce_sum.65
  212.7 60.8 %all-to-all-done.6 = f32[16,328,256]{2,1,0:T(8,128)} async-done(((f32[16,328,256]{2,1,0:T(8,128)}), f32[16,328,256]{2,1,0:T(8,128)}, u32[]{:S(2)}, u32[]{:S(2)}) %all-to-all-start.6) | async-done | bytes 5373984 | tf_op jit(solution)/shard_map/all_to_all | solution.py:98
  274.4 11.1 %all-to-all-start.3 = ((bf16[16,32,512]{2,1,0:T(8,128)(2,1)}), bf16[16,32,512]{2,1,0:T(8,128)(2,1)S(1)}, u32[]{:S(2)}, u32[]{:S(2)}) async-start(bf16[16,32,512]{2,1,0:T(8,128)(2,1)} %broadcast_in_dim.9), calls=%async_computation.3 | async-start | bytes 1048576 | tf_op jit(solution)/shard_map/all_to_all | solution.py:105
  285.5 2.9 reduce_sum.69
  288.4 14.4 %all-to-all-done.3 = bf16[16,32,512]{2,1,0:T(8,128)(2,1)S(1)} async-done(((bf16[16,32,512]{2,1,0:T(8,128)(2,1)}), bf16[16,32,512]{2,1,0:T(8,128)(2,1)S(1)}, u32[]{:S(2)}, u32[]{:S(2)}) %all-to-all-start.3) | async-done | bytes 524320 | tf_op jit(solution)/shard_map/all_to_all | solution.py:105
  302.8 1.2 broadcast_in_dim.11
  304.0 5.7 %all-to-all-start.7 = ((f32[16,72,256]{2,1,0:T(8,128)}), f32[16,72,256]{2,1,0:T(8,128)S(1)}, u32[]{:S(2)}, u32[]{:S(2)}) async-start(f32[16,72,256]{2,1,0:T(8,128)} %broadcast_in_dim.11), calls=%async_computation.7 | async-start | bytes 2359296 | tf_op jit(solution)/shard_map/all_to_all | solution.py:105
  309.7 1.7 slice.48
  311.4 15.5 %all-to-all-done.7 = f32[16,72,256]{2,1,0:T(8,128)S(1)} async-done(((f32[16,72,256]{2,1,0:T(8,128)}), f32[16,72,256]{2,1,0:T(8,128)S(1)}, u32[]{:S(2)}, u32[]{:S(2)}) %all-to-all-start.7) | async-done | bytes 1179680 | tf_op jit(solution)/shard_map/all_to_all | solution.py:105
  329.7 1.6 reshape.111
  331.3 1.7 reshape.114
  333.1 2.0 reshape.110
  335.8 1.9 copy.27
  (55 shorter events, 9.5 us)
Async XLA Ops:
  0.6 1.6 copy-start
  52.4 11.0 %copy-start.3 = (f32[512,512]{1,0:T(8,128)}, f32[512,512]{1,0:T(8,128)S(1)}, u32[]{:S(2)}) copy-start(f32[512,512]{1,0:T(8,128)S(1)} %fusion.12.mid_ref) | copy-start | bytes 3145732
  52.4 6.2 %collective-permute-start = (f32[31,512]{1,0:T(8,128)S(1)}, f32[31,512]{1,0:T(8,128)S(1)}, u32[]{:S(2)}, u32[]{:S(2)}) collective-permute-start(f32[31,512]{1,0:T(8,128)S(1)} %get-tuple-element.24), channel_id=1, source_target_pairs={{0,1},{1,2},{2,3},{3,4},{4,5},{5,6},{6,7},{7,8},{8,9},{9,10},{10,1... | collective-permute-start | bytes 190472 | tf_op jit(solution)/shard_map/ppermute | solution.py:17
  56.6 5.6 %collective-permute-start.1 = (f32[31,512]{1,0:T(8,128)S(1)}, f32[31,512]{1,0:T(8,128)S(1)}, u32[]{:S(2)}, u32[]{:S(2)}) collective-permute-start(f32[31,512]{1,0:T(8,128)S(1)} %get-tuple-element.25), channel_id=1, source_target_pairs={{1,0},{2,1},{3,2},{4,3},{5,4},{6,5},{7,6},{8,7},{9,8},{10,9},{11,1... | collective-permute-start | bytes 190472 | tf_op jit(solution)/shard_map/ppermute | solution.py:20
  63.4 8.3 %copy-start.11 = (bf16[512,128]{1,0:T(8,128)(2,1)S(1)}, bf16[512,128]{1,0:T(8,128)(2,1)}, u32[]{:S(2)}) copy-start(bf16[512,128]{1,0:T(8,128)(2,1)} %param.13) | copy-start | bytes 393220
  63.4 8.3 %copy-start.15 = (f32[512]{0:T(512)S(1)}, f32[512]{0:T(512)}, u32[]{:S(2)}) copy-start(f32[512]{0:T(512)} %param.12) | copy-start | bytes 6148
  70.2 3.8 %copy-start.9 = (bf16[512,512]{1,0:T(8,128)(2,1)S(1)}, bf16[512,512]{1,0:T(8,128)(2,1)}, u32[]{:S(2)}) copy-start(bf16[512,512]{1,0:T(8,128)(2,1)} %param.15) | copy-start | bytes 1572868
  70.2 3.8 %copy-start.14 = (bf16[128,512]{1,0:T(8,128)(2,1)S(1)}, bf16[128,512]{1,0:T(8,128)(2,1)}, u32[]{:S(2)}) copy-start(bf16[128,512]{1,0:T(8,128)(2,1)} %param.14) | copy-start | bytes 393220
  73.3 0.7 copy-start.6
  74.3 0.7 copy-start.12
  106.8 8.6 %copy-start.1 = (f32[512,512]{1,0:T(8,128)S(1)}, f32[512,512]{1,0:T(8,128)}, u32[]{:S(2)}) copy-start(f32[512,512]{1,0:T(8,128)} %shard_map.135) | copy-start | bytes 3145732
  106.8 8.6 %copy-start.13 = (bf16[512,128]{1,0:T(8,128)(2,1)S(1)}, bf16[512,128]{1,0:T(8,128)(2,1)}, u32[]{:S(2)}) copy-start(bf16[512,128]{1,0:T(8,128)(2,1)} %copy-done.12) | copy-start | bytes 393220
  108.9 34.2 %all-to-all-start.5 = ((f32[16,32,512]{2,1,0:T(8,128)}), f32[16,32,512]{2,1,0:T(8,128)}, u32[]{:S(2)}, u32[]{:S(2)}) async-start(f32[16,32,512]{2,1,0:T(8,128)} %broadcast_in_dim.10), calls=%async_computation.5 | async-start | bytes 2097152 | tf_op jit(solution)/shard_map/all_to_all | solution.py:105
  143.0 60.6 %all-to-all-start.2 = ((f32[16,32,512]{2,1,0:T(8,128)}), f32[16,32,512]{2,1,0:T(8,128)}, u32[]{:S(2)}, u32[]{:S(2)}) async-start(f32[16,32,512]{2,1,0:T(8,128)} %bitcast.48), calls=%async_computation.2 | async-start | bytes 2097152 | tf_op jit(solution)/shard_map/all_to_all | solution.py:98
  147.4 1.7 copy-start.10
  149.0 7.8 %copy-start.7 = (f32[512,128]{1,0:T(8,128)S(1)}, f32[512,128]{1,0:T(8,128)}, u32[]{:S(2)}) copy-start(f32[512,128]{1,0:T(8,128)} %copy-done.6) | copy-start | bytes 786436
  150.7 1.0 copy-start.2
  152.3 8.9 %collective-permute-start.2 = (f32[31,512]{1,0:T(8,128)}, f32[31,512]{1,0:T(8,128)S(1)}, u32[]{:S(2)}, u32[]{:S(2)}) collective-permute-start(f32[31,512]{1,0:T(8,128)} %get-tuple-element.22), channel_id=1, source_target_pairs={{0,1},{1,2},{2,3},{3,4},{4,5},{5,6},{6,7},{7,8},{8,9},{9,10},{10,1... | collective-permute-start | bytes 190472 | tf_op jit(solution)/shard_map/ppermute | solution.py:17
  154.7 6.6 %collective-permute-start.3 = (f32[31,512]{1,0:T(8,128)}, f32[31,512]{1,0:T(8,128)S(1)}, u32[]{:S(2)}, u32[]{:S(2)}) collective-permute-start(f32[31,512]{1,0:T(8,128)} %get-tuple-element.23), channel_id=1, source_target_pairs={{1,0},{2,1},{3,2},{4,3},{5,4},{6,5},{7,6},{8,7},{9,8},{10,9},{11,1... | collective-permute-start | bytes 190472 | tf_op jit(solution)/shard_map/ppermute | solution.py:20
  186.3 5.7 %copy-start.8 = (f32[256,256]{1,0:T(8,128)S(1)}, f32[256,256]{1,0:T(8,128)}, u32[]{:S(2)}) copy-start(f32[256,256]{1,0:T(8,128)} %reshape.106) | copy-start | bytes 786436
  203.6 69.9 %all-to-all-start.6 = ((f32[16,328,256]{2,1,0:T(8,128)}), f32[16,328,256]{2,1,0:T(8,128)}, u32[]{:S(2)}, u32[]{:S(2)}) async-start(f32[16,328,256]{2,1,0:T(8,128)} %pad_maximum_fusion), calls=%async_computation.6 | async-start | bytes 10747904 | tf_op jit(solution)/shard_map/all_to_all | solution.py:98
  274.4 28.4 %all-to-all-start.3 = ((bf16[16,32,512]{2,1,0:T(8,128)(2,1)}), bf16[16,32,512]{2,1,0:T(8,128)(2,1)S(1)}, u32[]{:S(2)}, u32[]{:S(2)}) async-start(bf16[16,32,512]{2,1,0:T(8,128)(2,1)} %broadcast_in_dim.9), calls=%async_computation.3 | async-start | bytes 1048576 | tf_op jit(solution)/shard_map/all_to_all | solution.py:105
  288.4 15.6 %copy-start.5 = (f32[328,256]{1,0:T(8,128)}, f32[328,256]{1,0:T(8,128)S(1)}, u32[]{:S(2)}) copy-start(f32[328,256]{1,0:T(8,128)S(1)} %reduce_sum.69) | copy-start | bytes 1007620
  302.8 1.2 copy-start.4
  304.0 22.9 %all-to-all-start.7 = ((f32[16,72,256]{2,1,0:T(8,128)}), f32[16,72,256]{2,1,0:T(8,128)S(1)}, u32[]{:S(2)}, u32[]{:S(2)}) async-start(f32[16,72,256]{2,1,0:T(8,128)} %broadcast_in_dim.11), calls=%async_computation.7 | async-start | bytes 2359296 | tf_op jit(solution)/shard_map/all_to_all | solution.py:105

commit v5 on v4

--- a/solution.py
+++ b/solution.py
@@ -154,7 +154,9 @@
     small = jnp.concatenate([g.reshape(-1, width) for g in grads]).reshape(nt, -1, width)
     readin_part = local_readin.reshape(nt, -1, width)
     cut = readin_part.shape[1]
-    reduced = scatter_sum(jnp.concatenate([readin_part, small], axis=1), "tm")
+    packed = jnp.concatenate([readin_part, small], axis=1)
+    denoised, packed = lax.optimization_barrier((denoised, packed))
+    reduced = scatter_sum(packed, "tm")
     grad_readin = reduced[:cut]
     small_sum = gather_all(reduced[cut:], "tm").reshape(-1, width)
     outs = []

time: 339 us -> 339 us (level)
  blocking collectives: 76.6 us -> 113 us
  waiting for transfers between devices: 121 us -> 95.2 us
  starting transfers between devices: 43.9 us -> 33.1 us
  local copies, waits for them, and re-layouts: 38.9 us -> 35.1 us
    all_to_all x2, blocking collectives: 59.8 us -> 96.7 us  [scatter_sum(): got = lax.all_to_all(parts, axis, 0, 0, tiled=False)]
    all_to_all x3, waiting for transfers between devices: 56.4 us -> 37.4 us  [gather_all(): return lax.all_to_all(spread, axis, 0, 0, tiled=False)]
    all_to_all x3, starting transfers between devices: 21.2 us -> 13.3 us  [gather_all(): return lax.all_to_all(spread, axis, 0, 0, tiled=False)]
    all_to_all x2, waiting for transfers between devices: 60.8 us -> 54.1 us  [scatter_sum(): got = lax.all_to_all(parts, axis, 0, 0, tiled=False)]
    all_to_all x2, starting transfers between devices: 12.1 us -> 8.13 us  [scatter_sum(): got = lax.all_to_all(parts, axis, 0, 0, tiled=False)]
  transfers between devices with their start and end apart: 9 -> 9, of which waited for: 5 -> 5; matrix products, arithmetic and copies ran while one was open for 14% -> 12% of each run, Pallas kernels for 3% -> 3%
where the time goes in v5:
time: 339 us; the launch traced here: 336 us
  blocking collectives  113 us (33%)
  waiting for transfers between devices  95.2 us (28%)
  local copies, waits for them, and re-layouts  35.1 us (10%)
  starting transfers between devices  33.1 us (10%)
  matrix products  20.7 us (6%)
  other arithmetic  19.6 us (6%)
  Pallas kernels  18.2 us (5%)
    all_to_all x2, blocking collectives, scatter_sum(): got = lax.all_to_all(parts, axis, 0, 0, tiled=False)  96.7 us
    all_to_all x2, waiting for transfers between devices, scatter_sum(): got = lax.all_to_all(parts, axis, 0, 0, tiled=False)  54.1 us
    all_to_all x3, waiting for transfers between devices, gather_all(): return lax.all_to_all(spread, axis, 0, 0, tiled=False)  37.4 us
    all_to_all x1, blocking collectives, gather_all(): return lax.all_to_all(spread, axis, 0, 0, tiled=False)  16.8 us
    all_to_all x3, starting transfers between devices, gather_all(): return lax.all_to_all(spread, axis, 0, 0, tiled=False)  13.3 us
    pallas_call x1, Pallas kernels, bwd_conv(): pl.pallas_call(_bwd_conv_kernel, out_shape=(jax.ShapeDtypeStruct((rows, w...  11.4 us
    dot_general x4, matrix products, over_time(): lax.dot_general(left, right, (((0,), (0,)), ((), ())), preferred_element_...  10.7 us
    all_to_all x2, starting transfers between devices, scatter_sum(): got = lax.all_to_all(parts, axis, 0, 0, tiled=False)  8.13 us
  transfers between devices with their start and end apart: 9, of which 5 were waited for; matrix products, arithmetic and copies ran while one was open for 12% of the time, Pallas kernels for 3%

profile of v5, /device:TPU:1, one launch (start us, length us, event | category | flops | bytes accessed | tf_op | source)
XLA Modules:
  0.0 336.4 jit_solution(1857218656939127071)
XLA Ops:
  0.6 1.6 copy-done
  2.2 3.4 %fusion.11 = f32[512,256]{1,0:T(8,128)S(1)} fusion(bf16[512,4096]{1,0:T(8,128)(2,1)} %param.8, bf16[4096,256]{1,0:T(8,128)(2,1)S(1)} %copy-done), kind=kOutput, calls=%fused_computation.30 | convolution fusion | flops 1073741824 | bytes 6815744 | tf_op jit(solution)/shard_map/dot_general | solution.py:120
  5.7 28.6 %all_to_all.40 = f32[16,32,256]{2,1,0:T(8,128)S(1)} all-to-all(f32[16,32,256]{2,1,0:T(8,128)S(1)} %bitcast.50), channel_id=1, replica_groups=mesh['neuron'=16,'tm'=16] {'neuron'}, dimensions={0} | all-to-all | bytes 1048576 | tf_op jit(solution)/shard_map/all_to_all | solution.py:98
  34.3 16.8 %all_to_all.41 = bf16[16,32,256]{2,1,0:T(8,128)(2,1)S(1)} all-to-all(bf16[16,32,256]{2,1,0:T(8,128)(2,1)S(1)} %broadcast_in_dim.8), channel_id=1, replica_groups=mesh['neuron'=16,'tm'=16] {'neuron'}, dimensions={0} | all-to-all | bytes 524288 | tf_op jit(solution)/shard_map/all_to_all | solution.py:105
  51.1 1.2 fusion.12.mid_ref
  52.4 4.2 %collective-permute-start = (f32[31,512]{1,0:T(8,128)S(1)}, f32[31,512]{1,0:T(8,128)S(1)}, u32[]{:S(2)}, u32[]{:S(2)}) collective-permute-start(f32[31,512]{1,0:T(8,128)S(1)} %get-tuple-element.28), channel_id=1, source_target_pairs={{0,1},{1,2},{2,3},{3,4},{4,5},{5,6},{6,7},{7,8},{8,9},{9,10},{10,1... | collective-permute-start | bytes 190472 | tf_op jit(solution)/shard_map/ppermute | solution.py:17
  56.6 1.9 collective-permute-start.1
  58.6 3.6 %collective-permute-done.1 = f32[31,512]{1,0:T(8,128)S(1)} collective-permute-done((f32[31,512]{1,0:T(8,128)S(1)}, f32[31,512]{1,0:T(8,128)S(1)}, u32[]{:S(2)}, u32[]{:S(2)}) %collective-permute-start.1) | collective-permute-done | bytes 63520 | tf_op jit(solution)/shard_map/ppermute | solution.py:20
  62.2 1.2 pad_maximum_fusion.1.x_ref
  63.4 6.8 %shard_map.135 = f32[512,512]{1,0:T(8,128)} custom-call(f32[574,512]{1,0:T(8,128)} %pad_maximum_fusion.1.x_ref, f32[512,512]{1,0:T(8,128)} %copy-done.3, f32[63,512]{1,0:T(8,128)} %k_ref.3), custom_call_target="tpu_custom_call" | custom-call | tf_op jit(solution)/shard_map/pallas_call | solution.py:38
  70.2 1.4 multiply_reduce_fusion.1
  71.7 1.6 fusion.5
  74.3 1.3 fusion.13
  75.6 3.8 %all-to-all-start.4 = ((f32[16,32,512]{2,1,0:T(8,128)}), f32[16,32,512]{2,1,0:T(8,128)S(1)}, u32[]{:S(2)}, u32[]{:S(2)}) async-start(f32[16,32,512]{2,1,0:T(8,128)} %bitcast.4), calls=%async_computation.4 | async-start | bytes 2097152 | tf_op jit(solution)/shard_map/all_to_all | solution.py:98
  79.4 2.2 fusion.7
  81.6 26.3 %all-to-all-done.4 = f32[16,32,512]{2,1,0:T(8,128)S(1)} async-done(((f32[16,32,512]{2,1,0:T(8,128)}), f32[16,32,512]{2,1,0:T(8,128)S(1)}, u32[]{:S(2)}, u32[]{:S(2)}) %all-to-all-start.4) | async-done | bytes 1048608 | tf_op jit(solution)/shard_map/all_to_all | solution.py:98
  109.0 4.3 %all-to-all-start.2 = ((f32[16,32,512]{2,1,0:T(8,128)}), f32[16,32,512]{2,1,0:T(8,128)}, u32[]{:S(2)}, u32[]{:S(2)}) async-start(f32[16,32,512]{2,1,0:T(8,128)} %bitcast.47), calls=%async_computation.2 | async-start | bytes 2097152 | tf_op jit(solution)/shard_map/all_to_all | solution.py:98
  113.4 2.0 reduce_sum.66
  115.4 27.8 %all-to-all-done.2 = f32[16,32,512]{2,1,0:T(8,128)} async-done(((f32[16,32,512]{2,1,0:T(8,128)}), f32[16,32,512]{2,1,0:T(8,128)}, u32[]{:S(2)}, u32[]{:S(2)}) %all-to-all-start.2) | async-done | bytes 1048608 | tf_op jit(solution)/shard_map/all_to_all | solution.py:98
  143.2 2.0 broadcast_in_dim.10
  145.1 4.4 %all-to-all-start.5 = ((f32[16,32,512]{2,1,0:T(8,128)}), f32[16,32,512]{2,1,0:T(8,128)}, u32[]{:S(2)}, u32[]{:S(2)}) async-start(f32[16,32,512]{2,1,0:T(8,128)} %broadcast_in_dim.10), calls=%async_computation.5 | async-start | bytes 2097152 | tf_op jit(solution)/shard_map/all_to_all | solution.py:105
  150.7 1.7 reshape.106
  152.4 2.1 fusion.6
  154.5 1.7 reshape.107
  156.2 1.3 reduce_sum.65
  157.5 21.9 %all-to-all-done.5 = f32[16,32,512]{2,1,0:T(8,128)} async-done(((f32[16,32,512]{2,1,0:T(8,128)}), f32[16,32,512]{2,1,0:T(8,128)}, u32[]{:S(2)}, u32[]{:S(2)}) %all-to-all-start.5) | async-done | bytes 1048608 | tf_op jit(solution)/shard_map/all_to_all | solution.py:105
  179.3 1.6 fusion.3
  181.0 1.6 multiply_subtract_fusion.d_ref
  183.3 3.6 %collective-permute-start.2 = (f32[31,512]{1,0:T(8,128)}, f32[31,512]{1,0:T(8,128)S(1)}, u32[]{:S(2)}, u32[]{:S(2)}) collective-permute-start(f32[31,512]{1,0:T(8,128)} %get-tuple-element.26), channel_id=1, source_target_pairs={{0,1},{1,2},{2,3},{3,4},{4,5},{5,6},{6,7},{7,8},{8,9},{9,10},{10,1... | collective-permute-start | bytes 190472 | tf_op jit(solution)/shard_map/ppermute | solution.py:17
  186.9 1.9 collective-permute-start.3
  189.7 4.8 %all-to-all-start.3 = ((bf16[16,32,512]{2,1,0:T(8,128)(2,1)}), bf16[16,32,512]{2,1,0:T(8,128)(2,1)}, u32[]{:S(2)}, u32[]{:S(2)}) async-start(bf16[16,32,512]{2,1,0:T(8,128)(2,1)} %broadcast_in_dim.9), calls=%async_computation.3 | async-start | bytes 1048576 | tf_op jit(solution)/shard_map/all_to_all | solution.py:105
  194.6 2.4 pad_maximum_fusion.2.g_ref
  197.0 11.4 %shard_map.136 = (bf16[512,512]{1,0:T(8,128)(2,1)}, f32[63,512]{1,0:T(8,128)}) custom-call(f32[574,512]{1,0:T(8,128)} %pad_maximum_fusion.2.g_ref, f32[512,512]{1,0:T(8,128)} %copy-done.2, f32[574,512]{1,0:T(8,128)} %pad_maximum_fusion.1.x_ref, f32[63,512]{1,0:T(8,128)} %k_ref.3), custom_call_target="tpu_custom_call" | custom-call | tf_op jit(solution)/shard_map/pallas_call | solution.py:71
  208.5 1.6 reshape.104
  210.1 1.4 fusion.14
  212.3 6.1 %convolution_bitcast_fusion = f32[4096,256]{0,1:T(8,128)} fusion(bf16[512,4096]{1,0:T(8,128)(2,1)} %param.8, bf16[512,512]{1,0:T(8,128)(2,1)S(1)} %copy-done.5, bf16[256,512]{1,0:T(8,128)(2,1)} %param.10), kind=kOutput, calls=%fused_computation | convolution fusion | flops 1208090624 | bytes 9175040 | tf_op jit(solution)/shard_map/dot_general | solution.py:92
  218.4 5.7 %copy.21 = f32[4096,256]{1,0:T(8,128)} copy(f32[4096,256]{0,1:T(8,128)} %convolution_bitcast_fusion) | data formatting | bytes 8388608 | tf_op jit(solution)/shard_map/reshape | solution.py:155
  224.1 3.0 concatenate.14
  227.1 5.1 %pad_maximum_fusion = f32[16,328,256]{2,1,0:T(8,128)} fusion(f32[16,72,256]{2,1,0:T(8,128)S(1)} %bitcast.46, f32[16,256,256]{2,1,0:T(8,128)} %bitcast.41), kind=kLoop, calls=%fused_computation.1 | loop fusion | flops 1343488 | bytes 10747904 | tf_op jit(solution)/shard_map/concatenate | solution.py:157
  232.2 68.1 %all_to_all.42 = f32[16,328,256]{2,1,0:T(8,128)} all-to-all(f32[16,328,256]{2,1,0:T(8,128)} %pad_maximum_fusion), channel_id=1, replica_groups=mesh['neuron'=16,'tm'=16] {'tm'}, dimensions={0} | all-to-all | bytes 10747904 | tf_op jit(solution)/shard_map/all_to_all | solution.py:98
  300.3 2.9 reduce_sum.69
  304.3 4.1 %all-to-all-start.7 = ((f32[16,72,256]{2,1,0:T(8,128)}), f32[16,72,256]{2,1,0:T(8,128)S(1)}, u32[]{:S(2)}, u32[]{:S(2)}) async-start(f32[16,72,256]{2,1,0:T(8,128)} %broadcast_in_dim.11), calls=%async_computation.7 | async-start | bytes 2359296 | tf_op jit(solution)/shard_map/all_to_all | solution.py:105
  308.5 1.7 slice.48
  310.2 15.5 %all-to-all-done.7 = f32[16,72,256]{2,1,0:T(8,128)S(1)} async-done(((f32[16,72,256]{2,1,0:T(8,128)}), f32[16,72,256]{2,1,0:T(8,128)S(1)}, u32[]{:S(2)}, u32[]{:S(2)}) %all-to-all-start.7) | async-done | bytes 1179680 | tf_op jit(solution)/shard_map/all_to_all | solution.py:105
  328.5 1.6 reshape.111
  330.1 1.7 reshape.114
  331.8 2.0 reshape.110
  334.5 1.9 copy.27
  (57 shorter events, 10.4 us)
Async XLA Ops:
  0.6 1.6 copy-start
  52.4 11.0 %copy-start.3 = (f32[512,512]{1,0:T(8,128)}, f32[512,512]{1,0:T(8,128)S(1)}, u32[]{:S(2)}) copy-start(f32[512,512]{1,0:T(8,128)S(1)} %fusion.12.mid_ref) | copy-start | bytes 3145732
  52.4 6.2 %collective-permute-start = (f32[31,512]{1,0:T(8,128)S(1)}, f32[31,512]{1,0:T(8,128)S(1)}, u32[]{:S(2)}, u32[]{:S(2)}) collective-permute-start(f32[31,512]{1,0:T(8,128)S(1)} %get-tuple-element.28), channel_id=1, source_target_pairs={{0,1},{1,2},{2,3},{3,4},{4,5},{5,6},{6,7},{7,8},{8,9},{9,10},{10,1... | collective-permute-start | bytes 190472 | tf_op jit(solution)/shard_map/ppermute | solution.py:17
  56.6 5.6 %collective-permute-start.1 = (f32[31,512]{1,0:T(8,128)S(1)}, f32[31,512]{1,0:T(8,128)S(1)}, u32[]{:S(2)}, u32[]{:S(2)}) collective-permute-start(f32[31,512]{1,0:T(8,128)S(1)} %get-tuple-element.29), channel_id=1, source_target_pairs={{1,0},{2,1},{3,2},{4,3},{5,4},{6,5},{7,6},{8,7},{9,8},{10,9},{11,1... | collective-permute-start | bytes 190472 | tf_op jit(solution)/shard_map/ppermute | solution.py:20
  63.4 8.3 %copy-start.11 = (bf16[512,128]{1,0:T(8,128)(2,1)S(1)}, bf16[512,128]{1,0:T(8,128)(2,1)}, u32[]{:S(2)}) copy-start(bf16[512,128]{1,0:T(8,128)(2,1)} %param.13) | copy-start | bytes 393220
  63.4 8.3 %copy-start.16 = (f32[512]{0:T(512)S(1)}, f32[512]{0:T(512)}, u32[]{:S(2)}) copy-start(f32[512]{0:T(512)} %param.12) | copy-start | bytes 6148
  70.2 3.8 %copy-start.9 = (bf16[512,512]{1,0:T(8,128)(2,1)S(1)}, bf16[512,512]{1,0:T(8,128)(2,1)}, u32[]{:S(2)}) copy-start(bf16[512,512]{1,0:T(8,128)(2,1)} %param.15) | copy-start | bytes 1572868
  70.2 3.8 %copy-start.14 = (bf16[128,512]{1,0:T(8,128)(2,1)S(1)}, bf16[128,512]{1,0:T(8,128)(2,1)}, u32[]{:S(2)}) copy-start(bf16[128,512]{1,0:T(8,128)(2,1)} %param.14) | copy-start | bytes 393220
  73.3 0.7 copy-start.7
  74.3 1.3 copy-start.12
  75.6 3.8 %copy-start.15 = (bf16[128,512]{1,0:T(8,128)(2,1)S(1)}, bf16[128,512]{1,0:T(8,128)(2,1)}, u32[]{:S(2)}) copy-start(bf16[128,512]{1,0:T(8,128)(2,1)} %param.14) | copy-start | bytes 393220
  75.6 32.4 %all-to-all-start.4 = ((f32[16,32,512]{2,1,0:T(8,128)}), f32[16,32,512]{2,1,0:T(8,128)S(1)}, u32[]{:S(2)}, u32[]{:S(2)}) async-start(f32[16,32,512]{2,1,0:T(8,128)} %bitcast.4), calls=%async_computation.4 | async-start | bytes 2097152 | tf_op jit(solution)/shard_map/all_to_all | solution.py:98
  108.0 1.0 copy-start.4
  109.0 34.2 %all-to-all-start.2 = ((f32[16,32,512]{2,1,0:T(8,128)}), f32[16,32,512]{2,1,0:T(8,128)}, u32[]{:S(2)}, u32[]{:S(2)}) async-start(f32[16,32,512]{2,1,0:T(8,128)} %bitcast.47), calls=%async_computation.2 | async-start | bytes 2097152 | tf_op jit(solution)/shard_map/all_to_all | solution.py:98
  113.3 36.2 %copy-start.1 = (f32[512,512]{1,0:T(8,128)S(1)}, f32[512,512]{1,0:T(8,128)}, u32[]{:S(2)}) copy-start(f32[512,512]{1,0:T(8,128)} %shard_map.135) | copy-start | bytes 3145732
  113.3 36.2 %copy-start.13 = (bf16[512,128]{1,0:T(8,128)(2,1)S(1)}, bf16[512,128]{1,0:T(8,128)(2,1)}, u32[]{:S(2)}) copy-start(bf16[512,128]{1,0:T(8,128)(2,1)} %copy-done.12) | copy-start | bytes 393220
  145.1 34.2 %all-to-all-start.5 = ((f32[16,32,512]{2,1,0:T(8,128)}), f32[16,32,512]{2,1,0:T(8,128)}, u32[]{:S(2)}, u32[]{:S(2)}) async-start(f32[16,32,512]{2,1,0:T(8,128)} %broadcast_in_dim.10), calls=%async_computation.5 | async-start | bytes 2097152 | tf_op jit(solution)/shard_map/all_to_all | solution.py:105
  179.3 1.6 copy-start.10
  182.6 6.3 %copy-start.2 = (f32[512,512]{1,0:T(8,128)}, f32[512,512]{1,0:T(8,128)S(1)}, u32[]{:S(2)}) copy-start(f32[512,512]{1,0:T(8,128)S(1)} %multiply_subtract_fusion.d_ref) | copy-start | bytes 3145732
  183.3 11.3 %collective-permute-start.2 = (f32[31,512]{1,0:T(8,128)}, f32[31,512]{1,0:T(8,128)S(1)}, u32[]{:S(2)}, u32[]{:S(2)}) collective-permute-start(f32[31,512]{1,0:T(8,128)} %get-tuple-element.26), channel_id=1, source_target_pairs={{0,1},{1,2},{2,3},{3,4},{4,5},{5,6},{6,7},{7,8},{8,9},{9,10},{10,1... | collective-permute-start | bytes 190472 | tf_op jit(solution)/shard_map/ppermute | solution.py:17
  186.9 7.7 %collective-permute-start.3 = (f32[31,512]{1,0:T(8,128)}, f32[31,512]{1,0:T(8,128)}, u32[]{:S(2)}, u32[]{:S(2)}) collective-permute-start(f32[31,512]{1,0:T(8,128)} %get-tuple-element.27), channel_id=1, source_target_pairs={{1,0},{2,1},{3,2},{4,3},{5,4},{6,5},{7,6},{8,7},{9,8},{10,9},{11,1... | collective-permute-start | bytes 190472 | tf_op jit(solution)/shard_map/ppermute | solution.py:20
  189.7 42.5 %all-to-all-start.3 = ((bf16[16,32,512]{2,1,0:T(8,128)(2,1)}), bf16[16,32,512]{2,1,0:T(8,128)(2,1)}, u32[]{:S(2)}, u32[]{:S(2)}) async-start(bf16[16,32,512]{2,1,0:T(8,128)(2,1)} %broadcast_in_dim.9), calls=%async_computation.3 | async-start | bytes 1048576 | tf_op jit(solution)/shard_map/all_to_all | solution.py:105
  208.5 3.9 %copy-start.5 = (bf16[512,512]{1,0:T(8,128)(2,1)S(1)}, bf16[512,512]{1,0:T(8,128)(2,1)}, u32[]{:S(2)}) copy-start(bf16[512,512]{1,0:T(8,128)(2,1)} %get-tuple-element.11) | copy-start | bytes 1572868
  218.4 5.7 %copy-start.8 = (f32[256,256]{1,0:T(8,128)S(1)}, f32[256,256]{1,0:T(8,128)}, u32[]{:S(2)}) copy-start(f32[256,256]{1,0:T(8,128)} %reshape.106) | copy-start | bytes 786436
  303.2 1.1 copy-start.6
  304.3 21.4 %all-to-all-start.7 = ((f32[16,72,256]{2,1,0:T(8,128)}), f32[16,72,256]{2,1,0:T(8,128)S(1)}, u32[]{:S(2)}, u32[]{:S(2)}) async-start(f32[16,72,256]{2,1,0:T(8,128)} %broadcast_in_dim.11), calls=%async_computation.7 | async-start | bytes 2359296 | tf_op jit(solution)/shard_map/all_to_all | solution.py:105

commit v6 on v5

--- a/solution.py
+++ b/solution.py
@@ -136,6 +136,7 @@
     partial_normed = jnp.dot(dpre, w_one.T, preferred_element_type=jnp.float32)
     dnormed_rows = scatter_sum(split_rows(partial_normed, nn), "neuron")
     dnormed = gather_all(dnormed_rows, "neuron").reshape(rows, -1)
+    partial_mix, dnormed = lax.optimization_barrier((partial_mix, dnormed))
     mix_rows = scatter_sum(split_rows(partial_mix, nn), "neuron")
     mixed_rows = lax.dynamic_slice_in_dim(mixed, me * share, share, 0)
     denoised_rows = (mixed_rows + mix_rows).astype(jnp.bfloat16)

time: 339 us -> 325 us (0.959)
  waiting for transfers between devices: 95.2 us -> 59.4 us
  blocking collectives: 113 us -> 146 us
  starting transfers between devices: 33.1 us -> 27.8 us
    all_to_all x2 -> x1, waiting for transfers between devices: 54.1 us -> 12.8 us  [scatter_sum(): got = lax.all_to_all(parts, axis, 0, 0, tiled=False)]
    all_to_all x2 -> x3, blocking collectives: 96.7 us -> 129 us  [scatter_sum(): got = lax.all_to_all(parts, axis, 0, 0, tiled=False)]
    all_to_all x3, waiting for transfers between devices: 37.4 us -> 43 us  [gather_all(): return lax.all_to_all(spread, axis, 0, 0, tiled=False)]
    all_to_all x2 -> x1, starting transfers between devices: 8.13 us -> 4.35 us  [scatter_sum(): got = lax.all_to_all(parts, axis, 0, 0, tiled=False)]
  transfers between devices with their start and end apart: 9 -> 8, of which waited for: 5 -> 4; matrix products, arithmetic and copies ran while one was open for 12% -> 13% of each run, Pallas kernels for 3% -> 4%
where the time goes in v6:
time: 325 us; the launch traced here: 324 us
  blocking collectives  146 us (45%)
  waiting for transfers between devices  59.4 us (18%)
  local copies, waits for them, and re-layouts  34.5 us (11%)
  starting transfers between devices  27.8 us (9%)
  matrix products  19.9 us (6%)
  Pallas kernels  18.2 us (6%)
  other arithmetic  17.3 us (5%)
    all_to_all x3, blocking collectives, scatter_sum(): got = lax.all_to_all(parts, axis, 0, 0, tiled=False)  129 us
    all_to_all x3, waiting for transfers between devices, gather_all(): return lax.all_to_all(spread, axis, 0, 0, tiled=False)  43 us
    all_to_all x1, blocking collectives, gather_all(): return lax.all_to_all(spread, axis, 0, 0, tiled=False)  16.8 us
    all_to_all x3, starting transfers between devices, gather_all(): return lax.all_to_all(spread, axis, 0, 0, tiled=False)  13 us
    all_to_all x1, waiting for transfers between devices, scatter_sum(): got = lax.all_to_all(parts, axis, 0, 0, tiled=False)  12.8 us
    pallas_call x1, Pallas kernels, bwd_conv(): pl.pallas_call(_bwd_conv_kernel, out_shape=(jax.ShapeDtypeStruct((rows, w...  11.4 us
    dot_general x4, matrix products, over_time(): lax.dot_general(left, right, (((0,), (0,)), ((), ())), preferred_element_...  10.7 us
    pallas_call x1, Pallas kernels, fwd_conv(): pl.pallas_call(_fwd_conv_kernel, out_shape=jax.ShapeDtypeStruct((rows, wi...  6.82 us
  transfers between devices with their start and end apart: 8, of which 4 were waited for; matrix products, arithmetic and copies ran while one was open for 13% of the time, Pallas kernels for 4%

profile of v6, /device:TPU:1, one launch (start us, length us, event | category | flops | bytes accessed | tf_op | source)
XLA Modules:
  0.0 323.8 jit_solution(3046805250651845510)
XLA Ops:
  0.6 1.6 copy-done
  2.2 3.4 %fusion.9 = f32[512,256]{1,0:T(8,128)S(1)} fusion(bf16[512,4096]{1,0:T(8,128)(2,1)} %param.8, bf16[4096,256]{1,0:T(8,128)(2,1)S(1)} %copy-done), kind=kOutput, calls=%fused_computation.27 | convolution fusion | flops 1073741824 | bytes 6815744 | tf_op jit(solution)/shard_map/dot_general | solution.py:120
  5.7 28.6 %all_to_all.40 = f32[16,32,256]{2,1,0:T(8,128)S(1)} all-to-all(f32[16,32,256]{2,1,0:T(8,128)S(1)} %bitcast.41), channel_id=1, replica_groups=mesh['neuron'=16,'tm'=16] {'neuron'}, dimensions={0} | all-to-all | bytes 1048576 | tf_op jit(solution)/shard_map/all_to_all | solution.py:98
  34.3 16.8 %all_to_all.41 = bf16[16,32,256]{2,1,0:T(8,128)(2,1)S(1)} all-to-all(bf16[16,32,256]{2,1,0:T(8,128)(2,1)S(1)} %broadcast_in_dim.8), channel_id=1, replica_groups=mesh['neuron'=16,'tm'=16] {'neuron'}, dimensions={0} | all-to-all | bytes 524288 | tf_op jit(solution)/shard_map/all_to_all | solution.py:105
  51.1 1.2 fusion.10.mid_ref
  52.4 4.2 %collective-permute-start = (f32[31,512]{1,0:T(8,128)S(1)}, f32[31,512]{1,0:T(8,128)S(1)}, u32[]{:S(2)}, u32[]{:S(2)}) collective-permute-start(f32[31,512]{1,0:T(8,128)S(1)} %get-tuple-element.32), channel_id=1, source_target_pairs={{0,1},{1,2},{2,3},{3,4},{4,5},{5,6},{6,7},{7,8},{8,9},{9,10},{10,1... | collective-permute-start | bytes 190472 | tf_op jit(solution)/shard_map/ppermute | solution.py:17
  56.6 1.9 collective-permute-start.1
  58.6 3.6 %collective-permute-done.1 = f32[31,512]{1,0:T(8,128)S(1)} collective-permute-done((f32[31,512]{1,0:T(8,128)S(1)}, f32[31,512]{1,0:T(8,128)S(1)}, u32[]{:S(2)}, u32[]{:S(2)}) %collective-permute-start.1) | collective-permute-done | bytes 63520 | tf_op jit(solution)/shard_map/ppermute | solution.py:20
  62.2 1.2 pad_maximum_fusion.1.x_ref
  63.4 6.8 %shard_map.135 = f32[512,512]{1,0:T(8,128)} custom-call(f32[574,512]{1,0:T(8,128)} %pad_maximum_fusion.1.x_ref, f32[512,512]{1,0:T(8,128)} %copy-done.4, f32[63,512]{1,0:T(8,128)} %k_ref.3), custom_call_target="tpu_custom_call" | custom-call | tf_op jit(solution)/shard_map/pallas_call | solution.py:38
  70.2 1.4 multiply_reduce_fusion.2
  71.7 1.6 fusion.3
  75.0 31.2 %all_to_all.42 = f32[16,32,512]{2,1,0:T(8,128)S(1)} all-to-all(f32[16,32,512]{2,1,0:T(8,128)S(1)} %bitcast.37), channel_id=1, replica_groups=mesh['neuron'=16,'tm'=16] {'neuron'}, dimensions={0} | all-to-all | bytes 2097152 | tf_op jit(solution)/shard_map/all_to_all | solution.py:98
  106.2 1.1 broadcast_in_dim.9
  107.4 4.3 %all-to-all-start.3 = ((f32[16,32,512]{2,1,0:T(8,128)}), f32[16,32,512]{2,1,0:T(8,128)}, u32[]{:S(2)}, u32[]{:S(2)}) async-start(f32[16,32,512]{2,1,0:T(8,128)} %broadcast_in_dim.9), calls=%async_computation.3 | async-start | bytes 2097152 | tf_op jit(solution)/shard_map/all_to_all | solution.py:105
  111.8 2.3 fusion.5
  114.1 27.5 %all-to-all-done.3 = f32[16,32,512]{2,1,0:T(8,128)} async-done(((f32[16,32,512]{2,1,0:T(8,128)}), f32[16,32,512]{2,1,0:T(8,128)}, u32[]{:S(2)}, u32[]{:S(2)}) %all-to-all-start.3) | async-done | bytes 1048608 | tf_op jit(solution)/shard_map/all_to_all | solution.py:105
  141.6 4.4 %all-to-all-start.4 = ((f32[16,32,512]{2,1,0:T(8,128)}), f32[16,32,512]{2,1,0:T(8,128)}, u32[]{:S(2)}, u32[]{:S(2)}) async-start(f32[16,32,512]{2,1,0:T(8,128)} %bitcast.38), calls=%async_computation.4 | async-start | bytes 2097152 | tf_op jit(solution)/shard_map/all_to_all | solution.py:98
  146.0 1.1 fusion.2
  147.1 1.7 reshape.106
  148.8 2.1 fusion.4
  150.9 1.7 reshape.107
  152.6 1.6 multiply_reduce_fusion
  154.2 1.7 multiply_subtract_fusion.d_ref
  156.0 1.0 copy-done.2
  157.6 2.4 collective-permute-start.2
  160.0 2.0 collective-permute-start.3
  161.9 12.8 %all-to-all-done.4 = f32[16,32,512]{2,1,0:T(8,128)} async-done(((f32[16,32,512]{2,1,0:T(8,128)}), f32[16,32,512]{2,1,0:T(8,128)}, u32[]{:S(2)}, u32[]{:S(2)}) %all-to-all-start.4) | async-done | bytes 1048608 | tf_op jit(solution)/shard_map/all_to_all | solution.py:98
  174.7 1.3 reduce_sum.66
  176.9 4.5 %all-to-all-start.5 = ((bf16[16,32,512]{2,1,0:T(8,128)(2,1)}), bf16[16,32,512]{2,1,0:T(8,128)(2,1)}, u32[]{:S(2)}, u32[]{:S(2)}) async-start(bf16[16,32,512]{2,1,0:T(8,128)(2,1)} %broadcast_in_dim.10), calls=%async_computation.5 | async-start | bytes 1048576 | tf_op jit(solution)/shard_map/all_to_all | solution.py:105
  181.4 2.0 pad_maximum_fusion.2.g_ref
  183.4 11.4 %shard_map.136 = (bf16[512,512]{1,0:T(8,128)(2,1)}, f32[63,512]{1,0:T(8,128)}) custom-call(f32[574,512]{1,0:T(8,128)} %pad_maximum_fusion.2.g_ref, f32[512,512]{1,0:T(8,128)} %copy-done.2, f32[574,512]{1,0:T(8,128)} %pad_maximum_fusion.1.x_ref, f32[63,512]{1,0:T(8,128)} %k_ref.3), custom_call_target="tpu_custom_call" | custom-call | tf_op jit(solution)/shard_map/pallas_call | solution.py:71
  194.8 1.6 reshape.104
  196.5 1.4 fusion.12
  198.7 6.0 %convolution_bitcast_fusion = f32[4096,256]{0,1:T(8,128)} fusion(bf16[512,4096]{1,0:T(8,128)(2,1)} %param.8, bf16[512,512]{1,0:T(8,128)(2,1)S(1)} %copy-done.5, bf16[256,512]{1,0:T(8,128)(2,1)} %param.10), kind=kOutput, calls=%fused_computation | convolution fusion | flops 1208090624 | bytes 9175040 | tf_op jit(solution)/shard_map/dot_general | solution.py:92
  204.7 5.7 %copy.21 = f32[4096,256]{1,0:T(8,128)} copy(f32[4096,256]{0,1:T(8,128)} %convolution_bitcast_fusion) | data formatting | bytes 8388608 | tf_op jit(solution)/shard_map/reshape | solution.py:156
  210.5 3.0 concatenate.14
  213.4 5.1 %pad_maximum_fusion = f32[16,328,256]{2,1,0:T(8,128)} fusion(f32[16,72,256]{2,1,0:T(8,128)S(1)} %bitcast.36, f32[16,256,256]{2,1,0:T(8,128)} %bitcast.31), kind=kLoop, calls=%fused_computation.1 | loop fusion | flops 1343488 | bytes 10747904 | tf_op jit(solution)/shard_map/concatenate | solution.py:158
  218.5 69.2 %all_to_all.43 = f32[16,328,256]{2,1,0:T(8,128)} all-to-all(f32[16,328,256]{2,1,0:T(8,128)} %pad_maximum_fusion), channel_id=1, replica_groups=mesh['neuron'=16,'tm'=16] {'tm'}, dimensions={0} | all-to-all | bytes 10747904 | tf_op jit(solution)/shard_map/all_to_all | solution.py:98
  287.7 2.9 reduce_sum.69
  290.6 1.1 broadcast_in_dim.11
  291.8 4.1 %all-to-all-start.7 = ((f32[16,72,256]{2,1,0:T(8,128)}), f32[16,72,256]{2,1,0:T(8,128)S(1)}, u32[]{:S(2)}, u32[]{:S(2)}) async-start(f32[16,72,256]{2,1,0:T(8,128)} %broadcast_in_dim.11), calls=%async_computation.7 | async-start | bytes 2359296 | tf_op jit(solution)/shard_map/all_to_all | solution.py:105
  295.9 1.7 slice.48
  297.6 15.5 %all-to-all-done.7 = f32[16,72,256]{2,1,0:T(8,128)S(1)} async-done(((f32[16,72,256]{2,1,0:T(8,128)}), f32[16,72,256]{2,1,0:T(8,128)S(1)}, u32[]{:S(2)}, u32[]{:S(2)}) %all-to-all-start.7) | async-done | bytes 1179680 | tf_op jit(solution)/shard_map/all_to_all | solution.py:105
  315.9 1.6 reshape.111
  317.5 1.7 reshape.114
  319.2 2.0 reshape.110
  321.9 1.9 copy.27
  (52 shorter events, 7.8 us)
Async XLA Ops:
  0.6 1.6 copy-start
  52.4 11.0 %copy-start.4 = (f32[512,512]{1,0:T(8,128)}, f32[512,512]{1,0:T(8,128)S(1)}, u32[]{:S(2)}) copy-start(f32[512,512]{1,0:T(8,128)S(1)} %fusion.10.mid_ref) | copy-start | bytes 3145732
  52.4 6.2 %collective-permute-start = (f32[31,512]{1,0:T(8,128)S(1)}, f32[31,512]{1,0:T(8,128)S(1)}, u32[]{:S(2)}, u32[]{:S(2)}) collective-permute-start(f32[31,512]{1,0:T(8,128)S(1)} %get-tuple-element.32), channel_id=1, source_target_pairs={{0,1},{1,2},{2,3},{3,4},{4,5},{5,6},{6,7},{7,8},{8,9},{9,10},{10,1... | collective-permute-start | bytes 190472 | tf_op jit(solution)/shard_map/ppermute | solution.py:17
  56.6 5.6 %collective-permute-start.1 = (f32[31,512]{1,0:T(8,128)S(1)}, f32[31,512]{1,0:T(8,128)S(1)}, u32[]{:S(2)}, u32[]{:S(2)}) collective-permute-start(f32[31,512]{1,0:T(8,128)S(1)} %get-tuple-element.33), channel_id=1, source_target_pairs={{1,0},{2,1},{3,2},{4,3},{5,4},{6,5},{7,6},{8,7},{9,8},{10,9},{11,1... | collective-permute-start | bytes 190472 | tf_op jit(solution)/shard_map/ppermute | solution.py:20
  63.4 8.3 %copy-start.10 = (bf16[512,128]{1,0:T(8,128)(2,1)S(1)}, bf16[512,128]{1,0:T(8,128)(2,1)}, u32[]{:S(2)}) copy-start(bf16[512,128]{1,0:T(8,128)(2,1)} %param.13) | copy-start | bytes 393220
  63.4 8.3 %copy-start.14 = (f32[512]{0:T(512)S(1)}, f32[512]{0:T(512)}, u32[]{:S(2)}) copy-start(f32[512]{0:T(512)} %param.12) | copy-start | bytes 6148
  70.2 3.8 %copy-start.9 = (bf16[512,512]{1,0:T(8,128)(2,1)S(1)}, bf16[512,512]{1,0:T(8,128)(2,1)}, u32[]{:S(2)}) copy-start(bf16[512,512]{1,0:T(8,128)(2,1)} %param.15) | copy-start | bytes 1572868
  70.2 3.8 %copy-start.13 = (bf16[128,512]{1,0:T(8,128)(2,1)S(1)}, bf16[128,512]{1,0:T(8,128)(2,1)}, u32[]{:S(2)}) copy-start(bf16[128,512]{1,0:T(8,128)(2,1)} %param.14) | copy-start | bytes 393220
  73.3 0.7 copy-start.7
  74.3 0.7 copy-start.11
  107.4 34.2 %all-to-all-start.3 = ((f32[16,32,512]{2,1,0:T(8,128)}), f32[16,32,512]{2,1,0:T(8,128)}, u32[]{:S(2)}, u32[]{:S(2)}) async-start(f32[16,32,512]{2,1,0:T(8,128)} %broadcast_in_dim.9), calls=%async_computation.3 | async-start | bytes 2097152 | tf_op jit(solution)/shard_map/all_to_all | solution.py:105
  111.7 34.2 %copy-start.1 = (f32[512,512]{1,0:T(8,128)S(1)}, f32[512,512]{1,0:T(8,128)}, u32[]{:S(2)}) copy-start(f32[512,512]{1,0:T(8,128)} %shard_map.135) | copy-start | bytes 3145732
  111.7 34.2 %copy-start.12 = (bf16[512,128]{1,0:T(8,128)(2,1)S(1)}, bf16[512,128]{1,0:T(8,128)(2,1)}, u32[]{:S(2)}) copy-start(bf16[512,128]{1,0:T(8,128)(2,1)} %copy-done.11) | copy-start | bytes 393220
  141.6 33.2 %all-to-all-start.4 = ((f32[16,32,512]{2,1,0:T(8,128)}), f32[16,32,512]{2,1,0:T(8,128)}, u32[]{:S(2)}, u32[]{:S(2)}) async-start(f32[16,32,512]{2,1,0:T(8,128)} %bitcast.38), calls=%async_computation.4 | async-start | bytes 2097152 | tf_op jit(solution)/shard_map/all_to_all | solution.py:98
  156.0 1.0 copy-start.2
  157.6 23.8 %collective-permute-start.2 = (f32[31,512]{1,0:T(8,128)}, f32[31,512]{1,0:T(8,128)S(1)}, u32[]{:S(2)}, u32[]{:S(2)}) collective-permute-start(f32[31,512]{1,0:T(8,128)} %get-tuple-element.30), channel_id=1, source_target_pairs={{0,1},{1,2},{2,3},{3,4},{4,5},{5,6},{6,7},{7,8},{8,9},{9,10},{10,1... | collective-permute-start | bytes 190472 | tf_op jit(solution)/shard_map/ppermute | solution.py:17
  160.0 21.4 %collective-permute-start.3 = (f32[31,512]{1,0:T(8,128)}, f32[31,512]{1,0:T(8,128)}, u32[]{:S(2)}, u32[]{:S(2)}) collective-permute-start(f32[31,512]{1,0:T(8,128)} %get-tuple-element.31), channel_id=1, source_target_pairs={{1,0},{2,1},{3,2},{4,3},{5,4},{6,5},{7,6},{8,7},{9,8},{10,9},{11,1... | collective-permute-start | bytes 190472 | tf_op jit(solution)/shard_map/ppermute | solution.py:20
  176.0 5.4 %copy-start.3 = (f32[512,512]{1,0:T(8,128)S(1)}, f32[512,512]{1,0:T(8,128)}, u32[]{:S(2)}) copy-start(f32[512,512]{1,0:T(8,128)} %copy-done.2) | copy-start | bytes 3145732
  176.9 41.6 %all-to-all-start.5 = ((bf16[16,32,512]{2,1,0:T(8,128)(2,1)}), bf16[16,32,512]{2,1,0:T(8,128)(2,1)}, u32[]{:S(2)}, u32[]{:S(2)}) async-start(bf16[16,32,512]{2,1,0:T(8,128)(2,1)} %broadcast_in_dim.10), calls=%async_computation.5 | async-start | bytes 1048576 | tf_op jit(solution)/shard_map/all_to_all | solution.py:105
  194.8 3.9 %copy-start.5 = (bf16[512,512]{1,0:T(8,128)(2,1)S(1)}, bf16[512,512]{1,0:T(8,128)(2,1)}, u32[]{:S(2)}) copy-start(bf16[512,512]{1,0:T(8,128)(2,1)} %get-tuple-element.15) | copy-start | bytes 1572868
  204.7 5.7 %copy-start.8 = (f32[256,256]{1,0:T(8,128)S(1)}, f32[256,256]{1,0:T(8,128)}, u32[]{:S(2)}) copy-start(f32[256,256]{1,0:T(8,128)} %reshape.106) | copy-start | bytes 786436
  290.6 1.1 copy-start.6
  291.8 21.4 %all-to-all-start.7 = ((f32[16,72,256]{2,1,0:T(8,128)}), f32[16,72,256]{2,1,0:T(8,128)S(1)}, u32[]{:S(2)}, u32[]{:S(2)}) async-start(f32[16,72,256]{2,1,0:T(8,128)} %broadcast_in_dim.11), calls=%async_computation.7 | async-start | bytes 2359296 | tf_op jit(solution)/shard_map/all_to_all | solution.py:105

commit v7 on v6

--- a/solution.py
+++ b/solution.py
@@ -97,6 +97,26 @@
 def scatter_sum(parts, axis):
     got = lax.all_to_all(parts, axis, 0, 0, tiled=False)
     return jnp.sum(got, axis=0)
+
+
+def pair_scatter_sum(parts, axis):
+    count, rows = parts.shape[0], parts.shape[1]
+    core = lax.axis_index(axis) % 2
+    pair = [(i, i ^ 1) for i in range(count)]
+    grouped = parts.reshape((count // 2, 2) + parts.shape[1:])
+    mine = lax.dynamic_index_in_dim(grouped, core, axis=1, keepdims=False)
+    theirs = lax.dynamic_index_in_dim(grouped, 1 - core, axis=1, keepdims=False)
+    chip = mine + lax.ppermute(theirs, axis, pair)
+    first, second = chip[:, : rows // 2], chip[:, rows // 2 :]
+    slabs = jnp.where(
+        core == 0, jnp.stack([first, second], axis=1), jnp.stack([second, first], axis=1)
+    ).reshape((count, rows // 2) + parts.shape[2:])
+    got = lax.all_to_all(slabs, axis, 0, 0, tiled=False).reshape(
+        (count // 2, 2, rows // 2) + parts.shape[2:]
+    )
+    same = jnp.sum(lax.dynamic_index_in_dim(got, core, axis=1, keepdims=False), axis=0)
+    cross = jnp.sum(lax.dynamic_index_in_dim(got, 1 - core, axis=1, keepdims=False), axis=0)
+    return jnp.concatenate([same, lax.ppermute(cross, axis, pair)], axis=0)
 
 
 def gather_all(piece, axis):
@@ -157,7 +177,7 @@
     cut = readin_part.shape[1]
     packed = jnp.concatenate([readin_part, small], axis=1)
     denoised, packed = lax.optimization_barrier((denoised, packed))
-    reduced = scatter_sum(packed, "tm")
+    reduced = pair_scatter_sum(packed, "tm")
     grad_readin = reduced[:cut]
     small_sum = gather_all(reduced[cut:], "tm").reshape(-1, width)
     outs = []

time: 325 us -> 309 us (0.951)
  blocking collectives: 146 us -> 118 us
  starting transfers between devices: 27.8 us -> 37.3 us
  waiting for transfers between devices: 59.4 us -> 54.7 us
    all_to_all x3 -> x2, blocking collectives: 129 us -> 61.2 us  [scatter_sum(): got = lax.all_to_all(parts, axis, 0, 0, tiled=False)]
    all_to_all x0 -> x1, blocking collectives: none -> 40.1 us  [pair_scatter_sum(): lax.all_to_all(slabs, axis, 0, 0, tiled=False)]
    ppermute x0 -> x2, waiting for transfers between devices: none -> 6.01 us  [the longest x1 4.97 us: pair_scatter_sum(): chip = mine + lax.ppermute(theirs, axis, pair)]
    all_to_all x1, waiting for transfers between devices: 12.8 us -> 8.05 us  [scatter_sum(): got = lax.all_to_all(parts, axis, 0, 0, tiled=False)]
    ppermute x2, starting transfers between devices: 3.88 us -> 8.4 us  [with_halo(): lax.ppermute(lax.slice_in_dim(block, 0, width, axis=dim), axis, backward)]
    all_to_all x3, waiting for transfers between devices: 43 us -> 39.3 us  [gather_all(): return lax.all_to_all(spread, axis, 0, 0, tiled=False)]
    ppermute x2, waiting for transfers between devices: 3.65 us -> 0.01 us  [with_halo(): lax.ppermute(lax.slice_in_dim(block, 0, width, axis=dim), axis, backward)]
    squeeze x0 -> x1, local copies, waits for them, and re-layouts: none -> 3.55 us  [pair_scatter_sum(): theirs = lax.dynamic_index_in_dim(grouped, 1 - core, axis=1, keepdims=False)]
  transfers between devices with their start and end apart: 8 -> 10, of which waited for: 4 -> 6; matrix products, arithmetic and copies ran while one was open for 13% -> 14% of each run, Pallas kernels for 4% -> 4%
where the time goes in v7:
time: 309 us; the launch traced here: 307 us
  blocking collectives  118 us (38%)
  waiting for transfers between devices  54.7 us (18%)
  local copies, waits for them, and re-layouts  37.4 us (12%)
  starting transfers between devices  37.3 us (12%)
  matrix products  20.9 us (7%)
  other arithmetic  19.8 us (6%)
  Pallas kernels  18.2 us (6%)
    all_to_all x2, blocking collectives, scatter_sum(): got = lax.all_to_all(parts, axis, 0, 0, tiled=False)  61.2 us
    all_to_all x1, blocking collectives, pair_scatter_sum(): lax.all_to_all(slabs, axis, 0, 0, tiled=False)  40.1 us
    all_to_all x3, waiting for transfers between devices, gather_all(): return lax.all_to_all(spread, axis, 0, 0, tiled=False)  39.3 us
    all_to_all x1, blocking collectives, gather_all(): return lax.all_to_all(spread, axis, 0, 0, tiled=False)  16.8 us
    all_to_all x3, starting transfers between devices, gather_all(): return lax.all_to_all(spread, axis, 0, 0, tiled=False)  15.6 us
    pallas_call x1, Pallas kernels, bwd_conv(): pl.pallas_call(_bwd_conv_kernel, out_shape=(jax.ShapeDtypeStruct((rows, w...  11.4 us
    dot_general x4, matrix products, over_time(): lax.dot_general(left, right, (((0,), (0,)), ((), ())), preferred_element_...  10.7 us
    ppermute x2, starting transfers between devices, with_halo(): lax.ppermute(lax.slice_in_dim(block, 0, width, axis=dim), axis, backward)  8.4 us
  transfers between devices with their start and end apart: 10, of which 6 were waited for; matrix products, arithmetic and copies ran while one was open for 14% of the time, Pallas kernels for 4%

profile of v7, /device:TPU:1, one launch (start us, length us, event | category | flops | bytes accessed | tf_op | source)
XLA Modules:
  0.0 307.3 jit_solution(9227384708687517004)
XLA Ops:
  0.6 1.6 copy-done
  2.2 3.4 %fusion.9 = f32[512,256]{1,0:T(8,128)S(1)} fusion(bf16[512,4096]{1,0:T(8,128)(2,1)} %param.8, bf16[4096,256]{1,0:T(8,128)(2,1)S(1)} %copy-done), kind=kOutput, calls=%fused_computation.35 | convolution fusion | flops 1073741824 | bytes 6815744 | tf_op jit(solution)/shard_map/dot_general | solution.py:140
  5.7 28.6 %all_to_all.40 = f32[16,32,256]{2,1,0:T(8,128)S(1)} all-to-all(f32[16,32,256]{2,1,0:T(8,128)S(1)} %bitcast.56), channel_id=1, replica_groups=mesh['neuron'=16,'tm'=16] {'neuron'}, dimensions={0} | all-to-all | bytes 1048576 | tf_op jit(solution)/shard_map/all_to_all | solution.py:98
  34.3 16.8 %all_to_all.41 = bf16[16,32,256]{2,1,0:T(8,128)(2,1)S(1)} all-to-all(bf16[16,32,256]{2,1,0:T(8,128)(2,1)S(1)} %broadcast_in_dim.8), channel_id=1, replica_groups=mesh['neuron'=16,'tm'=16] {'neuron'}, dimensions={0} | all-to-all | bytes 524288 | tf_op jit(solution)/shard_map/all_to_all | solution.py:125
  51.1 1.2 fusion.10.mid_ref
  52.4 4.0 %collective-permute-start.1 = (f32[31,512]{1,0:T(8,128)S(1)}, f32[31,512]{1,0:T(8,128)S(1)}, u32[]{:S(2)}, u32[]{:S(2)}) collective-permute-start(f32[31,512]{1,0:T(8,128)S(1)} %get-tuple-element.30), channel_id=1, source_target_pairs={{1,0},{2,1},{3,2},{4,3},{5,4},{6,5},{7,6},{8,7},{9,8},{10,9},{11,1... | collective-permute-start | bytes 190472 | tf_op jit(solution)/shard_map/ppermute | solution.py:20
  56.5 2.1 collective-permute-start
  58.6 1.3 collective-permute-done
  59.9 1.2 pad_maximum_fusion.1.x_ref
  61.0 6.8 %shard_map.135 = f32[512,512]{1,0:T(8,128)} custom-call(f32[574,512]{1,0:T(8,128)} %pad_maximum_fusion.1.x_ref, f32[512,512]{1,0:T(8,128)} %copy-done.3, f32[63,512]{1,0:T(8,128)} %k_ref.3), custom_call_target="tpu_custom_call" | custom-call | tf_op jit(solution)/shard_map/pallas_call | solution.py:38
  67.9 1.4 multiply_reduce_fusion.2
  69.3 1.6 fusion.3
  71.6 1.4 fusion.1
  73.6 32.6 %all_to_all.42 = f32[16,32,512]{2,1,0:T(8,128)S(1)} all-to-all(f32[16,32,512]{2,1,0:T(8,128)S(1)} %bitcast.52), channel_id=1, replica_groups=mesh['neuron'=16,'tm'=16] {'neuron'}, dimensions={0} | all-to-all | bytes 2097152 | tf_op jit(solution)/shard_map/all_to_all | solution.py:98
  107.4 4.5 %all-to-all-start.3 = ((f32[16,32,512]{2,1,0:T(8,128)}), f32[16,32,512]{2,1,0:T(8,128)}, u32[]{:S(2)}, u32[]{:S(2)}) async-start(f32[16,32,512]{2,1,0:T(8,128)} %broadcast_in_dim.9), calls=%async_computation.3 | async-start | bytes 2097152 | tf_op jit(solution)/shard_map/all_to_all | solution.py:125
  111.9 2.2 fusion.5
  114.2 23.7 %all-to-all-done.3 = f32[16,32,512]{2,1,0:T(8,128)} async-done(((f32[16,32,512]{2,1,0:T(8,128)}), f32[16,32,512]{2,1,0:T(8,128)}, u32[]{:S(2)}, u32[]{:S(2)}) %all-to-all-start.3) | async-done | bytes 1048608 | tf_op jit(solution)/shard_map/all_to_all | solution.py:125
  137.9 7.2 %all-to-all-start.4 = ((f32[16,32,512]{2,1,0:T(8,128)}), f32[16,32,512]{2,1,0:T(8,128)}, u32[]{:S(2)}, u32[]{:S(2)}) async-start(f32[16,32,512]{2,1,0:T(8,128)} %bitcast.53), calls=%async_computation.4 | async-start | bytes 2097152 | tf_op jit(solution)/shard_map/all_to_all | solution.py:98
  146.3 1.7 reshape.117
  148.0 2.1 fusion.4
  150.1 1.7 reshape.118
  151.8 1.6 multiply_reduce_fusion
  153.4 1.7 multiply_subtract_fusion.d_ref
  156.8 4.4 %collective-permute-start.3 = (f32[31,512]{1,0:T(8,128)}, f32[31,512]{1,0:T(8,128)S(1)}, u32[]{:S(2)}, u32[]{:S(2)}) collective-permute-start(f32[31,512]{1,0:T(8,128)} %get-tuple-element.28), channel_id=1, source_target_pairs={{1,0},{2,1},{3,2},{4,3},{5,4},{6,5},{7,6},{8,7},{9,8},{10,9},{11,1... | collective-permute-start | bytes 190472 | tf_op jit(solution)/shard_map/ppermute | solution.py:20
  161.1 1.9 collective-permute-start.2
  163.1 8.1 %all-to-all-done.4 = f32[16,32,512]{2,1,0:T(8,128)} async-done(((f32[16,32,512]{2,1,0:T(8,128)}), f32[16,32,512]{2,1,0:T(8,128)}, u32[]{:S(2)}, u32[]{:S(2)}) %all-to-all-start.4) | async-done | bytes 1048608 | tf_op jit(solution)/shard_map/all_to_all | solution.py:98
  171.1 1.3 reduce_sum.75
  173.3 7.2 %all-to-all-start.5 = ((bf16[16,32,512]{2,1,0:T(8,128)(2,1)}), bf16[16,32,512]{2,1,0:T(8,128)(2,1)}, u32[]{:S(2)}, u32[]{:S(2)}) async-start(bf16[16,32,512]{2,1,0:T(8,128)(2,1)} %broadcast_in_dim.10), calls=%async_computation.5 | async-start | bytes 1048576 | tf_op jit(solution)/shard_map/all_to_all | solution.py:125
  180.6 2.4 pad_maximum_fusion.2.g_ref
  183.0 11.4 %shard_map.136 = (bf16[512,512]{1,0:T(8,128)(2,1)}, f32[63,512]{1,0:T(8,128)}) custom-call(f32[574,512]{1,0:T(8,128)} %pad_maximum_fusion.2.g_ref, f32[512,512]{1,0:T(8,128)} %copy-done.2, f32[574,512]{1,0:T(8,128)} %pad_maximum_fusion.1.x_ref, f32[63,512]{1,0:T(8,128)} %k_ref.3), custom_call_target="tpu_custom_call" | custom-call | tf_op jit(solution)/shard_map/pallas_call | solution.py:71
  194.4 1.4 fusion.12
  196.7 1.6 reshape.115
  198.3 6.0 %convolution_bitcast_fusion = f32[4096,256]{0,1:T(8,128)} fusion(bf16[512,4096]{1,0:T(8,128)(2,1)} %param.8, bf16[512,512]{1,0:T(8,128)(2,1)S(1)} %copy-done.4, bf16[256,512]{1,0:T(8,128)(2,1)} %param.10), kind=kOutput, calls=%fused_computation | convolution fusion | flops 1208090624 | bytes 9175040 | tf_op jit(solution)/shard_map/dot_general | solution.py:92
  204.3 5.7 %copy.18 = f32[4096,256]{1,0:T(8,128)} copy(f32[4096,256]{0,1:T(8,128)} %convolution_bitcast_fusion) | data formatting | bytes 8388608 | tf_op jit(solution)/shard_map/reshape | solution.py:176
  210.0 3.0 concatenate.17
  213.0 5.0 %pad_maximum_fusion = f32[16,328,256]{2,1,0:T(8,128)} fusion(f32[16,72,256]{2,1,0:T(8,128)S(1)} %bitcast.51, f32[16,256,256]{2,1,0:T(8,128)} %bitcast.44), kind=kLoop, calls=%fused_computation.1 | loop fusion | flops 1343488 | bytes 10747904 | tf_op jit(solution)/shard_map/concatenate | solution.py:178
  218.0 3.6 %dynamic-slice_bitcast_fusion = f32[8,328,256]{2,1,0:T(8,128)} fusion(f32[8,2,328,256]{3,2,1,0:T(8,128)} %bitcast.42, s32[]{:T(128)S(6)} %select_n.36), kind=kLoop, calls=%fused_computation.4 | loop fusion | bytes 5373956 | tf_op jit(solution)/shard_map/jit(dynamic_index_in_dim)/squeeze | solution.py:108
  221.6 1.3 collective-permute-start.4
  222.9 5.0 %collective-permute-done.4 = f32[8,328,256]{2,1,0:T(8,128)} collective-permute-done((f32[8,328,256]{2,1,0:T(8,128)}, f32[8,328,256]{2,1,0:T(8,128)}, u32[]{:S(2)}, u32[]{:S(2)}) %collective-permute-start.4) | collective-permute-done | bytes 2687008 | tf_op jit(solution)/shard_map/ppermute | solution.py:109
  227.9 2.9 bitcast_add_fusion
  231.6 40.1 %all_to_all.43 = f32[16,164,256]{2,1,0:T(8,128)S(1)} all-to-all(f32[16,164,256]{2,1,0:T(8,128)S(1)} %bitcast.46), channel_id=1, replica_groups=mesh['neuron'=16,'tm'=16] {'tm'}, dimensions={0} | all-to-all | bytes 5373952 | tf_op jit(solution)/shard_map/all_to_all | solution.py:114
  275.5 3.9 %all-to-all-start.7 = ((f32[16,72,256]{2,1,0:T(8,128)}), f32[16,72,256]{2,1,0:T(8,128)S(1)}, u32[]{:S(2)}, u32[]{:S(2)}) async-start(f32[16,72,256]{2,1,0:T(8,128)} %broadcast_in_dim.11), calls=%async_computation.7 | async-start | bytes 2359296 | tf_op jit(solution)/shard_map/all_to_all | solution.py:125
  279.4 1.6 pad_maximum_fusion.3
  281.0 15.6 %all-to-all-done.7 = f32[16,72,256]{2,1,0:T(8,128)S(1)} async-done(((f32[16,72,256]{2,1,0:T(8,128)}), f32[16,72,256]{2,1,0:T(8,128)S(1)}, u32[]{:S(2)}, u32[]{:S(2)}) %all-to-all-start.7) | async-done | bytes 1179680 | tf_op jit(solution)/shard_map/all_to_all | solution.py:125
  298.8 2.0 reshape.123
  300.8 1.6 reshape.124
  303.0 1.7 reshape.126
  305.4 1.9 copy.21
  (55 shorter events, 15.4 us)
Async XLA Ops:
  0.6 1.6 copy-start
  52.4 8.7 %copy-start.3 = (f32[512,512]{1,0:T(8,128)}, f32[512,512]{1,0:T(8,128)S(1)}, u32[]{:S(2)}) copy-start(f32[512,512]{1,0:T(8,128)S(1)} %fusion.10.mid_ref) | copy-start | bytes 3145732
  52.4 6.2 %collective-permute-start.1 = (f32[31,512]{1,0:T(8,128)S(1)}, f32[31,512]{1,0:T(8,128)S(1)}, u32[]{:S(2)}, u32[]{:S(2)}) collective-permute-start(f32[31,512]{1,0:T(8,128)S(1)} %get-tuple-element.30), channel_id=1, source_target_pairs={{1,0},{2,1},{3,2},{4,3},{5,4},{6,5},{7,6},{8,7},{9,8},{10,9},{11,1... | collective-permute-start | bytes 190472 | tf_op jit(solution)/shard_map/ppermute | solution.py:20
  56.5 3.4 %collective-permute-start = (f32[31,512]{1,0:T(8,128)S(1)}, f32[31,512]{1,0:T(8,128)S(1)}, u32[]{:S(2)}, u32[]{:S(2)}) collective-permute-start(f32[31,512]{1,0:T(8,128)S(1)} %get-tuple-element.29), channel_id=1, source_target_pairs={{0,1},{1,2},{2,3},{3,4},{4,5},{5,6},{6,7},{7,8},{8,9},{9,10},{10,1... | collective-permute-start | bytes 190472 | tf_op jit(solution)/shard_map/ppermute | solution.py:17
  61.0 8.2 %copy-start.7 = (bf16[512,128]{1,0:T(8,128)(2,1)S(1)}, bf16[512,128]{1,0:T(8,128)(2,1)}, u32[]{:S(2)}) copy-start(bf16[512,128]{1,0:T(8,128)(2,1)} %param.13) | copy-start | bytes 393220
  61.0 8.2 %copy-start.11 = (f32[512]{0:T(512)S(1)}, f32[512]{0:T(512)}, u32[]{:S(2)}) copy-start(f32[512]{0:T(512)} %param.12) | copy-start | bytes 6148
  70.9 0.7 copy-start.5
  72.9 0.7 copy-start.8
  107.4 37.7 %copy-start.1 = (f32[512,512]{1,0:T(8,128)S(1)}, f32[512,512]{1,0:T(8,128)}, u32[]{:S(2)}) copy-start(f32[512,512]{1,0:T(8,128)} %shard_map.135) | copy-start | bytes 3145732
  107.4 37.7 %copy-start.9 = (bf16[512,128]{1,0:T(8,128)(2,1)S(1)}, bf16[512,128]{1,0:T(8,128)(2,1)}, u32[]{:S(2)}) copy-start(bf16[512,128]{1,0:T(8,128)(2,1)} %copy-done.8) | copy-start | bytes 393220
  107.4 30.5 %all-to-all-start.3 = ((f32[16,32,512]{2,1,0:T(8,128)}), f32[16,32,512]{2,1,0:T(8,128)}, u32[]{:S(2)}, u32[]{:S(2)}) async-start(f32[16,32,512]{2,1,0:T(8,128)} %broadcast_in_dim.9), calls=%async_computation.3 | async-start | bytes 2097152 | tf_op jit(solution)/shard_map/all_to_all | solution.py:125
  137.9 33.2 %all-to-all-start.4 = ((f32[16,32,512]{2,1,0:T(8,128)}), f32[16,32,512]{2,1,0:T(8,128)}, u32[]{:S(2)}, u32[]{:S(2)}) async-start(f32[16,32,512]{2,1,0:T(8,128)} %bitcast.53), calls=%async_computation.4 | async-start | bytes 2097152 | tf_op jit(solution)/shard_map/all_to_all | solution.py:98
  155.1 1.0 copy-start.2
  156.8 23.8 %collective-permute-start.3 = (f32[31,512]{1,0:T(8,128)}, f32[31,512]{1,0:T(8,128)S(1)}, u32[]{:S(2)}, u32[]{:S(2)}) collective-permute-start(f32[31,512]{1,0:T(8,128)} %get-tuple-element.28), channel_id=1, source_target_pairs={{1,0},{2,1},{3,2},{4,3},{5,4},{6,5},{7,6},{8,7},{9,8},{10,9},{11,1... | collective-permute-start | bytes 190472 | tf_op jit(solution)/shard_map/ppermute | solution.py:20
  161.1 19.4 %collective-permute-start.2 = (f32[31,512]{1,0:T(8,128)}, f32[31,512]{1,0:T(8,128)}, u32[]{:S(2)}, u32[]{:S(2)}) collective-permute-start(f32[31,512]{1,0:T(8,128)} %get-tuple-element.27), channel_id=1, source_target_pairs={{0,1},{1,2},{2,3},{3,4},{4,5},{5,6},{6,7},{7,8},{8,9},{9,10},{10,1... | collective-permute-start | bytes 190472 | tf_op jit(solution)/shard_map/ppermute | solution.py:17
  173.3 44.8 %all-to-all-start.5 = ((bf16[16,32,512]{2,1,0:T(8,128)(2,1)}), bf16[16,32,512]{2,1,0:T(8,128)(2,1)}, u32[]{:S(2)}, u32[]{:S(2)}) async-start(bf16[16,32,512]{2,1,0:T(8,128)(2,1)} %broadcast_in_dim.10), calls=%async_computation.5 | async-start | bytes 1048576 | tf_op jit(solution)/shard_map/all_to_all | solution.py:125
  194.4 3.9 %copy-start.4 = (bf16[512,512]{1,0:T(8,128)(2,1)S(1)}, bf16[512,512]{1,0:T(8,128)(2,1)}, u32[]{:S(2)}) copy-start(bf16[512,512]{1,0:T(8,128)(2,1)} %get-tuple-element.15) | copy-start | bytes 1572868
  204.3 5.7 %copy-start.6 = (f32[256,256]{1,0:T(8,128)S(1)}, f32[256,256]{1,0:T(8,128)}, u32[]{:S(2)}) copy-start(f32[256,256]{1,0:T(8,128)} %reshape.117) | copy-start | bytes 786436
  221.6 6.3 %collective-permute-start.4 = (f32[8,328,256]{2,1,0:T(8,128)}, f32[8,328,256]{2,1,0:T(8,128)}, u32[]{:S(2)}, u32[]{:S(2)}) collective-permute-start(f32[8,328,256]{2,1,0:T(8,128)} %dynamic-slice_bitcast_fusion), channel_id=1, source_target_pairs={{0,1},{1,0},{2,3},{3,2},{4,5},{5,4},{6,7},{7,6},{8,9},{9,8},{10,11... | collective-permute-start | bytes 8060936 | tf_op jit(solution)/shard_map/ppermute | solution.py:109
  272.0 1.8 collective-permute-start.5
  273.7 0.7 copy-start.10
  275.5 21.1 %all-to-all-start.7 = ((f32[16,72,256]{2,1,0:T(8,128)}), f32[16,72,256]{2,1,0:T(8,128)S(1)}, u32[]{:S(2)}, u32[]{:S(2)}) async-start(f32[16,72,256]{2,1,0:T(8,128)} %broadcast_in_dim.11), calls=%async_computation.7 | async-start | bytes 2359296 | tf_op jit(solution)/shard_map/all_to_all | solution.py:125

commit v8 on v7

--- a/solution.py
+++ b/solution.py
@@ -156,17 +156,17 @@
     partial_normed = jnp.dot(dpre, w_one.T, preferred_element_type=jnp.float32)
     dnormed_rows = scatter_sum(split_rows(partial_normed, nn), "neuron")
     dnormed = gather_all(dnormed_rows, "neuron").reshape(rows, -1)
-    partial_mix, dnormed = lax.optimization_barrier((partial_mix, dnormed))
-    mix_rows = scatter_sum(split_rows(partial_mix, nn), "neuron")
-    mixed_rows = lax.dynamic_slice_in_dim(mixed, me * share, share, 0)
-    denoised_rows = (mixed_rows + mix_rows).astype(jnp.bfloat16)
-    denoised = gather_all(denoised_rows, "neuron").reshape(rows, -1)
     local_gain = jnp.sum(dnormed * mixed * scale, axis=0)
     dgained = dnormed * gain[None, :]
     inner = jnp.mean(dgained * mixed, axis=1, keepdims=True)
     dmixed = cotangent.astype(jnp.float32) + scale * dgained - mixed * scale**3 * inner
     padded_grad = with_halo(dmixed, (("tm", 0),), half)
     dlifted, local_kernel = bwd_conv(padded_grad, dmixed, padded, kernel)
+    partial_mix, dlifted = lax.optimization_barrier((partial_mix, dlifted))
+    mix_rows = scatter_sum(split_rows(partial_mix, nn), "neuron")
+    mixed_rows = lax.dynamic_slice_in_dim(mixed, me * share, share, 0)
+    denoised_rows = (mixed_rows + mix_rows).astype(jnp.bfloat16)
+    denoised = gather_all(denoised_rows, "neuron").reshape(rows, -1)
     local_proj = over_time(latent, dlifted)
     dlatent = jnp.dot(dlifted, proj.T, preferred_element_type=jnp.float32).astype(jnp.bfloat16)
     local_readin = over_time(signal, dlatent)
@@ -176,10 +176,11 @@
     readin_part = local_readin.reshape(nt, -1, width)
     cut = readin_part.shape[1]
     packed = jnp.concatenate([readin_part, small], axis=1)
-    denoised, packed = lax.optimization_barrier((denoised, packed))
     reduced = pair_scatter_sum(packed, "tm")
     grad_readin = reduced[:cut]
-    small_sum = gather_all(reduced[cut:], "tm").reshape(-1, width)
+    small_part = reduced[cut:]
+    denoised, small_part = lax.optimization_barrier((denoised, small_part))
+    small_sum = gather_all(small_part, "tm").reshape(-1, width)
     outs = []
     at = 0
     for g in grads:

time: 309 us -> 343 us (1.11)
  waiting for transfers between devices: 54.7 us -> 109 us
  blocking collectives: 118 us -> 78.2 us
  local copies, waits for them, and re-layouts: 37.4 us -> 46.5 us
  starting transfers between devices: 37.3 us -> 45.9 us
    all_to_all x1 -> x0, blocking collectives: 40.1 us -> none  [pair_scatter_sum(): lax.all_to_all(slabs, axis, 0, 0, tiled=False)]
    all_to_all x0 -> x1, waiting for transfers between devices: none -> 32.8 us  [pair_scatter_sum(): lax.all_to_all(slabs, axis, 0, 0, tiled=False)]
    concatenate x0 -> x2, local copies, waits for them, and re-layouts: none -> 13.9 us  [body(): packed = jnp.concatenate([readin_part, small], axis=1)]
    all_to_all x1, waiting for transfers between devices: 8.05 us -> 21.1 us  [scatter_sum(): got = lax.all_to_all(parts, axis, 0, 0, tiled=False)]
    all_to_all x3, waiting for transfers between devices: 39.3 us -> 52.1 us  [gather_all(): return lax.all_to_all(spread, axis, 0, 0, tiled=False)]
    all_to_all x0 -> x1, starting transfers between devices: none -> 8.23 us  [pair_scatter_sum(): lax.all_to_all(slabs, axis, 0, 0, tiled=False)]
    reshape x1 -> x0, local copies, waits for them, and re-layouts: 5.7 us -> none  [body(): readin_part = local_readin.reshape(nt, -1, width)]
    concatenate x1 -> x0, other arithmetic: 5.05 us -> none  [body(): packed = jnp.concatenate([readin_part, small], axis=1)]
  transfers between devices with their start and end apart: 10 -> 11, of which waited for: 6 -> 8; matrix products, arithmetic and copies ran while one was open for 14% -> 5% of each run, Pallas kernels for 4% -> 0%
where the time goes in v8:
time: 343 us; the launch traced here: 341 us
  waiting for transfers between devices  109 us (32%)
  blocking collectives  78.2 us (23%)
  local copies, waits for them, and re-layouts  46.5 us (14%)
  starting transfers between devices  45.9 us (13%)
  other arithmetic  21 us (6%)
  matrix products  20.7 us (6%)
  Pallas kernels  18.2 us (5%)
    all_to_all x2, blocking collectives, scatter_sum(): got = lax.all_to_all(parts, axis, 0, 0, tiled=False)  61.4 us
    all_to_all x3, waiting for transfers between devices, gather_all(): return lax.all_to_all(spread, axis, 0, 0, tiled=False)  52.1 us
    all_to_all x1, waiting for transfers between devices, pair_scatter_sum(): lax.all_to_all(slabs, axis, 0, 0, tiled=False)  32.8 us
    all_to_all x1, waiting for transfers between devices, scatter_sum(): got = lax.all_to_all(parts, axis, 0, 0, tiled=False)  21.1 us
    all_to_all x1, blocking collectives, gather_all(): return lax.all_to_all(spread, axis, 0, 0, tiled=False)  16.8 us
    all_to_all x3, starting transfers between devices, gather_all(): return lax.all_to_all(spread, axis, 0, 0, tiled=False)  15.3 us
    concatenate x2, local copies, waits for them, and re-layouts, body(): packed = jnp.concatenate([readin_part, small], axis=1)  13.9 us
    pallas_call x1, Pallas kernels, bwd_conv(): pl.pallas_call(_bwd_conv_kernel, out_shape=(jax.ShapeDtypeStruct((rows, w...  11.4 us
  transfers between devices with their start and end apart: 11, of which 8 were waited for; matrix products, arithmetic and copies ran while one was open for 5% of the time, Pallas kernels for 0%

profile of v8, /device:TPU:1, one launch (start us, length us, event | category | flops | bytes accessed | tf_op | source)
XLA Modules:
  0.0 340.8 jit_solution(14317952315889294861)
XLA Ops:
  0.6 1.6 copy-done
  2.2 3.4 %fusion.16 = f32[512,256]{1,0:T(8,128)S(1)} fusion(bf16[512,4096]{1,0:T(8,128)(2,1)} %param.8, bf16[4096,256]{1,0:T(8,128)(2,1)S(1)} %copy-done), kind=kOutput, calls=%fused_computation.44 | convolution fusion | flops 1073741824 | bytes 6815744 | tf_op jit(solution)/shard_map/dot_general | solution.py:140
  5.7 28.6 %all_to_all.40 = f32[16,32,256]{2,1,0:T(8,128)S(1)} all-to-all(f32[16,32,256]{2,1,0:T(8,128)S(1)} %bitcast.62), channel_id=1, replica_groups=mesh['neuron'=16,'tm'=16] {'neuron'}, dimensions={0} | all-to-all | bytes 1048576 | tf_op jit(solution)/shard_map/all_to_all | solution.py:98
  34.3 16.8 %all_to_all.41 = bf16[16,32,256]{2,1,0:T(8,128)(2,1)S(1)} all-to-all(bf16[16,32,256]{2,1,0:T(8,128)(2,1)S(1)} %broadcast_in_dim.8), channel_id=1, replica_groups=mesh['neuron'=16,'tm'=16] {'neuron'}, dimensions={0} | all-to-all | bytes 524288 | tf_op jit(solution)/shard_map/all_to_all | solution.py:125
  51.1 1.2 fusion.17.mid_ref
  52.4 4.0 %collective-permute-start.1 = (f32[31,512]{1,0:T(8,128)S(1)}, f32[31,512]{1,0:T(8,128)S(1)}, u32[]{:S(2)}, u32[]{:S(2)}) collective-permute-start(f32[31,512]{1,0:T(8,128)S(1)} %get-tuple-element.30), channel_id=1, source_target_pairs={{1,0},{2,1},{3,2},{4,3},{5,4},{6,5},{7,6},{8,7},{9,8},{10,9},{11,1... | collective-permute-start | bytes 190472 | tf_op jit(solution)/shard_map/ppermute | solution.py:20
  56.5 2.1 collective-permute-start
  58.6 1.3 collective-permute-done
  59.9 1.2 pad_maximum_fusion.x_ref
  61.1 6.8 %shard_map.135 = f32[512,512]{1,0:T(8,128)} custom-call(f32[574,512]{1,0:T(8,128)} %pad_maximum_fusion.x_ref, f32[512,512]{1,0:T(8,128)} %copy-done.3, f32[63,512]{1,0:T(8,128)} %k_ref.3), custom_call_target="tpu_custom_call" | custom-call | tf_op jit(solution)/shard_map/pallas_call | solution.py:38
  67.9 1.4 multiply_reduce_fusion.1
  69.3 1.6 fusion.10
  71.6 1.4 fusion.6
  73.6 32.8 %all_to_all.42 = f32[16,32,512]{2,1,0:T(8,128)} all-to-all(f32[16,32,512]{2,1,0:T(8,128)S(1)} %bitcast.57), channel_id=1, replica_groups=mesh['neuron'=16,'tm'=16] {'neuron'}, dimensions={0} | all-to-all | bytes 2097152 | tf_op jit(solution)/shard_map/all_to_all | solution.py:98
  106.4 2.0 reduce_sum.74
  108.5 2.0 broadcast_in_dim.9
  110.4 4.3 %all-to-all-start.3 = ((f32[16,32,512]{2,1,0:T(8,128)}), f32[16,32,512]{2,1,0:T(8,128)}, u32[]{:S(2)}, u32[]{:S(2)}) async-start(f32[16,32,512]{2,1,0:T(8,128)} %broadcast_in_dim.9), calls=%async_computation.3 | async-start | bytes 2097152 | tf_op jit(solution)/shard_map/all_to_all | solution.py:125
  114.8 2.3 fusion.12
  118.2 22.5 %all-to-all-done.3 = f32[16,32,512]{2,1,0:T(8,128)} async-done(((f32[16,32,512]{2,1,0:T(8,128)}), f32[16,32,512]{2,1,0:T(8,128)}, u32[]{:S(2)}, u32[]{:S(2)}) %all-to-all-start.3) | async-done | bytes 1048608 | tf_op jit(solution)/shard_map/all_to_all | solution.py:125
  140.7 1.6 fusion.8
  142.4 1.7 multiply_subtract_fusion.d_ref
  145.8 7.2 %collective-permute-start.3 = (f32[31,512]{1,0:T(8,128)}, f32[31,512]{1,0:T(8,128)S(1)}, u32[]{:S(2)}, u32[]{:S(2)}) collective-permute-start(f32[31,512]{1,0:T(8,128)} %get-tuple-element.28), channel_id=1, source_target_pairs={{1,0},{2,1},{3,2},{4,3},{5,4},{6,5},{7,6},{8,7},{9,8},{10,9},{11,1... | collective-permute-start | bytes 190472 | tf_op jit(solution)/shard_map/ppermute | solution.py:20
  153.0 3.6 %collective-permute-start.2 = (f32[31,512]{1,0:T(8,128)}, f32[31,512]{1,0:T(8,128)S(1)}, u32[]{:S(2)}, u32[]{:S(2)}) collective-permute-start(f32[31,512]{1,0:T(8,128)} %get-tuple-element.27), channel_id=1, source_target_pairs={{0,1},{1,2},{2,3},{3,4},{4,5},{5,6},{6,7},{7,8},{8,9},{9,10},{10,1... | collective-permute-start | bytes 190472 | tf_op jit(solution)/shard_map/ppermute | solution.py:17
  157.6 1.7 reshape.114
  159.3 1.7 reshape.115
  161.0 2.4 pad_maximum_fusion.1.g_ref
  163.4 11.4 %shard_map.136 = (bf16[512,512]{1,0:T(8,128)(2,1)}, f32[63,512]{1,0:T(8,128)}) custom-call(f32[574,512]{1,0:T(8,128)} %pad_maximum_fusion.1.g_ref, f32[512,512]{1,0:T(8,128)} %copy-done.2, f32[574,512]{1,0:T(8,128)} %pad_maximum_fusion.x_ref, f32[63,512]{1,0:T(8,128)} %k_ref.3), custom_call_target="tpu_custom_call" | custom-call | tf_op jit(solution)/shard_map/pallas_call | solution.py:71
  174.8 6.2 %convolution_bitcast_fusion = f32[4096,256]{0,1:T(8,128)} fusion(bf16[512,4096]{1,0:T(8,128)(2,1)} %param.8, bf16[512,512]{1,0:T(8,128)(2,1)} %get-tuple-element.15, bf16[256,512]{1,0:T(8,128)(2,1)} %param.10), kind=kOutput, calls=%fused_computation.4 | convolution fusion | flops 1208090624 | bytes 9175040 | tf_op jit(solution)/shard_map/dot_general | solution.py:92
  181.0 2.2 fusion.19
  183.2 6.6 %concatenate.22 = f32[8,2,256,256]{2,1,0,3:T(2,128)} reshape(f32[4096,256]{0,1:T(8,128)} %convolution_bitcast_fusion) | data formatting | bytes 8388608 | tf_op jit(solution)/shard_map/concatenate | solution.py:178
  189.8 7.3 %copy.16 = f32[8,2,256,256]{3,2,0,1:T(8,128)} copy(f32[8,2,256,256]{2,1,0,3:T(2,128)} %concatenate.22) | data formatting | bytes 8388608 | tf_op jit(solution)/shard_map/concatenate | solution.py:178
  197.1 1.9 reshape.111
  199.9 6.2 %concatenate.23 = f32[1152,256]{1,0:T(8,128)} concatenate(f32[512,256]{1,0:T(8,128)} %reshape.111, f32[126,256]{1,0:T(8,128)S(1)} %reshape.112, f32[2,256]{1,0:T(2,128)S(1)} %reshape.113, f32[256,256]{1,0:T(8,128)S(1)} %copy-done.6, f32[256,256]{1,0:T(8,128)} %reshape.115), dimensions={0} | concatenate | bytes 2359296 | tf_op jit(solution)/shard_map/concatenate | solution.py:175
  206.1 3.5 %fusion.1 = f32[8,328,256]{2,1,0:T(8,128)} fusion(s32[]{:T(128)S(6)} %select_n.36, f32[8,2,256,256]{3,2,0,1:T(8,128)} %copy.16, f32[8,2,72,256]{3,2,1,0:T(8,128)} %bitcast.55), kind=kLoop, calls=%fused_computation.7 | loop fusion | flops 671744 | bytes 8060932 | tf_op jit(solution)/shard_map/jit(dynamic_index_in_dim)/squeeze | solution.py:108
  209.6 4.3 %all-to-all-start.4 = ((f32[16,32,512]{2,1,0:T(8,128)}), f32[16,32,512]{2,1,0:T(8,128)}, u32[]{:S(2)}, u32[]{:S(2)}) async-start(f32[16,32,512]{2,1,0:T(8,128)} %bitcast.58), calls=%async_computation.4 | async-start | bytes 2097152 | tf_op jit(solution)/shard_map/all_to_all | solution.py:98
  215.0 2.8 fusion.4
  218.3 1.8 copy.18
  220.1 21.1 %all-to-all-done.4 = f32[16,32,512]{2,1,0:T(8,128)} async-done(((f32[16,32,512]{2,1,0:T(8,128)}), f32[16,32,512]{2,1,0:T(8,128)}, u32[]{:S(2)}, u32[]{:S(2)}) %all-to-all-start.4) | async-done | bytes 1048608 | tf_op jit(solution)/shard_map/all_to_all | solution.py:98
  241.2 8.2 %all-to-all-start.6 = ((f32[16,164,256]{2,1,0:T(8,128)}), f32[16,164,256]{2,1,0:T(8,128)}, u32[]{:S(2)}, u32[]{:S(2)}) async-start(f32[16,164,256]{2,1,0:T(8,128)} %bitcast.54), calls=%async_computation.6 | async-start | bytes 5505024 | tf_op jit(solution)/shard_map/all_to_all | solution.py:114
  249.5 1.3 reduce_sum.76
  250.8 32.8 %all-to-all-done.6 = f32[16,164,256]{2,1,0:T(8,128)} async-done(((f32[16,164,256]{2,1,0:T(8,128)}), f32[16,164,256]{2,1,0:T(8,128)}, u32[]{:S(2)}, u32[]{:S(2)}) %all-to-all-start.6) | async-done | bytes 2687008 | tf_op jit(solution)/shard_map/all_to_all | solution.py:114
  284.5 3.6 %all-to-all-start.5 = ((bf16[16,32,512]{2,1,0:T(8,128)(2,1)}), bf16[16,32,512]{2,1,0:T(8,128)(2,1)S(1)}, u32[]{:S(2)}, u32[]{:S(2)}) async-start(bf16[16,32,512]{2,1,0:T(8,128)(2,1)} %broadcast_in_dim.10), calls=%async_computation.5 | async-start | bytes 1048576 | tf_op jit(solution)/shard_map/all_to_all | solution.py:125
  288.1 2.0 dynamic-slice_reduce_fusion
  292.1 13.0 %all-to-all-done.5 = bf16[16,32,512]{2,1,0:T(8,128)(2,1)S(1)} async-done(((bf16[16,32,512]{2,1,0:T(8,128)(2,1)}), bf16[16,32,512]{2,1,0:T(8,128)(2,1)S(1)}, u32[]{:S(2)}, u32[]{:S(2)}) %all-to-all-start.5) | async-done | bytes 524320 | tf_op jit(solution)/shard_map/all_to_all | solution.py:125
  306.2 7.4 %all-to-all-start.7 = ((f32[16,72,256]{2,1,0:T(8,128)}), f32[16,72,256]{2,1,0:T(8,128)}, u32[]{:S(2)}, u32[]{:S(2)}) async-start(f32[16,72,256]{2,1,0:T(8,128)} %broadcast_in_dim.11), calls=%async_computation.7 | async-start | bytes 2359296 | tf_op jit(solution)/shard_map/all_to_all | solution.py:125
  314.3 16.6 %all-to-all-done.7 = f32[16,72,256]{2,1,0:T(8,128)} async-done(((f32[16,72,256]{2,1,0:T(8,128)}), f32[16,72,256]{2,1,0:T(8,128)}, u32[]{:S(2)}, u32[]{:S(2)}) %all-to-all-start.7) | async-done | bytes 1179680 | tf_op jit(solution)/shard_map/all_to_all | solution.py:125
  333.6 1.8 fusion.13
  337.6 1.7 reshape.121
  (56 shorter events, 18.9 us)
Async XLA Ops:
  0.6 1.6 copy-start
  52.4 8.7 %copy-start.3 = (f32[512,512]{1,0:T(8,128)}, f32[512,512]{1,0:T(8,128)S(1)}, u32[]{:S(2)}) copy-start(f32[512,512]{1,0:T(8,128)S(1)} %fusion.17.mid_ref) | copy-start | bytes 3145732
  52.4 6.2 %collective-permute-start.1 = (f32[31,512]{1,0:T(8,128)S(1)}, f32[31,512]{1,0:T(8,128)S(1)}, u32[]{:S(2)}, u32[]{:S(2)}) collective-permute-start(f32[31,512]{1,0:T(8,128)S(1)} %get-tuple-element.30), channel_id=1, source_target_pairs={{1,0},{2,1},{3,2},{4,3},{5,4},{6,5},{7,6},{8,7},{9,8},{10,9},{11,1... | collective-permute-start | bytes 190472 | tf_op jit(solution)/shard_map/ppermute | solution.py:20
  56.5 3.4 %collective-permute-start = (f32[31,512]{1,0:T(8,128)S(1)}, f32[31,512]{1,0:T(8,128)S(1)}, u32[]{:S(2)}, u32[]{:S(2)}) collective-permute-start(f32[31,512]{1,0:T(8,128)S(1)} %get-tuple-element.29), channel_id=1, source_target_pairs={{0,1},{1,2},{2,3},{3,4},{4,5},{5,6},{6,7},{7,8},{8,9},{9,10},{10,1... | collective-permute-start | bytes 190472 | tf_op jit(solution)/shard_map/ppermute | solution.py:17
  61.1 8.2 %copy-start.8 = (bf16[512,128]{1,0:T(8,128)(2,1)S(1)}, bf16[512,128]{1,0:T(8,128)(2,1)}, u32[]{:S(2)}) copy-start(bf16[512,128]{1,0:T(8,128)(2,1)} %param.13) | copy-start | bytes 393220
  61.1 8.2 %copy-start.11 = (f32[512]{0:T(512)S(1)}, f32[512]{0:T(512)}, u32[]{:S(2)}) copy-start(f32[512]{0:T(512)} %param.12) | copy-start | bytes 6148
  70.9 0.7 copy-start.4
  72.9 0.7 copy-start.9
  106.4 10.6 %copy-start.1 = (f32[512,512]{1,0:T(8,128)S(1)}, f32[512,512]{1,0:T(8,128)}, u32[]{:S(2)}) copy-start(f32[512,512]{1,0:T(8,128)} %shard_map.135) | copy-start | bytes 3145732
  106.4 10.6 %copy-start.10 = (bf16[512,128]{1,0:T(8,128)(2,1)S(1)}, bf16[512,128]{1,0:T(8,128)(2,1)}, u32[]{:S(2)}) copy-start(bf16[512,128]{1,0:T(8,128)(2,1)} %copy-done.9) | copy-start | bytes 393220
  110.4 30.3 %all-to-all-start.3 = ((f32[16,32,512]{2,1,0:T(8,128)}), f32[16,32,512]{2,1,0:T(8,128)}, u32[]{:S(2)}, u32[]{:S(2)}) async-start(f32[16,32,512]{2,1,0:T(8,128)} %broadcast_in_dim.9), calls=%async_computation.3 | async-start | bytes 2097152 | tf_op jit(solution)/shard_map/all_to_all | solution.py:125
  140.7 15.9 %copy-start.5 = (f32[512,128]{1,0:T(8,128)S(1)}, f32[512,128]{1,0:T(8,128)}, u32[]{:S(2)}) copy-start(f32[512,128]{1,0:T(8,128)} %copy-done.4) | copy-start | bytes 786436
  140.7 15.9 %copy-start.7 = (bf16[512,512]{1,0:T(8,128)(2,1)S(1)}, bf16[512,512]{1,0:T(8,128)(2,1)}, u32[]{:S(2)}) copy-start(bf16[512,512]{1,0:T(8,128)(2,1)} %param.15) | copy-start | bytes 1572868
  144.1 1.0 copy-start.2
  145.8 15.3 %collective-permute-start.3 = (f32[31,512]{1,0:T(8,128)}, f32[31,512]{1,0:T(8,128)S(1)}, u32[]{:S(2)}, u32[]{:S(2)}) collective-permute-start(f32[31,512]{1,0:T(8,128)} %get-tuple-element.28), channel_id=1, source_target_pairs={{1,0},{2,1},{3,2},{4,3},{5,4},{6,5},{7,6},{8,7},{9,8},{10,9},{11,1... | collective-permute-start | bytes 190472 | tf_op jit(solution)/shard_map/ppermute | solution.py:20
  153.0 8.0 %collective-permute-start.2 = (f32[31,512]{1,0:T(8,128)}, f32[31,512]{1,0:T(8,128)S(1)}, u32[]{:S(2)}, u32[]{:S(2)}) collective-permute-start(f32[31,512]{1,0:T(8,128)} %get-tuple-element.27), channel_id=1, source_target_pairs={{0,1},{1,2},{2,3},{3,4},{4,5},{5,6},{6,7},{7,8},{8,9},{9,10},{10,1... | collective-permute-start | bytes 190472 | tf_op jit(solution)/shard_map/ppermute | solution.py:17
  189.8 10.1 %copy-start.6 = (f32[256,256]{1,0:T(8,128)S(1)}, f32[256,256]{1,0:T(8,128)}, u32[]{:S(2)}) copy-start(f32[256,256]{1,0:T(8,128)} %reshape.114) | copy-start | bytes 786436
  209.6 5.3 %collective-permute-start.4 = (f32[8,328,256]{2,1,0:T(8,128)}, f32[8,328,256]{2,1,0:T(8,128)}, u32[]{:S(2)}, u32[]{:S(2)}) collective-permute-start(f32[8,328,256]{2,1,0:T(8,128)} %fusion.1), channel_id=1, source_target_pairs={{0,1},{1,0},{2,3},{3,2},{4,5},{5,4},{6,7},{7,6},{8,9},{9,8},{10,11... | collective-permute-start | bytes 8060936 | tf_op jit(solution)/shard_map/ppermute | solution.py:109
  209.6 31.6 %all-to-all-start.4 = ((f32[16,32,512]{2,1,0:T(8,128)}), f32[16,32,512]{2,1,0:T(8,128)}, u32[]{:S(2)}, u32[]{:S(2)}) async-start(f32[16,32,512]{2,1,0:T(8,128)} %bitcast.58), calls=%async_computation.4 | async-start | bytes 2097152 | tf_op jit(solution)/shard_map/all_to_all | solution.py:98
  241.2 42.4 %all-to-all-start.6 = ((f32[16,164,256]{2,1,0:T(8,128)}), f32[16,164,256]{2,1,0:T(8,128)}, u32[]{:S(2)}, u32[]{:S(2)}) async-start(f32[16,164,256]{2,1,0:T(8,128)} %bitcast.54), calls=%async_computation.6 | async-start | bytes 5505024 | tf_op jit(solution)/shard_map/all_to_all | solution.py:114
  284.5 20.7 %all-to-all-start.5 = ((bf16[16,32,512]{2,1,0:T(8,128)(2,1)}), bf16[16,32,512]{2,1,0:T(8,128)(2,1)S(1)}, u32[]{:S(2)}, u32[]{:S(2)}) async-start(bf16[16,32,512]{2,1,0:T(8,128)(2,1)} %broadcast_in_dim.10), calls=%async_computation.5 | async-start | bytes 1048576 | tf_op jit(solution)/shard_map/all_to_all | solution.py:125
  290.0 2.1 collective-permute-start.5
  306.2 24.7 %all-to-all-start.7 = ((f32[16,72,256]{2,1,0:T(8,128)}), f32[16,72,256]{2,1,0:T(8,128)}, u32[]{:S(2)}, u32[]{:S(2)}) async-start(f32[16,72,256]{2,1,0:T(8,128)} %broadcast_in_dim.11), calls=%async_computation.7 | async-start | bytes 2359296 | tf_op jit(solution)/shard_map/all_to_all | solution.py:125

commit v9 on v7

--- a/solution.py
+++ b/solution.py
@@ -157,16 +157,18 @@
     dnormed_rows = scatter_sum(split_rows(partial_normed, nn), "neuron")
     dnormed = gather_all(dnormed_rows, "neuron").reshape(rows, -1)
     partial_mix, dnormed = lax.optimization_barrier((partial_mix, dnormed))
-    mix_rows = scatter_sum(split_rows(partial_mix, nn), "neuron")
-    mixed_rows = lax.dynamic_slice_in_dim(mixed, me * share, share, 0)
-    denoised_rows = (mixed_rows + mix_rows).astype(jnp.bfloat16)
-    denoised = gather_all(denoised_rows, "neuron").reshape(rows, -1)
+    mix_got = lax.all_to_all(split_rows(partial_mix, nn), "neuron", 0, 0, tiled=False)
     local_gain = jnp.sum(dnormed * mixed * scale, axis=0)
     dgained = dnormed * gain[None, :]
     inner = jnp.mean(dgained * mixed, axis=1, keepdims=True)
     dmixed = cotangent.astype(jnp.float32) + scale * dgained - mixed * scale**3 * inner
     padded_grad = with_halo(dmixed, (("tm", 0),), half)
     dlifted, local_kernel = bwd_conv(padded_grad, dmixed, padded, kernel)
+    mix_got, dlifted = lax.optimization_barrier((mix_got, dlifted))
+    mix_rows = jnp.sum(mix_got, axis=0)
+    mixed_rows = lax.dynamic_slice_in_dim(mixed, me * share, share, 0)
+    denoised_rows = (mixed_rows + mix_rows).astype(jnp.bfloat16)
+    denoised = gather_all(denoised_rows, "neuron").reshape(rows, -1)
     local_proj = over_time(latent, dlifted)
     dlatent = jnp.dot(dlifted, proj.T, preferred_element_type=jnp.float32).astype(jnp.bfloat16)
     local_readin = over_time(signal, dlatent)

time: 309 us -> 299 us (0.968)
  waiting for transfers between devices: 54.7 us -> 49.2 us
  local copies, waits for them, and re-layouts: 37.4 us -> 33 us
    all_to_all x1, waiting for transfers between devices: 8.05 us -> 2.44 us  [body(): lax.all_to_all(split_rows(partial_mix, nn), 'neuron', 0, 0, tiled=False)]
    unnamed x27 -> x31, local copies, waits for them, and re-layouts: 6.76 us -> 5.81 us
  transfers between devices with their start and end apart: 10 -> 10, of which waited for: 6 -> 7; matrix products, arithmetic and copies ran while one was open for 14% -> 12% of each run, Pallas kernels for 4% -> 4%
where the time goes in v9:
time: 299 us; the launch traced here: 297 us
  blocking collectives  120 us (40%)
  waiting for transfers between devices  49.2 us (16%)
  starting transfers between devices  37.2 us (12%)
  local copies, waits for them, and re-layouts  33 us (11%)
  matrix products  19.1 us (6%)
  other arithmetic  18.6 us (6%)
  Pallas kernels  18.2 us (6%)
    all_to_all x2, blocking collectives, scatter_sum(): got = lax.all_to_all(parts, axis, 0, 0, tiled=False)  61.2 us
    all_to_all x1, blocking collectives, pair_scatter_sum(): lax.all_to_all(slabs, axis, 0, 0, tiled=False)  42.3 us
    all_to_all x3, waiting for transfers between devices, gather_all(): return lax.all_to_all(spread, axis, 0, 0, tiled=False)  39.3 us
    all_to_all x1, blocking collectives, gather_all(): return lax.all_to_all(spread, axis, 0, 0, tiled=False)  16.8 us
    all_to_all x3, starting transfers between devices, gather_all(): return lax.all_to_all(spread, axis, 0, 0, tiled=False)  15.6 us
    pallas_call x1, Pallas kernels, bwd_conv(): pl.pallas_call(_bwd_conv_kernel, out_shape=(jax.ShapeDtypeStruct((rows, w...  11.4 us
    dot_general x4, matrix products, over_time(): lax.dot_general(left, right, (((0,), (0,)), ((), ())), preferred_element_...  8.9 us
    ppermute x2, starting transfers between devices, with_halo(): lax.ppermute(lax.slice_in_dim(block, 0, width, axis=dim), axis, backward)  8.39 us
  transfers between devices with their start and end apart: 10, of which 7 were waited for; matrix products, arithmetic and copies ran while one was open for 12% of the time, Pallas kernels for 4%

profile of v9, /device:TPU:1, one launch (start us, length us, event | category | flops | bytes accessed | tf_op | source)
XLA Modules:
  0.0 296.7 jit_solution(13584856844475492878)
XLA Ops:
  0.6 1.6 copy-done
  2.2 3.4 %fusion.9 = f32[512,256]{1,0:T(8,128)S(1)} fusion(bf16[512,4096]{1,0:T(8,128)(2,1)} %param.8, bf16[4096,256]{1,0:T(8,128)(2,1)S(1)} %copy-done), kind=kOutput, calls=%fused_computation.35 | convolution fusion | flops 1073741824 | bytes 6815744 | tf_op jit(solution)/shard_map/dot_general | solution.py:140
  5.7 28.6 %all_to_all.40 = f32[16,32,256]{2,1,0:T(8,128)S(1)} all-to-all(f32[16,32,256]{2,1,0:T(8,128)S(1)} %bitcast.56), channel_id=1, replica_groups=mesh['neuron'=16,'tm'=16] {'neuron'}, dimensions={0} | all-to-all | bytes 1048576 | tf_op jit(solution)/shard_map/all_to_all | solution.py:98
  34.3 16.8 %all_to_all.41 = bf16[16,32,256]{2,1,0:T(8,128)(2,1)S(1)} all-to-all(bf16[16,32,256]{2,1,0:T(8,128)(2,1)S(1)} %broadcast_in_dim.8), channel_id=1, replica_groups=mesh['neuron'=16,'tm'=16] {'neuron'}, dimensions={0} | all-to-all | bytes 524288 | tf_op jit(solution)/shard_map/all_to_all | solution.py:125
  51.1 1.2 fusion.10.mid_ref
  52.4 4.0 %collective-permute-start.1 = (f32[31,512]{1,0:T(8,128)S(1)}, f32[31,512]{1,0:T(8,128)S(1)}, u32[]{:S(2)}, u32[]{:S(2)}) collective-permute-start(f32[31,512]{1,0:T(8,128)S(1)} %get-tuple-element.34), channel_id=1, source_target_pairs={{1,0},{2,1},{3,2},{4,3},{5,4},{6,5},{7,6},{8,7},{9,8},{10,9},{11,1... | collective-permute-start | bytes 190472 | tf_op jit(solution)/shard_map/ppermute | solution.py:20
  56.5 2.1 collective-permute-start
  58.6 1.3 collective-permute-done
  59.9 1.2 pad_maximum_fusion.1.x_ref
  61.1 6.8 %shard_map.135 = f32[512,512]{1,0:T(8,128)} custom-call(f32[574,512]{1,0:T(8,128)} %pad_maximum_fusion.1.x_ref, f32[512,512]{1,0:T(8,128)} %copy-done.3, f32[63,512]{1,0:T(8,128)} %k_ref.3), custom_call_target="tpu_custom_call" | custom-call | tf_op jit(solution)/shard_map/pallas_call | solution.py:38
  67.9 1.4 multiply_reduce_fusion.2
  69.3 1.6 fusion.3
  71.6 1.4 fusion.1
  73.6 32.6 %all_to_all.42 = f32[16,32,512]{2,1,0:T(8,128)S(1)} all-to-all(f32[16,32,512]{2,1,0:T(8,128)S(1)} %bitcast.52), channel_id=1, replica_groups=mesh['neuron'=16,'tm'=16] {'neuron'}, dimensions={0} | all-to-all | bytes 2097152 | tf_op jit(solution)/shard_map/all_to_all | solution.py:98
  106.3 1.1 broadcast_in_dim.9
  107.4 4.5 %all-to-all-start.3 = ((f32[16,32,512]{2,1,0:T(8,128)}), f32[16,32,512]{2,1,0:T(8,128)}, u32[]{:S(2)}, u32[]{:S(2)}) async-start(f32[16,32,512]{2,1,0:T(8,128)} %broadcast_in_dim.9), calls=%async_computation.3 | async-start | bytes 2097152 | tf_op jit(solution)/shard_map/all_to_all | solution.py:125
  111.9 2.3 fusion.5
  114.2 23.7 %all-to-all-done.3 = f32[16,32,512]{2,1,0:T(8,128)} async-done(((f32[16,32,512]{2,1,0:T(8,128)}), f32[16,32,512]{2,1,0:T(8,128)}, u32[]{:S(2)}, u32[]{:S(2)}) %all-to-all-start.3) | async-done | bytes 1048608 | tf_op jit(solution)/shard_map/all_to_all | solution.py:125
  137.9 7.2 %all-to-all-start.4 = ((f32[16,32,512]{2,1,0:T(8,128)}), f32[16,32,512]{2,1,0:T(8,128)}, u32[]{:S(2)}, u32[]{:S(2)}) async-start(f32[16,32,512]{2,1,0:T(8,128)} %bitcast.53), calls=%async_computation.4 | async-start | bytes 2097152 | tf_op jit(solution)/shard_map/all_to_all | solution.py:160
  145.1 1.6 multiply_reduce_fusion
  146.7 1.7 multiply_subtract_fusion.d_ref
  148.5 4.3 %collective-permute-start.3 = (f32[31,512]{1,0:T(8,128)S(1)}, f32[31,512]{1,0:T(8,128)S(1)}, u32[]{:S(2)}, u32[]{:S(2)}) collective-permute-start(f32[31,512]{1,0:T(8,128)S(1)} %get-tuple-element.32), channel_id=1, source_target_pairs={{1,0},{2,1},{3,2},{4,3},{5,4},{6,5},{7,6},{8,7},{9,8},{10,9},{11,1... | collective-permute-start | bytes 190472 | tf_op jit(solution)/shard_map/ppermute | solution.py:20
  152.9 1.9 collective-permute-start.2
  154.8 1.1 fusion.2
  156.1 1.2 pad_maximum_fusion.2.g_ref
  157.3 11.4 %shard_map.136 = (bf16[512,512]{1,0:T(8,128)(2,1)}, f32[63,512]{1,0:T(8,128)}) custom-call(f32[574,512]{1,0:T(8,128)} %pad_maximum_fusion.2.g_ref, f32[512,512]{1,0:T(8,128)} %copy-done.2, f32[574,512]{1,0:T(8,128)} %pad_maximum_fusion.1.x_ref, f32[63,512]{1,0:T(8,128)} %k_ref.3), custom_call_target="tpu_custom_call" | custom-call | tf_op jit(solution)/shard_map/pallas_call | solution.py:71
  168.7 2.4 all-to-all-done.4
  171.1 1.3 reduce_sum.76
  173.3 7.2 %all-to-all-start.5 = ((bf16[16,32,512]{2,1,0:T(8,128)(2,1)}), bf16[16,32,512]{2,1,0:T(8,128)(2,1)}, u32[]{:S(2)}, u32[]{:S(2)}) async-start(bf16[16,32,512]{2,1,0:T(8,128)(2,1)} %broadcast_in_dim.10), calls=%async_computation.5 | async-start | bytes 1048576 | tf_op jit(solution)/shard_map/all_to_all | solution.py:125
  180.6 1.4 fusion.4
  185.4 6.0 %convolution_bitcast_fusion = f32[4096,256]{0,1:T(8,128)} fusion(bf16[512,4096]{1,0:T(8,128)(2,1)} %param.8, bf16[512,512]{1,0:T(8,128)(2,1)S(1)} %copy-done.4, bf16[256,512]{1,0:T(8,128)(2,1)} %param.10), kind=kOutput, calls=%fused_computation | convolution fusion | flops 1208090624 | bytes 9175040 | tf_op jit(solution)/shard_map/dot_general | solution.py:92
  191.4 5.7 %copy.18 = f32[4096,256]{1,0:T(8,128)} copy(f32[4096,256]{0,1:T(8,128)} %convolution_bitcast_fusion) | data formatting | bytes 8388608 | tf_op jit(solution)/shard_map/reshape | solution.py:178
  197.2 3.0 %concatenate.17 = f32[1152,256]{1,0:T(8,128)S(1)} concatenate(f32[512,256]{1,0:T(8,128)} %reshape.114, f32[126,256]{1,0:T(8,128)} %reshape.115, f32[2,256]{1,0:T(2,128)S(1)} %reshape.116, f32[256,256]{1,0:T(8,128)S(1)} %copy-done.7, f32[256,256]{1,0:T(8,128)} %reshape.118), dimensions={0} | concatenate | bytes 2359296 | tf_op jit(solution)/shard_map/concatenate | solution.py:177
  200.1 5.1 %pad_maximum_fusion = f32[16,328,256]{2,1,0:T(8,128)} fusion(f32[16,72,256]{2,1,0:T(8,128)S(1)} %bitcast.51, f32[16,256,256]{2,1,0:T(8,128)} %bitcast.44), kind=kLoop, calls=%fused_computation.1 | loop fusion | flops 1343488 | bytes 10747904 | tf_op jit(solution)/shard_map/concatenate | solution.py:180
  205.2 3.5 %dynamic-slice_bitcast_fusion = f32[8,328,256]{2,1,0:T(8,128)} fusion(f32[8,2,328,256]{3,2,1,0:T(8,128)} %bitcast.42, s32[]{:T(128)S(6)} %select_n.36), kind=kLoop, calls=%fused_computation.4 | loop fusion | bytes 5373956 | tf_op jit(solution)/shard_map/jit(dynamic_index_in_dim)/squeeze | solution.py:108
  208.7 1.3 collective-permute-start.4
  210.0 5.0 %collective-permute-done.4 = f32[8,328,256]{2,1,0:T(8,128)} collective-permute-done((f32[8,328,256]{2,1,0:T(8,128)}, f32[8,328,256]{2,1,0:T(8,128)}, u32[]{:S(2)}, u32[]{:S(2)}) %collective-permute-start.4) | collective-permute-done | bytes 2687008 | tf_op jit(solution)/shard_map/ppermute | solution.py:109
  215.0 2.9 bitcast_add_fusion
  218.7 42.3 %all_to_all.43 = f32[16,164,256]{2,1,0:T(8,128)S(1)} all-to-all(f32[16,164,256]{2,1,0:T(8,128)S(1)} %bitcast.46), channel_id=1, replica_groups=mesh['neuron'=16,'tm'=16] {'tm'}, dimensions={0} | all-to-all | bytes 5373952 | tf_op jit(solution)/shard_map/all_to_all | solution.py:114
  262.1 1.0 collective-permute-done.5
  263.8 1.1 broadcast_in_dim.11
  264.9 3.9 %all-to-all-start.7 = ((f32[16,72,256]{2,1,0:T(8,128)}), f32[16,72,256]{2,1,0:T(8,128)S(1)}, u32[]{:S(2)}, u32[]{:S(2)}) async-start(f32[16,72,256]{2,1,0:T(8,128)} %broadcast_in_dim.11), calls=%async_computation.7 | async-start | bytes 2359296 | tf_op jit(solution)/shard_map/all_to_all | solution.py:125
  268.7 1.6 pad_maximum_fusion.3
  270.4 15.6 %all-to-all-done.7 = f32[16,72,256]{2,1,0:T(8,128)S(1)} async-done(((f32[16,72,256]{2,1,0:T(8,128)}), f32[16,72,256]{2,1,0:T(8,128)S(1)}, u32[]{:S(2)}, u32[]{:S(2)}) %all-to-all-start.7) | async-done | bytes 1179680 | tf_op jit(solution)/shard_map/all_to_all | solution.py:125
  288.2 2.0 reshape.123
  290.2 1.6 reshape.124
  292.3 1.7 reshape.126
  294.8 1.9 copy.21
  (59 shorter events, 12.1 us)
Async XLA Ops:
  0.6 1.6 copy-start
  52.4 8.7 %copy-start.3 = (f32[512,512]{1,0:T(8,128)}, f32[512,512]{1,0:T(8,128)S(1)}, u32[]{:S(2)}) copy-start(f32[512,512]{1,0:T(8,128)S(1)} %fusion.10.mid_ref) | copy-start | bytes 3145732
  52.4 6.2 %collective-permute-start.1 = (f32[31,512]{1,0:T(8,128)S(1)}, f32[31,512]{1,0:T(8,128)S(1)}, u32[]{:S(2)}, u32[]{:S(2)}) collective-permute-start(f32[31,512]{1,0:T(8,128)S(1)} %get-tuple-element.34), channel_id=1, source_target_pairs={{1,0},{2,1},{3,2},{4,3},{5,4},{6,5},{7,6},{8,7},{9,8},{10,9},{11,1... | collective-permute-start | bytes 190472 | tf_op jit(solution)/shard_map/ppermute | solution.py:20
  56.5 3.4 %collective-permute-start = (f32[31,512]{1,0:T(8,128)S(1)}, f32[31,512]{1,0:T(8,128)S(1)}, u32[]{:S(2)}, u32[]{:S(2)}) collective-permute-start(f32[31,512]{1,0:T(8,128)S(1)} %get-tuple-element.33), channel_id=1, source_target_pairs={{0,1},{1,2},{2,3},{3,4},{4,5},{5,6},{6,7},{7,8},{8,9},{9,10},{10,1... | collective-permute-start | bytes 190472 | tf_op jit(solution)/shard_map/ppermute | solution.py:17
  61.1 8.2 %copy-start.8 = (bf16[512,128]{1,0:T(8,128)(2,1)S(1)}, bf16[512,128]{1,0:T(8,128)(2,1)}, u32[]{:S(2)}) copy-start(bf16[512,128]{1,0:T(8,128)(2,1)} %param.13) | copy-start | bytes 393220
  61.1 8.2 %copy-start.13 = (f32[512]{0:T(512)S(1)}, f32[512]{0:T(512)}, u32[]{:S(2)}) copy-start(f32[512]{0:T(512)} %param.12) | copy-start | bytes 6148
  70.9 0.7 copy-start.6
  72.9 0.7 copy-start.9
  107.4 37.7 %copy-start.1 = (f32[512,512]{1,0:T(8,128)S(1)}, f32[512,512]{1,0:T(8,128)}, u32[]{:S(2)}) copy-start(f32[512,512]{1,0:T(8,128)} %shard_map.135) | copy-start | bytes 3145732
  107.4 30.5 %all-to-all-start.3 = ((f32[16,32,512]{2,1,0:T(8,128)}), f32[16,32,512]{2,1,0:T(8,128)}, u32[]{:S(2)}, u32[]{:S(2)}) async-start(f32[16,32,512]{2,1,0:T(8,128)} %broadcast_in_dim.9), calls=%async_computation.3 | async-start | bytes 2097152 | tf_op jit(solution)/shard_map/all_to_all | solution.py:125
  137.9 33.2 %all-to-all-start.4 = ((f32[16,32,512]{2,1,0:T(8,128)}), f32[16,32,512]{2,1,0:T(8,128)}, u32[]{:S(2)}, u32[]{:S(2)}) async-start(f32[16,32,512]{2,1,0:T(8,128)} %bitcast.53), calls=%async_computation.4 | async-start | bytes 2097152 | tf_op jit(solution)/shard_map/all_to_all | solution.py:160
  145.1 9.7 %copy-start.10 = (bf16[512,128]{1,0:T(8,128)(2,1)S(1)}, bf16[512,128]{1,0:T(8,128)(2,1)}, u32[]{:S(2)}) copy-start(bf16[512,128]{1,0:T(8,128)(2,1)} %copy-done.9) | copy-start | bytes 393220
  148.5 7.6 %copy-start.2 = (f32[512,512]{1,0:T(8,128)}, f32[512,512]{1,0:T(8,128)S(1)}, u32[]{:S(2)}) copy-start(f32[512,512]{1,0:T(8,128)S(1)} %multiply_subtract_fusion.d_ref) | copy-start | bytes 3145732
  148.5 7.4 %collective-permute-start.3 = (f32[31,512]{1,0:T(8,128)S(1)}, f32[31,512]{1,0:T(8,128)S(1)}, u32[]{:S(2)}, u32[]{:S(2)}) collective-permute-start(f32[31,512]{1,0:T(8,128)S(1)} %get-tuple-element.32), channel_id=1, source_target_pairs={{1,0},{2,1},{3,2},{4,3},{5,4},{6,5},{7,6},{8,7},{9,8},{10,9},{11,1... | collective-permute-start | bytes 190472 | tf_op jit(solution)/shard_map/ppermute | solution.py:20
  152.9 3.2 %collective-permute-start.2 = (f32[31,512]{1,0:T(8,128)S(1)}, f32[31,512]{1,0:T(8,128)S(1)}, u32[]{:S(2)}, u32[]{:S(2)}) collective-permute-start(f32[31,512]{1,0:T(8,128)S(1)} %get-tuple-element.31), channel_id=1, source_target_pairs={{0,1},{1,2},{2,3},{3,4},{4,5},{5,6},{6,7},{7,8},{8,9},{9,10},{10,1... | collective-permute-start | bytes 190472 | tf_op jit(solution)/shard_map/ppermute | solution.py:17
  172.4 9.5 %copy-start.5 = (f32[512,128]{1,0:T(8,128)S(1)}, f32[512,128]{1,0:T(8,128)}, u32[]{:S(2)}) copy-start(f32[512,128]{1,0:T(8,128)} %fusion.2) | copy-start | bytes 786436
  172.4 11.1 %copy-start.12 = (f32[63,512]{1,0:T(8,128)S(1)}, f32[63,512]{1,0:T(8,128)}, u32[]{:S(2)}) copy-start(f32[63,512]{1,0:T(8,128)} %get-tuple-element.20) | copy-start | bytes 387076
  172.4 11.7 %copy-start.4 = (bf16[512,512]{1,0:T(8,128)(2,1)S(1)}, bf16[512,512]{1,0:T(8,128)(2,1)}, u32[]{:S(2)}) copy-start(bf16[512,512]{1,0:T(8,128)(2,1)} %get-tuple-element.19) | copy-start | bytes 1572868
  173.3 31.9 %all-to-all-start.5 = ((bf16[16,32,512]{2,1,0:T(8,128)(2,1)}), bf16[16,32,512]{2,1,0:T(8,128)(2,1)}, u32[]{:S(2)}, u32[]{:S(2)}) async-start(bf16[16,32,512]{2,1,0:T(8,128)(2,1)} %broadcast_in_dim.10), calls=%async_computation.5 | async-start | bytes 1048576 | tf_op jit(solution)/shard_map/all_to_all | solution.py:125
  191.4 5.7 %copy-start.7 = (f32[256,256]{1,0:T(8,128)S(1)}, f32[256,256]{1,0:T(8,128)}, u32[]{:S(2)}) copy-start(f32[256,256]{1,0:T(8,128)} %reshape.117) | copy-start | bytes 786436
  208.7 6.3 %collective-permute-start.4 = (f32[8,328,256]{2,1,0:T(8,128)}, f32[8,328,256]{2,1,0:T(8,128)}, u32[]{:S(2)}, u32[]{:S(2)}) collective-permute-start(f32[8,328,256]{2,1,0:T(8,128)} %dynamic-slice_bitcast_fusion), channel_id=1, source_target_pairs={{0,1},{1,0},{2,3},{3,2},{4,5},{5,4},{6,7},{7,6},{8,9},{9,8},{10,11... | collective-permute-start | bytes 8060936 | tf_op jit(solution)/shard_map/ppermute | solution.py:109
  261.3 1.8 collective-permute-start.5
  263.1 0.7 copy-start.11
  264.9 21.1 %all-to-all-start.7 = ((f32[16,72,256]{2,1,0:T(8,128)}), f32[16,72,256]{2,1,0:T(8,128)S(1)}, u32[]{:S(2)}, u32[]{:S(2)}) async-start(f32[16,72,256]{2,1,0:T(8,128)} %broadcast_in_dim.11), calls=%async_computation.7 | async-start | bytes 2359296 | tf_op jit(solution)/shard_map/all_to_all | solution.py:125

commit v10 on v9

--- a/solution.py
+++ b/solution.py
@@ -164,14 +164,14 @@
     dmixed = cotangent.astype(jnp.float32) + scale * dgained - mixed * scale**3 * inner
     padded_grad = with_halo(dmixed, (("tm", 0),), half)
     dlifted, local_kernel = bwd_conv(padded_grad, dmixed, padded, kernel)
-    mix_got, dlifted = lax.optimization_barrier((mix_got, dlifted))
+    local_proj = over_time(latent, dlifted)
+    dlatent = jnp.dot(dlifted, proj.T, preferred_element_type=jnp.float32).astype(jnp.bfloat16)
+    local_readin = over_time(signal, dlatent)
+    mix_got, local_readin = lax.optimization_barrier((mix_got, local_readin))
     mix_rows = jnp.sum(mix_got, axis=0)
     mixed_rows = lax.dynamic_slice_in_dim(mixed, me * share, share, 0)
     denoised_rows = (mixed_rows + mix_rows).astype(jnp.bfloat16)
     denoised = gather_all(denoised_rows, "neuron").reshape(rows, -1)
-    local_proj = over_time(latent, dlifted)
-    dlatent = jnp.dot(dlifted, proj.T, preferred_element_type=jnp.float32).astype(jnp.bfloat16)
-    local_readin = over_time(signal, dlatent)
     grads = (local_proj, local_kernel, local_gain, local_w_one, local_w_two)
     width = local_readin.shape[1]
     small = jnp.concatenate([g.reshape(-1, width) for g in grads]).reshape(nt, -1, width)

time: 299 us -> 304 us (1.017)
    all_to_all x3, starting transfers between devices: 15.6 us -> 19.7 us  [gather_all(): return lax.all_to_all(spread, axis, 0, 0, tiled=False)]
    unnamed x31 -> x27, local copies, waits for them, and re-layouts: 5.81 us -> 6.76 us
where the time goes in v10:
time: 304 us; the launch traced here: 303 us
  blocking collectives  119 us (39%)
  waiting for transfers between devices  48.7 us (16%)
  starting transfers between devices  40.1 us (13%)
  local copies, waits for them, and re-layouts  35 us (12%)
  other arithmetic  21.3 us (7%)
  matrix products  19.2 us (6%)
  Pallas kernels  18.2 us (6%)
    all_to_all x2, blocking collectives, scatter_sum(): got = lax.all_to_all(parts, axis, 0, 0, tiled=False)  61.2 us
    all_to_all x1, blocking collectives, pair_scatter_sum(): lax.all_to_all(slabs, axis, 0, 0, tiled=False)  41.2 us
    all_to_all x3, waiting for transfers between devices, gather_all(): return lax.all_to_all(spread, axis, 0, 0, tiled=False)  39.3 us
    all_to_all x3, starting transfers between devices, gather_all(): return lax.all_to_all(spread, axis, 0, 0, tiled=False)  19.7 us
    all_to_all x1, blocking collectives, gather_all(): return lax.all_to_all(spread, axis, 0, 0, tiled=False)  16.8 us
    pallas_call x1, Pallas kernels, bwd_conv(): pl.pallas_call(_bwd_conv_kernel, out_shape=(jax.ShapeDtypeStruct((rows, w...  11.4 us
    dot_general x4, matrix products, over_time(): lax.dot_general(left, right, (((0,), (0,)), ((), ())), preferred_element_...  9.05 us
    ppermute x2, starting transfers between devices, with_halo(): lax.ppermute(lax.slice_in_dim(block, 0, width, axis=dim), axis, backward)  8.39 us
  transfers between devices with their start and end apart: 10, of which 7 were waited for; matrix products, arithmetic and copies ran while one was open for 12% of the time, Pallas kernels for 4%

profile of v10, /device:TPU:1, one launch (start us, length us, event | category | flops | bytes accessed | tf_op | source)
XLA Modules:
  0.0 302.6 jit_solution(18132662563920715598)
XLA Ops:
  0.6 1.6 copy-done
  2.2 3.4 %fusion.9 = f32[512,256]{1,0:T(8,128)S(1)} fusion(bf16[512,4096]{1,0:T(8,128)(2,1)} %param.8, bf16[4096,256]{1,0:T(8,128)(2,1)S(1)} %copy-done), kind=kOutput, calls=%fused_computation.35 | convolution fusion | flops 1073741824 | bytes 6815744 | tf_op jit(solution)/shard_map/dot_general | solution.py:140
  5.7 28.6 %all_to_all.40 = f32[16,32,256]{2,1,0:T(8,128)S(1)} all-to-all(f32[16,32,256]{2,1,0:T(8,128)S(1)} %bitcast.56), channel_id=1, replica_groups=mesh['neuron'=16,'tm'=16] {'neuron'}, dimensions={0} | all-to-all | bytes 1048576 | tf_op jit(solution)/shard_map/all_to_all | solution.py:98
  34.3 16.8 %all_to_all.41 = bf16[16,32,256]{2,1,0:T(8,128)(2,1)S(1)} all-to-all(bf16[16,32,256]{2,1,0:T(8,128)(2,1)S(1)} %broadcast_in_dim.8), channel_id=1, replica_groups=mesh['neuron'=16,'tm'=16] {'neuron'}, dimensions={0} | all-to-all | bytes 524288 | tf_op jit(solution)/shard_map/all_to_all | solution.py:125
  51.1 1.2 fusion.10.mid_ref
  52.4 4.0 %collective-permute-start.1 = (f32[31,512]{1,0:T(8,128)S(1)}, f32[31,512]{1,0:T(8,128)S(1)}, u32[]{:S(2)}, u32[]{:S(2)}) collective-permute-start(f32[31,512]{1,0:T(8,128)S(1)} %get-tuple-element.34), channel_id=1, source_target_pairs={{1,0},{2,1},{3,2},{4,3},{5,4},{6,5},{7,6},{8,7},{9,8},{10,9},{11,1... | collective-permute-start | bytes 190472 | tf_op jit(solution)/shard_map/ppermute | solution.py:20
  56.5 2.1 collective-permute-start
  58.6 1.3 collective-permute-done
  59.9 1.2 pad_maximum_fusion.1.x_ref
  61.0 6.8 %shard_map.135 = f32[512,512]{1,0:T(8,128)} custom-call(f32[574,512]{1,0:T(8,128)} %pad_maximum_fusion.1.x_ref, f32[512,512]{1,0:T(8,128)} %copy-done.3, f32[63,512]{1,0:T(8,128)} %k_ref.3), custom_call_target="tpu_custom_call" | custom-call | tf_op jit(solution)/shard_map/pallas_call | solution.py:38
  67.9 1.4 multiply_reduce_fusion.2
  69.3 1.6 fusion.3
  71.6 1.4 fusion.1
  73.6 32.6 %all_to_all.42 = f32[16,32,512]{2,1,0:T(8,128)S(1)} all-to-all(f32[16,32,512]{2,1,0:T(8,128)S(1)} %bitcast.52), channel_id=1, replica_groups=mesh['neuron'=16,'tm'=16] {'neuron'}, dimensions={0} | all-to-all | bytes 2097152 | tf_op jit(solution)/shard_map/all_to_all | solution.py:98
  106.3 1.1 broadcast_in_dim.9
  107.4 4.5 %all-to-all-start.3 = ((f32[16,32,512]{2,1,0:T(8,128)}), f32[16,32,512]{2,1,0:T(8,128)}, u32[]{:S(2)}, u32[]{:S(2)}) async-start(f32[16,32,512]{2,1,0:T(8,128)} %broadcast_in_dim.9), calls=%async_computation.3 | async-start | bytes 2097152 | tf_op jit(solution)/shard_map/all_to_all | solution.py:125
  111.9 2.2 fusion.5
  114.2 23.7 %all-to-all-done.3 = f32[16,32,512]{2,1,0:T(8,128)} async-done(((f32[16,32,512]{2,1,0:T(8,128)}), f32[16,32,512]{2,1,0:T(8,128)}, u32[]{:S(2)}, u32[]{:S(2)}) %all-to-all-start.3) | async-done | bytes 1048608 | tf_op jit(solution)/shard_map/all_to_all | solution.py:125
  137.9 7.2 %all-to-all-start.4 = ((f32[16,32,512]{2,1,0:T(8,128)}), f32[16,32,512]{2,1,0:T(8,128)}, u32[]{:S(2)}, u32[]{:S(2)}) async-start(f32[16,32,512]{2,1,0:T(8,128)} %bitcast.53), calls=%async_computation.4 | async-start | bytes 2097152 | tf_op jit(solution)/shard_map/all_to_all | solution.py:160
  145.1 1.6 multiply_reduce_fusion
  146.7 1.7 multiply_subtract_fusion.d_ref
  150.1 4.3 %collective-permute-start.3 = (f32[31,512]{1,0:T(8,128)}, f32[31,512]{1,0:T(8,128)S(1)}, u32[]{:S(2)}, u32[]{:S(2)}) collective-permute-start(f32[31,512]{1,0:T(8,128)} %get-tuple-element.32), channel_id=1, source_target_pairs={{1,0},{2,1},{3,2},{4,3},{5,4},{6,5},{7,6},{8,7},{9,8},{10,9},{11,1... | collective-permute-start | bytes 190472 | tf_op jit(solution)/shard_map/ppermute | solution.py:20
  154.4 1.9 collective-permute-start.2
  156.9 1.2 collective-permute-done.2
  158.0 2.4 pad_maximum_fusion.2.g_ref
  160.4 11.4 %shard_map.136 = (bf16[512,512]{1,0:T(8,128)(2,1)}, f32[63,512]{1,0:T(8,128)}) custom-call(f32[574,512]{1,0:T(8,128)} %pad_maximum_fusion.2.g_ref, f32[512,512]{1,0:T(8,128)} %copy-done.2, f32[574,512]{1,0:T(8,128)} %pad_maximum_fusion.1.x_ref, f32[63,512]{1,0:T(8,128)} %k_ref.3), custom_call_target="tpu_custom_call" | custom-call | tf_op jit(solution)/shard_map/pallas_call | solution.py:71
  171.8 6.2 %convolution_bitcast_fusion = f32[4096,256]{0,1:T(8,128)} fusion(bf16[512,4096]{1,0:T(8,128)(2,1)} %param.8, bf16[512,512]{1,0:T(8,128)(2,1)} %get-tuple-element.17, bf16[256,512]{1,0:T(8,128)(2,1)} %param.10), kind=kOutput, calls=%fused_computation | convolution fusion | flops 1208090624 | bytes 9175040 | tf_op jit(solution)/shard_map/dot_general | solution.py:92
  178.0 2.0 reduce_sum.76
  181.7 11.4 %all-to-all-start.5 = ((bf16[16,32,512]{2,1,0:T(8,128)(2,1)}), bf16[16,32,512]{2,1,0:T(8,128)(2,1)}, u32[]{:S(2)}, u32[]{:S(2)}) async-start(bf16[16,32,512]{2,1,0:T(8,128)(2,1)} %broadcast_in_dim.10), calls=%async_computation.5 | async-start | bytes 1048576 | tf_op jit(solution)/shard_map/all_to_all | solution.py:125
  193.1 1.1 fusion.2
  194.2 1.8 reshape.117
  196.0 1.4 fusion.4
  199.4 3.0 %concatenate.17 = f32[1152,256]{1,0:T(8,128)S(1)} concatenate(f32[512,256]{1,0:T(8,128)} %reshape.114, f32[126,256]{1,0:T(8,128)S(1)} %reshape.115, f32[2,256]{1,0:T(2,128)S(1)} %reshape.116, f32[256,256]{1,0:T(8,128)} %reshape.117, f32[256,256]{1,0:T(8,128)} %reshape.118), dimensions={0} | concatenate | bytes 2359296 | tf_op jit(solution)/shard_map/concatenate | solution.py:177
  202.4 5.7 %copy.18 = f32[4096,256]{1,0:T(8,128)} copy(f32[4096,256]{0,1:T(8,128)} %convolution_bitcast_fusion) | data formatting | bytes 8388608 | tf_op jit(solution)/shard_map/reshape | solution.py:178
  208.1 5.0 %pad_maximum_fusion = f32[16,328,256]{2,1,0:T(8,128)} fusion(f32[16,72,256]{2,1,0:T(8,128)S(1)} %bitcast.51, f32[16,256,256]{2,1,0:T(8,128)} %bitcast.44), kind=kLoop, calls=%fused_computation.1 | loop fusion | flops 1343488 | bytes 10747904 | tf_op jit(solution)/shard_map/concatenate | solution.py:180
  213.2 3.6 %dynamic-slice_bitcast_fusion = f32[8,328,256]{2,1,0:T(8,128)} fusion(f32[8,2,328,256]{3,2,1,0:T(8,128)} %bitcast.42, s32[]{:T(128)S(6)} %select_n.36), kind=kLoop, calls=%fused_computation.4 | loop fusion | bytes 5373956 | tf_op jit(solution)/shard_map/jit(dynamic_index_in_dim)/squeeze | solution.py:108
  216.7 5.3 %collective-permute-done.4 = f32[8,328,256]{2,1,0:T(8,128)} collective-permute-done((f32[8,328,256]{2,1,0:T(8,128)}, f32[8,328,256]{2,1,0:T(8,128)}, u32[]{:S(2)}, u32[]{:S(2)}) %collective-permute-start.4) | collective-permute-done | bytes 2687008 | tf_op jit(solution)/shard_map/ppermute | solution.py:109
  222.0 2.9 bitcast_add_fusion
  225.8 41.2 %all_to_all.43 = f32[16,164,256]{2,1,0:T(8,128)S(1)} all-to-all(f32[16,164,256]{2,1,0:T(8,128)S(1)} %bitcast.46), channel_id=1, replica_groups=mesh['neuron'=16,'tm'=16] {'tm'}, dimensions={0} | all-to-all | bytes 5373952 | tf_op jit(solution)/shard_map/all_to_all | solution.py:114
  268.0 1.0 collective-permute-done.5
  269.7 1.1 broadcast_in_dim.11
  270.8 3.9 %all-to-all-start.7 = ((f32[16,72,256]{2,1,0:T(8,128)}), f32[16,72,256]{2,1,0:T(8,128)S(1)}, u32[]{:S(2)}, u32[]{:S(2)}) async-start(f32[16,72,256]{2,1,0:T(8,128)} %broadcast_in_dim.11), calls=%async_computation.7 | async-start | bytes 2359296 | tf_op jit(solution)/shard_map/all_to_all | solution.py:125
  274.7 1.6 pad_maximum_fusion.3
  276.3 15.6 %all-to-all-done.7 = f32[16,72,256]{2,1,0:T(8,128)S(1)} async-done(((f32[16,72,256]{2,1,0:T(8,128)}), f32[16,72,256]{2,1,0:T(8,128)S(1)}, u32[]{:S(2)}, u32[]{:S(2)}) %all-to-all-start.7) | async-done | bytes 1179680 | tf_op jit(solution)/shard_map/all_to_all | solution.py:125
  294.1 2.0 reshape.123
  296.1 1.6 reshape.124
  298.3 1.7 reshape.126
  300.7 1.9 copy.21
  (55 shorter events, 13.4 us)
Async XLA Ops:
  0.6 1.6 copy-start
  52.4 8.7 %copy-start.3 = (f32[512,512]{1,0:T(8,128)}, f32[512,512]{1,0:T(8,128)S(1)}, u32[]{:S(2)}) copy-start(f32[512,512]{1,0:T(8,128)S(1)} %fusion.10.mid_ref) | copy-start | bytes 3145732
  52.4 6.2 %collective-permute-start.1 = (f32[31,512]{1,0:T(8,128)S(1)}, f32[31,512]{1,0:T(8,128)S(1)}, u32[]{:S(2)}, u32[]{:S(2)}) collective-permute-start(f32[31,512]{1,0:T(8,128)S(1)} %get-tuple-element.34), channel_id=1, source_target_pairs={{1,0},{2,1},{3,2},{4,3},{5,4},{6,5},{7,6},{8,7},{9,8},{10,9},{11,1... | collective-permute-start | bytes 190472 | tf_op jit(solution)/shard_map/ppermute | solution.py:20
  56.5 3.4 %collective-permute-start = (f32[31,512]{1,0:T(8,128)S(1)}, f32[31,512]{1,0:T(8,128)S(1)}, u32[]{:S(2)}, u32[]{:S(2)}) collective-permute-start(f32[31,512]{1,0:T(8,128)S(1)} %get-tuple-element.33), channel_id=1, source_target_pairs={{0,1},{1,2},{2,3},{3,4},{4,5},{5,6},{6,7},{7,8},{8,9},{9,10},{10,1... | collective-permute-start | bytes 190472 | tf_op jit(solution)/shard_map/ppermute | solution.py:17
  61.0 8.2 %copy-start.6 = (bf16[512,128]{1,0:T(8,128)(2,1)S(1)}, bf16[512,128]{1,0:T(8,128)(2,1)}, u32[]{:S(2)}) copy-start(bf16[512,128]{1,0:T(8,128)(2,1)} %param.13) | copy-start | bytes 393220
  61.0 8.2 %copy-start.11 = (f32[512]{0:T(512)S(1)}, f32[512]{0:T(512)}, u32[]{:S(2)}) copy-start(f32[512]{0:T(512)} %param.12) | copy-start | bytes 6148
  70.9 0.7 copy-start.5
  72.9 0.7 copy-start.7
  107.4 37.7 %copy-start.1 = (f32[512,512]{1,0:T(8,128)S(1)}, f32[512,512]{1,0:T(8,128)}, u32[]{:S(2)}) copy-start(f32[512,512]{1,0:T(8,128)} %shard_map.135) | copy-start | bytes 3145732
  107.4 30.5 %all-to-all-start.3 = ((f32[16,32,512]{2,1,0:T(8,128)}), f32[16,32,512]{2,1,0:T(8,128)}, u32[]{:S(2)}, u32[]{:S(2)}) async-start(f32[16,32,512]{2,1,0:T(8,128)} %broadcast_in_dim.9), calls=%async_computation.3 | async-start | bytes 2097152 | tf_op jit(solution)/shard_map/all_to_all | solution.py:125
  137.9 40.1 %all-to-all-start.4 = ((f32[16,32,512]{2,1,0:T(8,128)}), f32[16,32,512]{2,1,0:T(8,128)}, u32[]{:S(2)}, u32[]{:S(2)}) async-start(f32[16,32,512]{2,1,0:T(8,128)} %bitcast.53), calls=%async_computation.4 | async-start | bytes 2097152 | tf_op jit(solution)/shard_map/all_to_all | solution.py:160
  148.4 1.0 copy-start.2
  150.1 6.8 %collective-permute-start.3 = (f32[31,512]{1,0:T(8,128)}, f32[31,512]{1,0:T(8,128)S(1)}, u32[]{:S(2)}, u32[]{:S(2)}) collective-permute-start(f32[31,512]{1,0:T(8,128)} %get-tuple-element.32), channel_id=1, source_target_pairs={{1,0},{2,1},{3,2},{4,3},{5,4},{6,5},{7,6},{8,7},{9,8},{10,9},{11,1... | collective-permute-start | bytes 190472 | tf_op jit(solution)/shard_map/ppermute | solution.py:20
  154.4 3.6 %collective-permute-start.2 = (f32[31,512]{1,0:T(8,128)}, f32[31,512]{1,0:T(8,128)S(1)}, u32[]{:S(2)}, u32[]{:S(2)}) collective-permute-start(f32[31,512]{1,0:T(8,128)} %get-tuple-element.31), channel_id=1, source_target_pairs={{0,1},{1,2},{2,3},{3,4},{4,5},{5,6},{6,7},{7,8},{8,9},{9,10},{10,1... | collective-permute-start | bytes 190472 | tf_op jit(solution)/shard_map/ppermute | solution.py:17
  178.0 15.0 %copy-start.8 = (bf16[512,128]{1,0:T(8,128)(2,1)S(1)}, bf16[512,128]{1,0:T(8,128)(2,1)}, u32[]{:S(2)}) copy-start(bf16[512,128]{1,0:T(8,128)(2,1)} %copy-done.7) | copy-start | bytes 393220
  181.7 31.5 %all-to-all-start.5 = ((bf16[16,32,512]{2,1,0:T(8,128)(2,1)}), bf16[16,32,512]{2,1,0:T(8,128)(2,1)}, u32[]{:S(2)}, u32[]{:S(2)}) async-start(bf16[16,32,512]{2,1,0:T(8,128)(2,1)} %broadcast_in_dim.10), calls=%async_computation.5 | async-start | bytes 1048576 | tf_op jit(solution)/shard_map/all_to_all | solution.py:125
  194.2 4.0 %copy-start.4 = (bf16[512,512]{1,0:T(8,128)(2,1)S(1)}, bf16[512,512]{1,0:T(8,128)(2,1)}, u32[]{:S(2)}) copy-start(bf16[512,512]{1,0:T(8,128)(2,1)} %get-tuple-element.17) | copy-start | bytes 1572868
  194.2 5.2 %copy-start.10 = (f32[63,512]{1,0:T(8,128)S(1)}, f32[63,512]{1,0:T(8,128)}, u32[]{:S(2)}) copy-start(f32[63,512]{1,0:T(8,128)} %get-tuple-element.20) | copy-start | bytes 387076
  216.7 5.3 %collective-permute-start.4 = (f32[8,328,256]{2,1,0:T(8,128)}, f32[8,328,256]{2,1,0:T(8,128)}, u32[]{:S(2)}, u32[]{:S(2)}) collective-permute-start(f32[8,328,256]{2,1,0:T(8,128)} %dynamic-slice_bitcast_fusion), channel_id=1, source_target_pairs={{0,1},{1,0},{2,3},{3,2},{4,5},{5,4},{6,7},{7,6},{8,9},{9,8},{10,11... | collective-permute-start | bytes 8060936 | tf_op jit(solution)/shard_map/ppermute | solution.py:109
  267.3 1.8 collective-permute-start.5
  269.1 0.7 copy-start.9
  270.8 21.1 %all-to-all-start.7 = ((f32[16,72,256]{2,1,0:T(8,128)}), f32[16,72,256]{2,1,0:T(8,128)S(1)}, u32[]{:S(2)}, u32[]{:S(2)}) async-start(f32[16,72,256]{2,1,0:T(8,128)} %broadcast_in_dim.11), calls=%async_computation.7 | async-start | bytes 2359296 | tf_op jit(solution)/shard_map/all_to_all | solution.py:125

commit v11 on v9

--- a/solution.py
+++ b/solution.py
@@ -155,13 +155,21 @@
     local_w_one = over_time(normed, dpre)
     partial_normed = jnp.dot(dpre, w_one.T, preferred_element_type=jnp.float32)
     dnormed_rows = scatter_sum(split_rows(partial_normed, nn), "neuron")
-    dnormed = gather_all(dnormed_rows, "neuron").reshape(rows, -1)
-    partial_mix, dnormed = lax.optimization_barrier((partial_mix, dnormed))
+    own = lambda x: lax.dynamic_slice_in_dim(x, me * share, share, 0)
+    mixed_own, scale_own = own(mixed), own(scale)
+    gain_part = jnp.sum(dnormed_rows * mixed_own * scale_own, axis=0)
+    dgained = dnormed_rows * gain[None, :]
+    inner = jnp.mean(dgained * mixed_own, axis=1, keepdims=True)
+    dmixed_own = (
+        own(cotangent).astype(jnp.float32)
+        + scale_own * dgained
+        - mixed_own * scale_own**3 * inner
+    )
+    got = gather_all(jnp.concatenate([dmixed_own, gain_part[None, :]], axis=0), "neuron")
+    dmixed = got[:, :share].reshape(rows, -1)
+    local_gain = jnp.sum(got[:, share], axis=0)
+    partial_mix, dmixed = lax.optimization_barrier((partial_mix, dmixed))
     mix_got = lax.all_to_all(split_rows(partial_mix, nn), "neuron", 0, 0, tiled=False)
-    local_gain = jnp.sum(dnormed * mixed * scale, axis=0)
-    dgained = dnormed * gain[None, :]
-    inner = jnp.mean(dgained * mixed, axis=1, keepdims=True)
-    dmixed = cotangent.astype(jnp.float32) + scale * dgained - mixed * scale**3 * inner
     padded_grad = with_halo(dmixed, (("tm", 0),), half)
     dlifted, local_kernel = bwd_conv(padded_grad, dmixed, padded, kernel)
     mix_got, dlifted = lax.optimization_barrier((mix_got, dlifted))

time: 299 us -> 311 us (1.040)
  blocking collectives: 120 us -> 84.3 us
  waiting for transfers between devices: 49.2 us -> 81.1 us
  starting transfers between devices: 37.2 us -> 43.8 us
  local copies, waits for them, and re-layouts: 33 us -> 39.4 us
    all_to_all x2 -> x1, blocking collectives: 61.2 us -> 28.6 us  [scatter_sum(): got = lax.all_to_all(parts, axis, 0, 0, tiled=False)]
    all_to_all x0 -> x1, waiting for transfers between devices: none -> 28.6 us  [scatter_sum(): got = lax.all_to_all(parts, axis, 0, 0, tiled=False)]
    all_to_all x3, waiting for transfers between devices: 39.3 us -> 44.8 us  [gather_all(): return lax.all_to_all(spread, axis, 0, 0, tiled=False)]
    all_to_all x0 -> x1, starting transfers between devices: none -> 4.34 us  [scatter_sum(): got = lax.all_to_all(parts, axis, 0, 0, tiled=False)]
    all_to_all x1, blocking collectives: 42.3 us -> 38.9 us  [pair_scatter_sum(): lax.all_to_all(slabs, axis, 0, 0, tiled=False)]
  transfers between devices with their start and end apart: 10 -> 11, of which waited for: 7 -> 6; matrix products, arithmetic and copies ran while one was open for 12% -> 13% of each run, Pallas kernels for 4% -> 4%
where the time goes in v11:
time: 311 us; the launch traced here: 309 us
  blocking collectives  84.3 us (27%)
  waiting for transfers between devices  81.1 us (26%)
  starting transfers between devices  43.8 us (14%)
  local copies, waits for them, and re-layouts  39.4 us (13%)
  matrix products  21.8 us (7%)
  other arithmetic  19.7 us (6%)
  Pallas kernels  18.2 us (6%)
    all_to_all x3, waiting for transfers between devices, gather_all(): return lax.all_to_all(spread, axis, 0, 0, tiled=False)  44.8 us
    all_to_all x1, blocking collectives, pair_scatter_sum(): lax.all_to_all(slabs, axis, 0, 0, tiled=False)  38.9 us
    all_to_all x1, blocking collectives, scatter_sum(): got = lax.all_to_all(parts, axis, 0, 0, tiled=False)  28.6 us
    all_to_all x1, waiting for transfers between devices, scatter_sum(): got = lax.all_to_all(parts, axis, 0, 0, tiled=False)  28.6 us
    all_to_all x3, starting transfers between devices, gather_all(): return lax.all_to_all(spread, axis, 0, 0, tiled=False)  18.3 us
    all_to_all x1, blocking collectives, gather_all(): return lax.all_to_all(spread, axis, 0, 0, tiled=False)  16.8 us
    pallas_call x1, Pallas kernels, bwd_conv(): pl.pallas_call(_bwd_conv_kernel, out_shape=(jax.ShapeDtypeStruct((rows, w...  11.4 us
    dot_general x4, matrix products, over_time(): lax.dot_general(left, right, (((0,), (0,)), ((), ())), preferred_element_...  10.6 us
  transfers between devices with their start and end apart: 11, of which 6 were waited for; matrix products, arithmetic and copies ran while one was open for 13% of the time, Pallas kernels for 4%

profile of v11, /device:TPU:1, one launch (start us, length us, event | category | flops | bytes accessed | tf_op | source)
XLA Modules:
  0.0 309.2 jit_solution(9424736549683160870)
XLA Ops:
  0.6 1.6 copy-done
  2.2 3.4 %fusion.10 = f32[512,256]{1,0:T(8,128)S(1)} fusion(bf16[512,4096]{1,0:T(8,128)(2,1)} %param.8, bf16[4096,256]{1,0:T(8,128)(2,1)S(1)} %copy-done), kind=kOutput, calls=%fused_computation.38 | convolution fusion | flops 1073741824 | bytes 6815744 | tf_op jit(solution)/shard_map/dot_general | solution.py:140
  5.7 28.6 %all_to_all.40 = f32[16,32,256]{2,1,0:T(8,128)S(1)} all-to-all(f32[16,32,256]{2,1,0:T(8,128)S(1)} %bitcast.64), channel_id=1, replica_groups=mesh['neuron'=16,'tm'=16] {'neuron'}, dimensions={0} | all-to-all | bytes 1048576 | tf_op jit(solution)/shard_map/all_to_all | solution.py:98
  34.3 16.8 %all_to_all.41 = bf16[16,32,256]{2,1,0:T(8,128)(2,1)S(1)} all-to-all(bf16[16,32,256]{2,1,0:T(8,128)(2,1)S(1)} %broadcast_in_dim.10), channel_id=1, replica_groups=mesh['neuron'=16,'tm'=16] {'neuron'}, dimensions={0} | all-to-all | bytes 524288 | tf_op jit(solution)/shard_map/all_to_all | solution.py:125
  51.1 1.2 fusion.11.mid_ref
  52.4 4.0 %collective-permute-start.1 = (f32[31,512]{1,0:T(8,128)S(1)}, f32[31,512]{1,0:T(8,128)S(1)}, u32[]{:S(2)}, u32[]{:S(2)}) collective-permute-start(f32[31,512]{1,0:T(8,128)S(1)} %get-tuple-element.36), channel_id=1, source_target_pairs={{1,0},{2,1},{3,2},{4,3},{5,4},{6,5},{7,6},{8,7},{9,8},{10,9},{11,1... | collective-permute-start | bytes 190472 | tf_op jit(solution)/shard_map/ppermute | solution.py:20
  56.5 2.1 collective-permute-start
  58.6 1.3 collective-permute-done
  61.1 6.8 %shard_map.135 = f32[512,512]{1,0:T(8,128)} custom-call(f32[574,512]{1,0:T(8,128)} %pad_maximum_fusion.1.x_ref, f32[512,512]{1,0:T(8,128)} %copy-done.2, f32[63,512]{1,0:T(8,128)} %k_ref.3), custom_call_target="tpu_custom_call" | custom-call | tf_op jit(solution)/shard_map/pallas_call | solution.py:38
  67.8 1.4 multiply_reduce_fusion
  69.2 1.6 fusion.4
  71.5 1.4 fusion.1
  72.9 1.3 fusion.12
  74.2 4.3 %all-to-all-start.2 = ((f32[16,32,512]{2,1,0:T(8,128)}), f32[16,32,512]{2,1,0:T(8,128)}, u32[]{:S(2)}, u32[]{:S(2)}) async-start(f32[16,32,512]{2,1,0:T(8,128)} %bitcast.60), calls=%async_computation.2 | async-start | bytes 2097152 | tf_op jit(solution)/shard_map/all_to_all | solution.py:98
  78.6 28.6 %all-to-all-done.2 = f32[16,32,512]{2,1,0:T(8,128)} async-done(((f32[16,32,512]{2,1,0:T(8,128)}), f32[16,32,512]{2,1,0:T(8,128)}, u32[]{:S(2)}, u32[]{:S(2)}) %all-to-all-start.2) | async-done | bytes 1048608 | tf_op jit(solution)/shard_map/all_to_all | solution.py:98
  107.2 1.3 reduce_sum.83
  110.7 4.6 %all-to-all-start.3 = ((f32[16,33,512]{2,1,0:T(8,128)}), f32[16,33,512]{2,1,0:T(8,128)}, u32[]{:S(2)}, u32[]{:S(2)}) async-start(f32[16,33,512]{2,1,0:T(8,128)} %broadcast_in_dim.12), calls=%async_computation.3 | async-start | bytes 2621440 | tf_op jit(solution)/shard_map/all_to_all | solution.py:125
  115.3 2.3 fusion.6
  117.6 29.2 %all-to-all-done.3 = f32[16,33,512]{2,1,0:T(8,128)} async-done(((f32[16,33,512]{2,1,0:T(8,128)}), f32[16,33,512]{2,1,0:T(8,128)}, u32[]{:S(2)}, u32[]{:S(2)}) %all-to-all-start.3) | async-done | bytes 1081376 | tf_op jit(solution)/shard_map/all_to_all | solution.py:125
  146.8 2.3 slice.62
  149.1 7.4 %all-to-all-start.4 = ((f32[16,32,512]{2,1,0:T(8,128)}), f32[16,32,512]{2,1,0:T(8,128)}, u32[]{:S(2)}, u32[]{:S(2)}) async-start(f32[16,32,512]{2,1,0:T(8,128)} %bitcast.61), calls=%async_computation.4 | async-start | bytes 2097152 | tf_op jit(solution)/shard_map/all_to_all | solution.py:172
  157.7 1.5 fusion.8
  159.2 3.8 %collective-permute-start.3 = (f32[31,512]{1,0:T(8,128)}, f32[31,512]{1,0:T(8,128)S(1)}, u32[]{:S(2)}, u32[]{:S(2)}) collective-permute-start(f32[31,512]{1,0:T(8,128)} %get-tuple-element.34), channel_id=1, source_target_pairs={{1,0},{2,1},{3,2},{4,3},{5,4},{6,5},{7,6},{8,7},{9,8},{10,9},{11,1... | collective-permute-start | bytes 190472 | tf_op jit(solution)/shard_map/ppermute | solution.py:20
  163.0 3.1 %collective-permute-start.2 = (f32[31,512]{1,0:T(8,128)}, f32[31,512]{1,0:T(8,128)S(1)}, u32[]{:S(2)}, u32[]{:S(2)}) collective-permute-start(f32[31,512]{1,0:T(8,128)} %get-tuple-element.33), channel_id=1, source_target_pairs={{0,1},{1,2},{2,3},{3,4},{4,5},{5,6},{6,7},{7,8},{8,9},{9,10},{10,1... | collective-permute-start | bytes 190472 | tf_op jit(solution)/shard_map/ppermute | solution.py:17
  166.1 2.1 fusion.5
  168.2 1.7 reshape.126
  169.9 1.7 reshape.127
  171.6 2.4 pad_maximum_fusion.2.g_ref
  174.0 11.4 %shard_map.136 = (bf16[512,512]{1,0:T(8,128)(2,1)}, f32[63,512]{1,0:T(8,128)}) custom-call(f32[574,512]{1,0:T(8,128)} %pad_maximum_fusion.2.g_ref, f32[512,512]{1,0:T(8,128)} %bitcast.54, f32[574,512]{1,0:T(8,128)} %pad_maximum_fusion.1.x_ref, f32[63,512]{1,0:T(8,128)} %k_ref.3), custom_call_target="tpu_custom_call" | custom-call | tf_op jit(solution)/shard_map/pallas_call | solution.py:71
  185.4 1.3 reduce_sum.86
  187.6 9.9 %all-to-all-start.5 = ((bf16[16,32,512]{2,1,0:T(8,128)(2,1)}), bf16[16,32,512]{2,1,0:T(8,128)(2,1)}, u32[]{:S(2)}, u32[]{:S(2)}) async-start(bf16[16,32,512]{2,1,0:T(8,128)(2,1)} %broadcast_in_dim.13), calls=%async_computation.5 | async-start | bytes 1048576 | tf_op jit(solution)/shard_map/all_to_all | solution.py:125
  198.5 1.6 reshape.124
  200.0 1.4 fusion.13
  202.3 6.0 %convolution_bitcast_fusion = f32[4096,256]{0,1:T(8,128)} fusion(bf16[512,4096]{1,0:T(8,128)(2,1)} %param.8, bf16[512,512]{1,0:T(8,128)(2,1)S(1)} %copy-done.3, bf16[256,512]{1,0:T(8,128)(2,1)} %param.10), kind=kOutput, calls=%fused_computation | convolution fusion | flops 1208090624 | bytes 9175040 | tf_op jit(solution)/shard_map/dot_general | solution.py:92
  208.3 5.7 %copy.18 = f32[4096,256]{1,0:T(8,128)} copy(f32[4096,256]{0,1:T(8,128)} %convolution_bitcast_fusion) | data formatting | bytes 8388608 | tf_op jit(solution)/shard_map/reshape | solution.py:186
  214.1 3.0 concatenate.21
  217.0 5.0 %pad_maximum_fusion = f32[16,328,256]{2,1,0:T(8,128)} fusion(f32[16,72,256]{2,1,0:T(8,128)S(1)} %bitcast.59, f32[16,256,256]{2,1,0:T(8,128)} %bitcast.49), kind=kLoop, calls=%fused_computation.1 | loop fusion | flops 1343488 | bytes 10747904 | tf_op jit(solution)/shard_map/concatenate | solution.py:188
  222.1 3.5 %dynamic-slice_bitcast_fusion = f32[8,328,256]{2,1,0:T(8,128)} fusion(f32[8,2,328,256]{3,2,1,0:T(8,128)} %bitcast.47, s32[]{:T(128)S(6)} %select_n.39), kind=kLoop, calls=%fused_computation.4 | loop fusion | bytes 5373956 | tf_op jit(solution)/shard_map/jit(dynamic_index_in_dim)/squeeze | solution.py:108
  225.6 5.3 %collective-permute-done.4 = f32[8,328,256]{2,1,0:T(8,128)} collective-permute-done((f32[8,328,256]{2,1,0:T(8,128)}, f32[8,328,256]{2,1,0:T(8,128)}, u32[]{:S(2)}, u32[]{:S(2)}) %collective-permute-start.4) | collective-permute-done | bytes 2687008 | tf_op jit(solution)/shard_map/ppermute | solution.py:109
  231.0 2.9 bitcast_add_fusion
  234.7 38.9 %all_to_all.42 = f32[16,164,256]{2,1,0:T(8,128)S(1)} all-to-all(f32[16,164,256]{2,1,0:T(8,128)S(1)} %bitcast.51), channel_id=1, replica_groups=mesh['neuron'=16,'tm'=16] {'tm'}, dimensions={0} | all-to-all | bytes 5373952 | tf_op jit(solution)/shard_map/all_to_all | solution.py:114
  277.5 3.9 %all-to-all-start.7 = ((f32[16,72,256]{2,1,0:T(8,128)}), f32[16,72,256]{2,1,0:T(8,128)S(1)}, u32[]{:S(2)}, u32[]{:S(2)}) async-start(f32[16,72,256]{2,1,0:T(8,128)} %broadcast_in_dim.14), calls=%async_computation.7 | async-start | bytes 2359296 | tf_op jit(solution)/shard_map/all_to_all | solution.py:125
  281.3 1.6 pad_maximum_fusion.3
  282.9 15.6 %all-to-all-done.7 = f32[16,72,256]{2,1,0:T(8,128)S(1)} async-done(((f32[16,72,256]{2,1,0:T(8,128)}), f32[16,72,256]{2,1,0:T(8,128)S(1)}, u32[]{:S(2)}, u32[]{:S(2)}) %all-to-all-start.7) | async-done | bytes 1179680 | tf_op jit(solution)/shard_map/all_to_all | solution.py:125
  300.8 2.0 reshape.132
  302.7 1.6 reshape.133
  304.9 1.7 reshape.135
  307.4 1.9 copy.21
  (58 shorter events, 16.4 us)
Async XLA Ops:
  0.6 1.6 copy-start
  52.4 8.7 %copy-start.2 = (f32[512,512]{1,0:T(8,128)}, f32[512,512]{1,0:T(8,128)S(1)}, u32[]{:S(2)}) copy-start(f32[512,512]{1,0:T(8,128)S(1)} %fusion.11.mid_ref) | copy-start | bytes 3145732
  52.4 6.2 %collective-permute-start.1 = (f32[31,512]{1,0:T(8,128)S(1)}, f32[31,512]{1,0:T(8,128)S(1)}, u32[]{:S(2)}, u32[]{:S(2)}) collective-permute-start(f32[31,512]{1,0:T(8,128)S(1)} %get-tuple-element.36), channel_id=1, source_target_pairs={{1,0},{2,1},{3,2},{4,3},{5,4},{6,5},{7,6},{8,7},{9,8},{10,9},{11,1... | collective-permute-start | bytes 190472 | tf_op jit(solution)/shard_map/ppermute | solution.py:20
  56.5 3.4 %collective-permute-start = (f32[31,512]{1,0:T(8,128)S(1)}, f32[31,512]{1,0:T(8,128)S(1)}, u32[]{:S(2)}, u32[]{:S(2)}) collective-permute-start(f32[31,512]{1,0:T(8,128)S(1)} %get-tuple-element.35), channel_id=1, source_target_pairs={{0,1},{1,2},{2,3},{3,4},{4,5},{5,6},{6,7},{7,8},{8,9},{9,10},{10,1... | collective-permute-start | bytes 190472 | tf_op jit(solution)/shard_map/ppermute | solution.py:17
  61.1 8.2 %copy-start.6 = (bf16[512,128]{1,0:T(8,128)(2,1)S(1)}, bf16[512,128]{1,0:T(8,128)(2,1)}, u32[]{:S(2)}) copy-start(bf16[512,128]{1,0:T(8,128)(2,1)} %param.13) | copy-start | bytes 393220
  61.1 8.2 %copy-start.10 = (f32[512]{0:T(512)S(1)}, f32[512]{0:T(512)}, u32[]{:S(2)}) copy-start(f32[512]{0:T(512)} %param.12) | copy-start | bytes 6148
  70.8 0.7 copy-start.4
  72.9 1.3 copy-start.7
  72.9 35.6 %copy-start.1 = (f32[512,512]{1,0:T(8,128)S(1)}, f32[512,512]{1,0:T(8,128)}, u32[]{:S(2)}) copy-start(f32[512,512]{1,0:T(8,128)} %shard_map.135) | copy-start | bytes 3145732
  74.2 33.0 %all-to-all-start.2 = ((f32[16,32,512]{2,1,0:T(8,128)}), f32[16,32,512]{2,1,0:T(8,128)}, u32[]{:S(2)}, u32[]{:S(2)}) async-start(f32[16,32,512]{2,1,0:T(8,128)} %bitcast.60), calls=%async_computation.2 | async-start | bytes 2097152 | tf_op jit(solution)/shard_map/all_to_all | solution.py:98
  110.7 36.1 %all-to-all-start.3 = ((f32[16,33,512]{2,1,0:T(8,128)}), f32[16,33,512]{2,1,0:T(8,128)}, u32[]{:S(2)}, u32[]{:S(2)}) async-start(f32[16,33,512]{2,1,0:T(8,128)} %broadcast_in_dim.12), calls=%async_computation.3 | async-start | bytes 2621440 | tf_op jit(solution)/shard_map/all_to_all | solution.py:125
  115.3 41.2 %copy-start.8 = (bf16[512,128]{1,0:T(8,128)(2,1)S(1)}, bf16[512,128]{1,0:T(8,128)(2,1)}, u32[]{:S(2)}) copy-start(bf16[512,128]{1,0:T(8,128)(2,1)} %copy-done.7) | copy-start | bytes 393220
  149.1 36.3 %all-to-all-start.4 = ((f32[16,32,512]{2,1,0:T(8,128)}), f32[16,32,512]{2,1,0:T(8,128)}, u32[]{:S(2)}, u32[]{:S(2)}) async-start(f32[16,32,512]{2,1,0:T(8,128)} %bitcast.61), calls=%async_computation.4 | async-start | bytes 2097152 | tf_op jit(solution)/shard_map/all_to_all | solution.py:172
  159.2 12.4 %collective-permute-start.3 = (f32[31,512]{1,0:T(8,128)}, f32[31,512]{1,0:T(8,128)S(1)}, u32[]{:S(2)}, u32[]{:S(2)}) collective-permute-start(f32[31,512]{1,0:T(8,128)} %get-tuple-element.34), channel_id=1, source_target_pairs={{1,0},{2,1},{3,2},{4,3},{5,4},{6,5},{7,6},{8,7},{9,8},{10,9},{11,1... | collective-permute-start | bytes 190472 | tf_op jit(solution)/shard_map/ppermute | solution.py:20
  163.0 8.6 %collective-permute-start.2 = (f32[31,512]{1,0:T(8,128)}, f32[31,512]{1,0:T(8,128)S(1)}, u32[]{:S(2)}, u32[]{:S(2)}) collective-permute-start(f32[31,512]{1,0:T(8,128)} %get-tuple-element.33), channel_id=1, source_target_pairs={{0,1},{1,2},{2,3},{3,4},{4,5},{5,6},{6,7},{7,8},{8,9},{9,10},{10,1... | collective-permute-start | bytes 190472 | tf_op jit(solution)/shard_map/ppermute | solution.py:17
  186.7 15.6 %copy-start.3 = (bf16[512,512]{1,0:T(8,128)(2,1)S(1)}, bf16[512,512]{1,0:T(8,128)(2,1)}, u32[]{:S(2)}) copy-start(bf16[512,512]{1,0:T(8,128)(2,1)} %get-tuple-element.19) | copy-start | bytes 1572868
  187.6 34.5 %all-to-all-start.5 = ((bf16[16,32,512]{2,1,0:T(8,128)(2,1)}), bf16[16,32,512]{2,1,0:T(8,128)(2,1)}, u32[]{:S(2)}, u32[]{:S(2)}) async-start(bf16[16,32,512]{2,1,0:T(8,128)(2,1)} %broadcast_in_dim.13), calls=%async_computation.5 | async-start | bytes 1048576 | tf_op jit(solution)/shard_map/all_to_all | solution.py:125
  208.3 5.7 %copy-start.5 = (f32[256,256]{1,0:T(8,128)S(1)}, f32[256,256]{1,0:T(8,128)}, u32[]{:S(2)}) copy-start(f32[256,256]{1,0:T(8,128)} %reshape.126) | copy-start | bytes 786436
  225.6 5.3 %collective-permute-start.4 = (f32[8,328,256]{2,1,0:T(8,128)}, f32[8,328,256]{2,1,0:T(8,128)}, u32[]{:S(2)}, u32[]{:S(2)}) collective-permute-start(f32[8,328,256]{2,1,0:T(8,128)} %dynamic-slice_bitcast_fusion), channel_id=1, source_target_pairs={{0,1},{1,0},{2,3},{3,2},{4,5},{5,4},{6,7},{7,6},{8,9},{9,8},{10,11... | collective-permute-start | bytes 8060936 | tf_op jit(solution)/shard_map/ppermute | solution.py:109
  273.9 1.8 collective-permute-start.5
  275.7 0.7 copy-start.9
  277.5 21.1 %all-to-all-start.7 = ((f32[16,72,256]{2,1,0:T(8,128)}), f32[16,72,256]{2,1,0:T(8,128)S(1)}, u32[]{:S(2)}, u32[]{:S(2)}) async-start(f32[16,72,256]{2,1,0:T(8,128)} %broadcast_in_dim.14), calls=%async_computation.7 | async-start | bytes 2359296 | tf_op jit(solution)/shard_map/all_to_all | solution.py:125
